TPU v7x, 512 devices: a whole 4x4x16 slice. The times are simulated.
512 devices in a mesh: row: 32 (over y, x, core), col: 16 (over z).
Axes of the slice: x: 4, y: 4, z: 16, core: 2. Of those that a mesh axis runs over, the one named last changes fastest.
Arguments:
- queries: bfloat16 [512, 16, 1024], P('row', None, 'col'), may hold values from -30 to 30
- new_keys: bfloat16 [512, 1024], P('row', 'col'), may hold values from -6 to 6
- new_values: bfloat16 [512, 1024], P('row', 'col'), may hold values from -12 to 12
- cache_keys: bfloat16 [512, 128, 1024], P('row', None, 'col'), may hold values from -8 to 8
- cache_values: bfloat16 [512, 128, 1024], P('row', None, 'col'), may hold values from -12 to 12
- lengths: int32 [512], P('row'), may hold values from 64 to 128
- parents: int32 [512], P('row'), may hold values from 0 to 511, as said below
- residual: bfloat16 [512, 16, 1024], P('row', None, 'col'), may hold values from -20 to 20
- norm_gain: bfloat16 [16, 1024], P(None, 'col'), may hold values from 0.5 to 1.5
- vocab_weight: bfloat16 [16, 1024, 64128], P(None, 'col', 'row')
Outputs:
- logprobs: float32 [512, 64128], P('col', 'row')
Inputs may be any that keep to these rules, and one draw needn't show every extreme that they name: Among the 16 child beams of one index of row, at most 2 have their parents on the beams of any single index of row, and exactly 2 do for some index.
All inputs are finite; a program needn't handle non-finite values.
Results may differ from a plain program's by a relative error of at most 0.0015.
Values may be sent and summed in bfloat16 or wider, within the bound.
No kernel may reach another device: no remote copies, remote signals or barrier semaphores. Data moves between devices by JAX's collectives and lax.ppermute only.
A program may use at most 64 MiB of HBM per device.

v0:
```python
import jax
import jax.numpy as jnp
from jax import lax
from jax.sharding import PartitionSpec as P

HEAD_DIM = 128
D = 16384


def from_partner(value, axis, distance):
    mask = 2**distance
    pairs = [(source, source ^ mask) for source in range(lax.axis_size(axis))]
    return lax.ppermute(value, axis, pairs)


def count_before(sources):
    entries = sources.shape[-1]
    earlier = jnp.arange(entries)[:, None] > jnp.arange(entries)[None, :]
    matching = sources[..., :, None] == sources[..., None, :]
    return jnp.sum(matching & earlier, axis=-1)


def attend(queries_in, key_cache, value_cache, key_new, value_new, live_rows):
    leading = queries_in.shape[:-2]
    group_size = queries_in.shape[-2]
    panel_width = queries_in.shape[-1]
    head_part = min(panel_width, HEAD_DIM)
    heads_here = panel_width // head_part
    context = key_cache.shape[-2]
    query_heads = queries_in.reshape(leading + (group_size, heads_here, head_part))
    key_heads = key_cache.reshape(leading + (context, heads_here, head_part))
    value_heads = value_cache.reshape(leading + (context, heads_here, head_part))
    fresh_key = key_new.reshape(leading + (heads_here, head_part))
    fresh_value = value_new.reshape(leading + (1, heads_here, head_part)).astype(jnp.float32)
    cached = jnp.einsum(
        "...jhe,...the->...jht", query_heads, key_heads, preferred_element_type=jnp.float32
    )
    own_score = jnp.einsum(
        "...jhe,...he->...jh", query_heads, fresh_key, preferred_element_type=jnp.float32
    )
    other_cached, other_own = from_partner((cached, own_score), "col", 0)
    cached = cached + other_cached
    own_score = own_score + other_own
    scale_factor = HEAD_DIM ** (-0.5)
    cached = cached * scale_factor
    own_score = own_score * scale_factor
    positions = lax.broadcasted_iota(jnp.int32, cached.shape, cached.ndim - 1)
    visible = positions < live_rows.reshape(leading + (1, 1, 1))
    peak_score = jnp.maximum(jnp.max(jnp.where(visible, cached, -jnp.inf), axis=-1), own_score)
    weight = jnp.where(visible, jnp.exp(cached - peak_score[..., None]), jnp.float32(0.0))
    weight_own = jnp.exp(own_score - peak_score)
    weight_sum = jnp.sum(weight, axis=-1) + weight_own
    rounded = weight.astype(jnp.bfloat16)
    rounded_own = lax.optimization_barrier(weight_own.astype(jnp.bfloat16)).astype(jnp.float32)
    summed = jnp.einsum(
        "...jht,...the->...jhe", rounded, value_heads, preferred_element_type=jnp.float32
    )
    own_part = rounded_own[..., None] * fresh_value
    result = (summed + own_part) / weight_sum[..., None]
    return result.reshape(leading + (group_size, panel_width)).astype(jnp.bfloat16)


def body(
    queries,
    new_keys,
    new_values,
    cache_keys,
    cache_values,
    lengths,
    parents,
    residual,
    norm_gain,
    vocab_weight,
):
    row_count = lax.axis_size("row")
    beam_count = parents.shape[0]
    slot_cap = max(2, (2 * beam_count + row_count - 1) // row_count)
    my_row = lax.axis_index("row")
    group_size = queries.shape[1]
    panel_width = queries.shape[2]
    source = parents // beam_count
    rank_in = count_before(source)
    slot_index = source * slot_cap + rank_in
    slot_range = jnp.arange(slot_cap, dtype=jnp.int32)
    all_parents, all_lengths = (
        lax.all_gather(parents, "row", axis=0, tiled=True),
        lax.all_gather(lengths, "row", axis=0, tiled=True),
    )
    parent_table = all_parents.reshape(row_count, beam_count)
    sources_all = parent_table // beam_count
    offsets_all = parent_table % beam_count
    ranks_all = count_before(sources_all)
    chosen = (sources_all[:, None, :] == my_row) & (
        ranks_all[:, None, :] == slot_range[None, :, None]
    )
    rows_sent = jnp.sum(jnp.where(chosen, offsets_all[:, None, :], 0), axis=2)
    got_keys, got_values = (
        lax.all_to_all(cache_keys[rows_sent], "row", split_axis=0, concat_axis=0, tiled=True),
        lax.all_to_all(cache_values[rows_sent], "row", split_axis=0, concat_axis=0, tiled=True),
    )
    context = cache_keys.shape[1]
    kept_keys = got_keys.reshape(row_count * slot_cap, context, panel_width)[slot_index]
    kept_values = got_values.reshape(row_count * slot_cap, context, panel_width)[slot_index]
    attended = attend(queries, kept_keys, kept_values, new_keys, new_values, all_lengths[parents])
    stream = residual.astype(jnp.float32) + attended.astype(jnp.float32)
    square_sums = lax.psum(jnp.sum(stream * stream, axis=(1, 2)), "col")
    scaling = lax.rsqrt(square_sums / D + 1e-05)
    normed = (stream * norm_gain.astype(jnp.float32)[None] * scaling[:, None, None]).astype(
        jnp.bfloat16
    )
    gathered = lax.all_gather(normed, "row", axis=0, tiled=True)
    flat_rows = gathered.reshape(gathered.shape[0], group_size * panel_width)
    flat_weight = vocab_weight.reshape(group_size * panel_width, vocab_weight.shape[2])
    logits = lax.psum_scatter(
        jnp.dot(flat_rows, flat_weight, preferred_element_type=jnp.float32),
        "col",
        scatter_dimension=0,
        tiled=True,
    )
    totals = lax.psum(jnp.sum(jnp.exp(logits), axis=1), "row")
    return logits - jnp.log(totals)[:, None]


def solution(mesh):
    placed = (
        P("row", None, "col"),
        P("row", "col"),
        P("row", "col"),
        P("row", None, "col"),
        P("row", None, "col"),
        P("row"),
        P("row"),
        P("row", None, "col"),
        P(None, "col"),
        P(None, "col", "row"),
    )
    return jax.shard_map(
        body, mesh=mesh, in_specs=placed, out_specs=P("col", "row"), check_vma=False
    )
```

profile of v0, /device:TPU:1, one launch (start us, length us, event | category | flops | bytes accessed | tf_op | source)
XLA Modules:
  0.0 322.9 jit_solution(3743280184073839747)
XLA Ops:
  6.5 0.0 copy-start
  6.5 1.3 dynamic-slice
  8.5 0.9 dynamic-update-slice
  9.4 0.8 dynamic-update-slice.1
  10.2 14.4 %all-reduce.2 = (s32[512]{0:T(512)S(1)}, s32[512]{0:T(512)S(1)}) all-reduce(s32[512]{0:T(512)S(1)} %dynamic-update-slice, s32[512]{0:T(512)S(1)} %dynamic-update-slice.1), channel_id=1, replica_groups=mesh['row'=32,'col'=16] {'row'}, use_global_device_ids=true, to_apply=%add | all-reduce | flops 1024 | bytes 8192
  24.7 0.1 reshape.188
  24.7 0.1 copy.23
  24.8 0.1 convert_reduce_fusion
  25.0 0.1 copy.27
  25.1 0.1 reshape.196
  25.2 0.0 copy-done
  25.2 1.7 gather_fusion.3
  26.9 11.0 %all-to-all-start.1 = ((bf16[32,2,128,64]{2,3,1,0:T(8,128)(2,1)}), bf16[32,2,128,64]{2,3,1,0:T(8,128)(2,1)S(1)}, u32[]{:S(2)}, u32[]{:S(2)}) async-start(bf16[32,2,128,64]{2,3,1,0:T(8,128)(2,1)} %bitcast.4), calls=%async_computation.1 | async-start | bytes 2097152 | tf_op jit(solution)/shard_map/all_to_all | solution.py:98
  37.9 0.0 copy-done.1
  37.9 1.7 gather_fusion
  39.6 0.0 copy-start.4
  39.6 15.3 %all-to-all-done.1 = bf16[32,2,128,64]{2,3,1,0:T(8,128)(2,1)S(1)} async-done(((bf16[32,2,128,64]{2,3,1,0:T(8,128)(2,1)}), bf16[32,2,128,64]{2,3,1,0:T(8,128)(2,1)S(1)}, u32[]{:S(2)}, u32[]{:S(2)}) %all-to-all-start.1) | async-done | bytes 1048608 | tf_op jit(solution)/shard_map/all_to_all | solution.py:98
  54.9 4.0 %all-to-all-start = ((bf16[32,2,128,64]{2,3,1,0:T(8,128)(2,1)}), bf16[32,2,128,64]{2,3,1,0:T(8,128)(2,1)S(1)}, u32[]{:S(2)}, u32[]{:S(2)}) async-start(bf16[32,2,128,64]{2,3,1,0:T(8,128)(2,1)} %bitcast.2), calls=%async_computation | async-start | bytes 2097152 | tf_op jit(solution)/shard_map/all_to_all | solution.py:99
  58.9 0.0 copy-start.5
  58.9 0.0 all-gather.2.cloned.1.call-start
  59.0 0.0 copy-done.7
  59.0 0.2 convert_reduce_fusion.1
  59.2 0.6 gather_fusion.4
  59.8 0.0 copy-done.2
  59.8 0.2 convolution_bitcast_fusion.1
  60.0 1.9 collective-permute-start
  61.9 0.1 fusion.16
  62.1 3.4 %collective-permute-start.1 = (f32[16,16,1]{1,0,2:T(8,128)S(1)}, f32[16,16,1]{1,0,2:T(8,128)S(1)}, u32[]{:S(2)}, u32[]{:S(2)}) collective-permute-start(f32[16,16,1]{1,0,2:T(8,128)S(1)} %bitcast.75), channel_id=1, source_target_pairs={{0,1},{1,0},{2,3},{3,2},{4,5},{5,4},{6,7},{7,6},{8,9},{9,8},{10,11... | collective-permute-start | bytes 3080 | tf_op jit(solution)/shard_map/ppermute | solution.py:13
  65.5 0.0 copy-done.3
  65.5 0.7 gather_fusion.2
  66.2 9.9 %all-to-all-done = bf16[32,2,128,64]{2,3,1,0:T(8,128)(2,1)S(1)} async-done(((bf16[32,2,128,64]{2,3,1,0:T(8,128)(2,1)}), bf16[32,2,128,64]{2,3,1,0:T(8,128)(2,1)S(1)}, u32[]{:S(2)}, u32[]{:S(2)}) %all-to-all-start) | async-done | bytes 1048608 | tf_op jit(solution)/shard_map/all_to_all | solution.py:99
  76.1 0.6 gather_fusion.1
  76.7 0.0 collective-permute-done
  76.7 0.2 select_reduce_fusion
  76.9 0.0 collective-permute-done.1
  76.9 0.2 fusion.7
  77.2 0.4 multiply_reduce_fusion
  77.6 26.0 %psum.14 = f32[16]{0:T(128)S(1)} all-reduce(f32[16]{0:T(128)S(1)} %get-tuple-element.13), channel_id=1, replica_groups=mesh['row'=32,'col'=16] {'col'}, use_global_device_ids=true, to_apply=%region_6.7 | all-reduce | flops 16 | bytes 128 | tf_op jit(solution)/shard_map/psum | solution.py:106
  103.6 0.7 multiply_convert_fusion
  104.4 0.0 all-gather.2.cloned.1.call-update
  104.4 0.0 reduce-scatter.2.cloned.1.call-start
  104.4 58.6 %all-gather.2.cloned.1.call-done = bf16[512,16,64]{2,1,0:T(8,128)(2,1)} async-done(((bf16[16,16,64]{2,1,0:T(8,128)(2,1)}), bf16[512,16,64]{2,1,0:T(8,128)(2,1)}) %all-gather.2.cloned.1.call-update) | async-done | bytes 1048592 | tf_op jit(solution)/shard_map/all_gather | solution.py:111
  163.0 7.4 %convolution_bitcast_fusion = f32[512,2004]{1,0:T(8,128)} fusion(bf16[16,64,2004]{2,1,0:T(8,128)(2,1)} %param.19, bf16[512,16,64]{2,1,0:T(8,128)(2,1)} %all-gather.2.cloned.1.call-done), kind=kOutput, calls=%fused_computation.5 | convolution fusion | flops 2101346304 | bytes 9256960 | tf_op jit(solution)/shard_map/dot_general | solution.py:115
  170.4 0.0 reduce-scatter.2.cloned.1.call-update
  170.5 69.5 %reduce-scatter.2.cloned.1.call-done = f32[32,2004]{1,0:T(8,128)} async-done(((f32[512,2004]{1,0:T(8,128)}), f32[32,2004]{1,0:T(8,128)}) %reduce-scatter.2.cloned.1.call-update) | async-done | bytes 256528 | tf_op jit(solution)/shard_map/reduce_scatter | solution.py:114
  240.0 1.1 exponential_reduce_fusion
  241.1 73.2 %psum.15 = f32[32]{0:T(128)S(1)} all-reduce(f32[32]{0:T(128)S(1)} %exponential_reduce_fusion), channel_id=1, replica_groups=mesh['row'=32,'col'=16] {'row'}, use_global_device_ids=true, to_apply=%region_9.10 | all-reduce | flops 32 | bytes 256 | tf_op jit(solution)/shard_map/psum | solution.py:120
  314.3 1.7 broadcast_subtract_fusion
  (27 shorter events, 0.2 us)
Async XLA Ops:
  6.5 18.7 %copy-start = (bf16[16,128,64]{1,2,0:T(8,128)(2,1)S(1)}, bf16[16,128,64]{1,2,0:T(8,128)(2,1)}, u32[]{:S(2)}) copy-start(bf16[16,128,64]{1,2,0:T(8,128)(2,1)} %param.13) | copy-start | bytes 786436
  26.9 11.0 %copy-start.1 = (bf16[16,128,64]{1,2,0:T(8,128)(2,1)S(1)}, bf16[16,128,64]{1,2,0:T(8,128)(2,1)}, u32[]{:S(2)}) copy-start(bf16[16,128,64]{1,2,0:T(8,128)(2,1)} %param.14) | copy-start | bytes 786436
  26.9 28.1 %all-to-all-start.1 = ((bf16[32,2,128,64]{2,3,1,0:T(8,128)(2,1)}), bf16[32,2,128,64]{2,3,1,0:T(8,128)(2,1)S(1)}, u32[]{:S(2)}, u32[]{:S(2)}) async-start(bf16[32,2,128,64]{2,3,1,0:T(8,128)(2,1)} %bitcast.4), calls=%async_computation.1 | async-start | bytes 2097152 | tf_op jit(solution)/shard_map/all_to_all | solution.py:98
  39.6 19.4 %copy-start.7 = (s32[16]{0:T(128)S(1)}, s32[16]{0:T(128)}, u32[]{:S(2)}) copy-start(s32[16]{0:T(128)} %param.16) | copy-start | bytes 196
  39.6 20.2 %copy-start.2 = (bf16[16,16,64]{2,1,0:T(8,128)(2,1)S(1)}, bf16[16,16,64]{2,1,0:T(8,128)(2,1)}, u32[]{:S(2)}) copy-start(bf16[16,16,64]{2,1,0:T(8,128)(2,1)} %param.10) | copy-start | bytes 98308
  39.6 22.3 %copy-start.6 = (bf16[16,64]{1,0:T(8,128)(2,1)S(1)}, bf16[16,64]{1,0:T(8,128)(2,1)}, u32[]{:S(2)}) copy-start(bf16[16,64]{1,0:T(8,128)(2,1)} %param.11) | copy-start | bytes 6148
  39.6 25.8 %copy-start.3 = (bf16[16,64]{1,0:T(8,128)(2,1)S(1)}, bf16[16,64]{1,0:T(8,128)(2,1)}, u32[]{:S(2)}) copy-start(bf16[16,64]{1,0:T(8,128)(2,1)} %param.12) | copy-start | bytes 6148
  39.6 25.9 %copy-start.4 = (bf16[16,64]{1,0:T(8,128)(2,1)S(1)}, bf16[16,64]{1,0:T(8,128)(2,1)}, u32[]{:S(2)}) copy-start(bf16[16,64]{1,0:T(8,128)(2,1)} %param.18) | copy-start | bytes 6148
  54.9 21.1 %all-to-all-start = ((bf16[32,2,128,64]{2,3,1,0:T(8,128)(2,1)}), bf16[32,2,128,64]{2,3,1,0:T(8,128)(2,1)S(1)}, u32[]{:S(2)}, u32[]{:S(2)}) async-start(bf16[32,2,128,64]{2,3,1,0:T(8,128)(2,1)} %bitcast.2), calls=%async_computation | async-start | bytes 2097152 | tf_op jit(solution)/shard_map/all_to_all | solution.py:99
  58.9 18.2 %copy-start.5 = (bf16[16,16,64]{2,1,0:T(8,128)(2,1)S(1)}, bf16[16,16,64]{2,1,0:T(8,128)(2,1)}, u32[]{:S(2)}) copy-start(bf16[16,16,64]{2,1,0:T(8,128)(2,1)} %param.17) | copy-start | bytes 98308
  58.9 104.1 %all-gather.2.cloned.1.call-start = ((), (), s32[]{:S(2)}) async-start(), calls=%async_computation.3 | async-start | bytes 2162688 | tf_op jit(solution)/shard_map/all_gather | solution.py:111
  60.0 16.7 %collective-permute-start = (f32[16,16,1,128]{3,1,0,2:T(8,128)S(1)}, f32[16,16,1,128]{3,1,0,2:T(8,128)S(1)}, u32[]{:S(2)}, u32[]{:S(2)}) collective-permute-start(f32[16,16,1,128]{3,1,0,2:T(8,128)S(1)} %convolution_bitcast_fusion.1), channel_id=1, source_target_pairs={{0,1},{1,0},{2,3},{3,2},{4,5},{5,4},{6,7},{7,6},{8,9},{9,8},{10,11... | collective-permute-start | bytes 393224 | tf_op jit(solution)/shard_map/ppermute | solution.py:13
  62.1 14.8 %collective-permute-start.1 = (f32[16,16,1]{1,0,2:T(8,128)S(1)}, f32[16,16,1]{1,0,2:T(8,128)S(1)}, u32[]{:S(2)}, u32[]{:S(2)}) collective-permute-start(f32[16,16,1]{1,0,2:T(8,128)S(1)} %bitcast.75), channel_id=1, source_target_pairs={{0,1},{1,0},{2,3},{3,2},{4,5},{5,4},{6,7},{7,6},{8,9},{9,8},{10,11... | collective-permute-start | bytes 3080 | tf_op jit(solution)/shard_map/ppermute | solution.py:13
  104.4 135.6 %reduce-scatter.2.cloned.1.call-start = ((), (), s32[]{:S(2)}) async-start(), calls=%async_computation.4 | async-start | bytes 4456448 | tf_op jit(solution)/shard_map/reduce_scatter | solution.py:114
Sparse Core Ops, SparseCore 0:
  104.5 58.4 all-gather.1
  170.6 69.3 reduce-scatter.1
where the time goes:
time: 323 us
  waiting for transfers between devices  153 us (47%)
  blocking collectives  114 us (35%)
  starting transfers between devices  20.3 us (6%)
  between operations  14.3 us (4%)
  local copies, waits for them, and re-layouts  8.63 us (3%)
  matrix products  8.17 us (3%)
  other arithmetic  4.38 us (1%)
    psum x1, blocking collectives, body(): totals = lax.psum(jnp.sum(jnp.exp(logits), axis=1), 'row')  73.2 us
    reduce_scatter x1, waiting for transfers between devices, body(): lax.psum_scatter(jnp.dot(flat_rows, flat_weight, preferred_element_type=j...  69.5 us
    all_gather x1, waiting for transfers between devices, body(): gathered = lax.all_gather(normed, 'row', axis=0, tiled=True)  58.6 us
    psum x1, blocking collectives, body(): square_sums = lax.psum(jnp.sum(stream * stream, axis=(1, 2)), 'col')  26 us
    all_to_all x1, waiting for transfers between devices, body(): lax.all_to_all(cache_keys[rows_sent], 'row', split_axis=0, concat_axis=0,...  15.3 us
    unnamed x1, blocking collectives  14.4 us
    all_to_all x1, starting transfers between devices, body(): lax.all_to_all(cache_keys[rows_sent], 'row', split_axis=0, concat_axis=0,...  11 us
    all_to_all x1, waiting for transfers between devices, body(): lax.all_to_all(cache_values[rows_sent], 'row', split_axis=0, concat_axis=...  9.9 us
  transfers between devices with their start and end apart: 6, of which 4 were waited for; matrix products, arithmetic and copies ran while one was open for 1% of the time, Pallas kernels for 0%

commit v1 on v0

--- a/solution.py
+++ b/solution.py
@@ -11,6 +11,16 @@
     mask = 2**distance
     pairs = [(source, source ^ mask) for source in range(lax.axis_size(axis))]
     return lax.ppermute(value, axis, pairs)
+
+
+def exchange_sum(value, axis):
+    size = lax.axis_size(axis)
+    distance = 1
+    while distance < size:
+        pairs = [(source, source ^ distance) for source in range(size)]
+        value = value + lax.ppermute(value, axis, pairs)
+        distance *= 2
+    return value
 
 
 def count_before(sources):
@@ -103,7 +113,7 @@
     kept_values = got_values.reshape(row_count * slot_cap, context, panel_width)[slot_index]
     attended = attend(queries, kept_keys, kept_values, new_keys, new_values, all_lengths[parents])
     stream = residual.astype(jnp.float32) + attended.astype(jnp.float32)
-    square_sums = lax.psum(jnp.sum(stream * stream, axis=(1, 2)), "col")
+    square_sums = exchange_sum(jnp.sum(stream * stream, axis=(1, 2)), "col")
     scaling = lax.rsqrt(square_sums / D + 1e-05)
     normed = (stream * norm_gain.astype(jnp.float32)[None] * scaling[:, None, None]).astype(
         jnp.bfloat16
@@ -117,7 +127,7 @@
         scatter_dimension=0,
         tiled=True,
     )
-    totals = lax.psum(jnp.sum(jnp.exp(logits), axis=1), "row")
+    totals = exchange_sum(jnp.sum(jnp.exp(logits), axis=1), "row")
     return logits - jnp.log(totals)[:, None]
 
 

time: 323 us -> 296 us (0.916); the launches traced: 323 us -> 291 us
  blocking collectives: 114 us -> 14.4 us
  starting transfers between devices: 20.3 us -> 69.9 us
  waiting for transfers between devices: 153 us -> 171 us
    psum x2 -> x0, blocking collectives: 99.2 us -> none  [the longest x1 73.2 us: body(): totals = lax.psum(jnp.sum(jnp.exp(logits), axis=1), 'row')]
    ppermute x0 -> x9, starting transfers between devices: none -> 49.6 us  [exchange_sum(): value = value + lax.ppermute(value, axis, pairs)]
    ppermute x0 -> x9, waiting for transfers between devices: none -> 15.3 us  [exchange_sum(): value = value + lax.ppermute(value, axis, pairs)]
  transfers between devices with their start and end apart: 6 -> 15, of which waited for: 4 -> 13; matrix products, arithmetic and copies ran while one was open for 1% -> 1% of each run, Pallas kernels for 0% -> 0%
where the time goes in v1:
time: 296 us; the launch traced here: 291 us
  waiting for transfers between devices  171 us (58%)
  starting transfers between devices  69.9 us (24%)
  blocking collectives  14.4 us (5%)
  between operations  14.4 us (5%)
  local copies, waits for them, and re-layouts  8.6 us (3%)
  matrix products  8.18 us (3%)
  other arithmetic  4.41 us (1%)
    reduce_scatter x1, waiting for transfers between devices, body(): lax.psum_scatter(jnp.dot(flat_rows, flat_weight, preferred_element_type=j...  69.8 us
    all_gather x1, waiting for transfers between devices, body(): gathered = lax.all_gather(normed, 'row', axis=0, tiled=True)  61.1 us
    ppermute x9, starting transfers between devices, exchange_sum(): value = value + lax.ppermute(value, axis, pairs)  49.6 us
    all_to_all x1, waiting for transfers between devices, body(): lax.all_to_all(cache_keys[rows_sent], 'row', split_axis=0, concat_axis=0,...  15.3 us
    ppermute x9, waiting for transfers between devices, exchange_sum(): value = value + lax.ppermute(value, axis, pairs)  15.3 us
    unnamed x1, blocking collectives  14.4 us
    all_to_all x1, starting transfers between devices, body(): lax.all_to_all(cache_keys[rows_sent], 'row', split_axis=0, concat_axis=0,...  11 us
    all_to_all x1, waiting for transfers between devices, body(): lax.all_to_all(cache_values[rows_sent], 'row', split_axis=0, concat_axis=...  9.91 us
  transfers between devices with their start and end apart: 15, of which 13 were waited for; matrix products, arithmetic and copies ran while one was open for 1% of the time, Pallas kernels for 0%

profile of v1, /device:TPU:1, one launch (start us, length us, event | category | flops | bytes accessed | tf_op | source)
XLA Modules:
  0.0 291.4 jit_solution(9781636424105929964)
XLA Ops:
  6.5 1.3 dynamic-slice
  8.5 0.9 dynamic-update-slice
  9.4 0.8 dynamic-update-slice.1
  10.2 14.4 %all-reduce.2 = (s32[512]{0:T(512)S(1)}, s32[512]{0:T(512)S(1)}) all-reduce(s32[512]{0:T(512)S(1)} %dynamic-update-slice, s32[512]{0:T(512)S(1)} %dynamic-update-slice.1), channel_id=1, replica_groups=mesh['row'=32,'col'=16] {'row'}, use_global_device_ids=true, to_apply=%add | all-reduce | flops 1024 | bytes 8192
  24.8 0.1 convert_reduce_fusion
  25.0 0.1 copy.27
  25.1 0.1 reshape.196
  25.2 1.6 gather_fusion.3
  26.9 11.0 %all-to-all-start.1 = ((bf16[32,2,128,64]{2,3,1,0:T(8,128)(2,1)}), bf16[32,2,128,64]{2,3,1,0:T(8,128)(2,1)S(1)}, u32[]{:S(2)}, u32[]{:S(2)}) async-start(bf16[32,2,128,64]{2,3,1,0:T(8,128)(2,1)} %bitcast.4), calls=%async_computation.1 | async-start | bytes 2097152 | tf_op jit(solution)/shard_map/all_to_all | solution.py:108
  37.9 1.7 gather_fusion
  39.6 15.3 %all-to-all-done.1 = bf16[32,2,128,64]{2,3,1,0:T(8,128)(2,1)S(1)} async-done(((bf16[32,2,128,64]{2,3,1,0:T(8,128)(2,1)}), bf16[32,2,128,64]{2,3,1,0:T(8,128)(2,1)S(1)}, u32[]{:S(2)}, u32[]{:S(2)}) %all-to-all-start.1) | async-done | bytes 1048608 | tf_op jit(solution)/shard_map/all_to_all | solution.py:108
  54.9 4.0 %all-to-all-start = ((bf16[32,2,128,64]{2,3,1,0:T(8,128)(2,1)}), bf16[32,2,128,64]{2,3,1,0:T(8,128)(2,1)S(1)}, u32[]{:S(2)}, u32[]{:S(2)}) async-start(bf16[32,2,128,64]{2,3,1,0:T(8,128)(2,1)} %bitcast.2), calls=%async_computation | async-start | bytes 2097152 | tf_op jit(solution)/shard_map/all_to_all | solution.py:109
  59.0 0.2 convert_reduce_fusion.1
  59.2 0.6 gather_fusion.4
  59.8 0.2 convolution_bitcast_fusion.1
  60.0 1.9 collective-permute-start
  61.9 0.1 fusion.16
  62.1 3.4 %collective-permute-start.1 = (f32[16,16,1]{1,0,2:T(8,128)S(1)}, f32[16,16,1]{1,0,2:T(8,128)S(1)}, u32[]{:S(2)}, u32[]{:S(2)}) collective-permute-start(f32[16,16,1]{1,0,2:T(8,128)S(1)} %bitcast.75), channel_id=1, source_target_pairs={{0,1},{1,0},{2,3},{3,2},{4,5},{5,4},{6,7},{7,6},{8,9},{9,8},{10,11... | collective-permute-start | bytes 3080 | tf_op jit(solution)/shard_map/ppermute | solution.py:13
  65.5 0.7 gather_fusion.2
  66.1 9.9 %all-to-all-done = bf16[32,2,128,64]{2,3,1,0:T(8,128)(2,1)S(1)} async-done(((bf16[32,2,128,64]{2,3,1,0:T(8,128)(2,1)}), bf16[32,2,128,64]{2,3,1,0:T(8,128)(2,1)S(1)}, u32[]{:S(2)}, u32[]{:S(2)}) %all-to-all-start) | async-done | bytes 1048608 | tf_op jit(solution)/shard_map/all_to_all | solution.py:109
  76.1 0.6 gather_fusion.1
  76.7 0.2 select_reduce_fusion
  76.9 0.2 fusion.7
  77.1 0.4 multiply_reduce_fusion
  77.6 1.9 collective-permute-start.2
  79.5 2.4 collective-permute-done.2
  81.9 1.9 collective-permute-start.3
  83.8 3.3 %collective-permute-done.3 = f32[16]{0:T(128)S(1)} collective-permute-done((f32[16]{0:T(128)S(1)}, f32[16]{0:T(128)S(1)}, u32[]{:S(2)}, u32[]{:S(2)}) %collective-permute-start.3) | collective-permute-done | bytes 96 | tf_op jit(solution)/shard_map/ppermute | solution.py:21
  87.1 6.4 %collective-permute-start.4 = (f32[16]{0:T(128)S(1)}, f32[16]{0:T(128)S(1)}, u32[]{:S(2)}, u32[]{:S(2)}) collective-permute-start(f32[16]{0:T(128)S(1)} %add.102), channel_id=1, source_target_pairs={{0,4},{1,5},{2,6},{3,7},{4,0},{5,1},{6,2},{7,3},{8,12},{9,13},{10,... | collective-permute-start | bytes 200 | tf_op jit(solution)/shard_map/ppermute | solution.py:21
  93.5 1.8 collective-permute-done.4
  95.3 12.2 %collective-permute-start.5 = (f32[16]{0:T(128)S(1)}, f32[16]{0:T(128)S(1)}, u32[]{:S(2)}, u32[]{:S(2)}) collective-permute-start(f32[16]{0:T(128)S(1)} %add.103), channel_id=1, source_target_pairs={{0,8},{1,9},{2,10},{3,11},{4,12},{5,13},{6,14},{7,15},{8,0},{9,1},... | collective-permute-start | bytes 200 | tf_op jit(solution)/shard_map/ppermute | solution.py:21
  107.5 0.9 collective-permute-done.5
  108.5 0.7 multiply_convert_fusion
  109.3 61.1 %all-gather.2.cloned.1.call-done = bf16[512,16,64]{2,1,0:T(8,128)(2,1)} async-done(((bf16[16,16,64]{2,1,0:T(8,128)(2,1)}), bf16[512,16,64]{2,1,0:T(8,128)(2,1)}) %all-gather.2.cloned.1.call-update) | async-done | bytes 1048592 | tf_op jit(solution)/shard_map/all_gather | solution.py:121
  170.3 7.4 %convolution_bitcast_fusion = f32[512,2004]{1,0:T(8,128)} fusion(bf16[16,64,2004]{2,1,0:T(8,128)(2,1)} %param.19, bf16[512,16,64]{2,1,0:T(8,128)(2,1)} %all-gather.2.cloned.1.call-done), kind=kOutput, calls=%fused_computation.5 | convolution fusion | flops 2101346304 | bytes 9256960 | tf_op jit(solution)/shard_map/dot_general | solution.py:125
  177.8 69.8 %reduce-scatter.2.cloned.1.call-done = f32[32,2004]{1,0:T(8,128)} async-done(((f32[512,2004]{1,0:T(8,128)}), f32[32,2004]{1,0:T(8,128)}) %reduce-scatter.2.cloned.1.call-update) | async-done | bytes 256528 | tf_op jit(solution)/shard_map/reduce_scatter | solution.py:124
  247.6 1.1 exponential_reduce_fusion
  248.7 13.0 %collective-permute-start.6 = (f32[32]{0:T(128)S(1)}, f32[32]{0:T(128)S(1)}, u32[]{:S(2)}, u32[]{:S(2)}) collective-permute-start(f32[32]{0:T(128)S(1)} %exponential_reduce_fusion), channel_id=1, source_target_pairs={{0,16},{16,0},{32,48},{48,32},{64,80},{80,64},{96,112},{112,96},{1... | collective-permute-start | bytes 392 | tf_op jit(solution)/shard_map/ppermute | solution.py:21
  261.7 0.8 collective-permute-done.6
  262.5 2.7 collective-permute-start.7
  265.3 1.6 collective-permute-done.7
  266.8 4.3 %collective-permute-start.8 = (f32[32]{0:T(128)S(1)}, f32[32]{0:T(128)S(1)}, u32[]{:S(2)}, u32[]{:S(2)}) collective-permute-start(f32[32]{0:T(128)S(1)} %add.107), channel_id=1, source_target_pairs={{0,64},{16,80},{32,96},{48,112},{64,0},{80,16},{96,32},{112,48},{1... | collective-permute-start | bytes 392 | tf_op jit(solution)/shard_map/ppermute | solution.py:21
  271.1 1.5 collective-permute-done.8
  272.7 2.9 %collective-permute-start.9 = (f32[32]{0:T(128)S(1)}, f32[32]{0:T(128)S(1)}, u32[]{:S(2)}, u32[]{:S(2)}) collective-permute-start(f32[32]{0:T(128)S(1)} %add.108), channel_id=1, source_target_pairs={{0,128},{16,144},{32,160},{48,176},{64,192},{80,208},{96,224},{112... | collective-permute-start | bytes 392 | tf_op jit(solution)/shard_map/ppermute | solution.py:21
  275.6 1.4 collective-permute-done.9
  277.0 4.1 %collective-permute-start.10 = (f32[32]{0:T(128)S(1)}, f32[32]{0:T(128)S(1)}, u32[]{:S(2)}, u32[]{:S(2)}) collective-permute-start(f32[32]{0:T(128)S(1)} %add.109), channel_id=1, source_target_pairs={{0,256},{16,272},{32,288},{48,304},{64,320},{80,336},{96,352},{112... | collective-permute-start | bytes 392 | tf_op jit(solution)/shard_map/ppermute | solution.py:21
  281.1 1.6 collective-permute-done.10
  282.8 1.7 broadcast_subtract_fusion
  (50 shorter events, 0.5 us)
Async XLA Ops:
  6.5 18.7 %copy-start = (bf16[16,128,64]{1,2,0:T(8,128)(2,1)S(1)}, bf16[16,128,64]{1,2,0:T(8,128)(2,1)}, u32[]{:S(2)}) copy-start(bf16[16,128,64]{1,2,0:T(8,128)(2,1)} %param.13) | copy-start | bytes 786436
  26.9 11.0 %copy-start.1 = (bf16[16,128,64]{1,2,0:T(8,128)(2,1)S(1)}, bf16[16,128,64]{1,2,0:T(8,128)(2,1)}, u32[]{:S(2)}) copy-start(bf16[16,128,64]{1,2,0:T(8,128)(2,1)} %param.14) | copy-start | bytes 786436
  26.9 28.1 %all-to-all-start.1 = ((bf16[32,2,128,64]{2,3,1,0:T(8,128)(2,1)}), bf16[32,2,128,64]{2,3,1,0:T(8,128)(2,1)S(1)}, u32[]{:S(2)}, u32[]{:S(2)}) async-start(bf16[32,2,128,64]{2,3,1,0:T(8,128)(2,1)} %bitcast.4), calls=%async_computation.1 | async-start | bytes 2097152 | tf_op jit(solution)/shard_map/all_to_all | solution.py:108
  39.6 19.4 %copy-start.7 = (s32[16]{0:T(128)S(1)}, s32[16]{0:T(128)}, u32[]{:S(2)}) copy-start(s32[16]{0:T(128)} %param.16) | copy-start | bytes 196
  39.6 20.2 %copy-start.2 = (bf16[16,16,64]{2,1,0:T(8,128)(2,1)S(1)}, bf16[16,16,64]{2,1,0:T(8,128)(2,1)}, u32[]{:S(2)}) copy-start(bf16[16,16,64]{2,1,0:T(8,128)(2,1)} %param.10) | copy-start | bytes 98308
  39.6 22.3 %copy-start.6 = (bf16[16,64]{1,0:T(8,128)(2,1)S(1)}, bf16[16,64]{1,0:T(8,128)(2,1)}, u32[]{:S(2)}) copy-start(bf16[16,64]{1,0:T(8,128)(2,1)} %param.11) | copy-start | bytes 6148
  39.6 25.9 %copy-start.3 = (bf16[16,64]{1,0:T(8,128)(2,1)S(1)}, bf16[16,64]{1,0:T(8,128)(2,1)}, u32[]{:S(2)}) copy-start(bf16[16,64]{1,0:T(8,128)(2,1)} %param.12) | copy-start | bytes 6148
  54.9 21.1 %all-to-all-start = ((bf16[32,2,128,64]{2,3,1,0:T(8,128)(2,1)}), bf16[32,2,128,64]{2,3,1,0:T(8,128)(2,1)S(1)}, u32[]{:S(2)}, u32[]{:S(2)}) async-start(bf16[32,2,128,64]{2,3,1,0:T(8,128)(2,1)} %bitcast.2), calls=%async_computation | async-start | bytes 2097152 | tf_op jit(solution)/shard_map/all_to_all | solution.py:109
  58.9 18.2 %copy-start.5 = (bf16[16,16,64]{2,1,0:T(8,128)(2,1)S(1)}, bf16[16,16,64]{2,1,0:T(8,128)(2,1)}, u32[]{:S(2)}) copy-start(bf16[16,16,64]{2,1,0:T(8,128)(2,1)} %param.17) | copy-start | bytes 98308
  58.9 111.4 %all-gather.2.cloned.1.call-start = ((), (), s32[]{:S(2)}) async-start(), calls=%async_computation.3 | async-start | bytes 2162688 | tf_op jit(solution)/shard_map/all_gather | solution.py:121
  59.8 47.7 %copy-start.4 = (bf16[16,64]{1,0:T(8,128)(2,1)S(1)}, bf16[16,64]{1,0:T(8,128)(2,1)}, u32[]{:S(2)}) copy-start(bf16[16,64]{1,0:T(8,128)(2,1)} %param.18) | copy-start | bytes 6148
  60.0 16.7 %collective-permute-start = (f32[16,16,1,128]{3,1,0,2:T(8,128)S(1)}, f32[16,16,1,128]{3,1,0,2:T(8,128)S(1)}, u32[]{:S(2)}, u32[]{:S(2)}) collective-permute-start(f32[16,16,1,128]{3,1,0,2:T(8,128)S(1)} %convolution_bitcast_fusion.1), channel_id=1, source_target_pairs={{0,1},{1,0},{2,3},{3,2},{4,5},{5,4},{6,7},{7,6},{8,9},{9,8},{10,11... | collective-permute-start | bytes 393224 | tf_op jit(solution)/shard_map/ppermute | solution.py:13
  62.1 14.8 %collective-permute-start.1 = (f32[16,16,1]{1,0,2:T(8,128)S(1)}, f32[16,16,1]{1,0,2:T(8,128)S(1)}, u32[]{:S(2)}, u32[]{:S(2)}) collective-permute-start(f32[16,16,1]{1,0,2:T(8,128)S(1)} %bitcast.75), channel_id=1, source_target_pairs={{0,1},{1,0},{2,3},{3,2},{4,5},{5,4},{6,7},{7,6},{8,9},{9,8},{10,11... | collective-permute-start | bytes 3080 | tf_op jit(solution)/shard_map/ppermute | solution.py:13
  77.6 4.3 %collective-permute-start.2 = (f32[16]{0:T(128)S(1)}, f32[16]{0:T(128)S(1)}, u32[]{:S(2)}, u32[]{:S(2)}) collective-permute-start(f32[16]{0:T(128)S(1)} %get-tuple-element.13), channel_id=1, source_target_pairs={{0,1},{1,0},{2,3},{3,2},{4,5},{5,4},{6,7},{7,6},{8,9},{9,8},{10,11... | collective-permute-start | bytes 200 | tf_op jit(solution)/shard_map/ppermute | solution.py:21
  81.9 5.2 %collective-permute-start.3 = (f32[16]{0:T(128)S(1)}, f32[16]{0:T(128)S(1)}, u32[]{:S(2)}, u32[]{:S(2)}) collective-permute-start(f32[16]{0:T(128)S(1)} %add.101), channel_id=1, source_target_pairs={{0,2},{1,3},{2,0},{3,1},{4,6},{5,7},{6,4},{7,5},{8,10},{9,11},{10,... | collective-permute-start | bytes 200 | tf_op jit(solution)/shard_map/ppermute | solution.py:21
  87.1 8.2 %collective-permute-start.4 = (f32[16]{0:T(128)S(1)}, f32[16]{0:T(128)S(1)}, u32[]{:S(2)}, u32[]{:S(2)}) collective-permute-start(f32[16]{0:T(128)S(1)} %add.102), channel_id=1, source_target_pairs={{0,4},{1,5},{2,6},{3,7},{4,0},{5,1},{6,2},{7,3},{8,12},{9,13},{10,... | collective-permute-start | bytes 200 | tf_op jit(solution)/shard_map/ppermute | solution.py:21
  95.3 13.2 %collective-permute-start.5 = (f32[16]{0:T(128)S(1)}, f32[16]{0:T(128)S(1)}, u32[]{:S(2)}, u32[]{:S(2)}) collective-permute-start(f32[16]{0:T(128)S(1)} %add.103), channel_id=1, source_target_pairs={{0,8},{1,9},{2,10},{3,11},{4,12},{5,13},{6,14},{7,15},{8,0},{9,1},... | collective-permute-start | bytes 200 | tf_op jit(solution)/shard_map/ppermute | solution.py:21
  109.2 138.4 %reduce-scatter.2.cloned.1.call-start = ((), (), s32[]{:S(2)}) async-start(), calls=%async_computation.4 | async-start | bytes 4456448 | tf_op jit(solution)/shard_map/reduce_scatter | solution.py:124
  248.7 13.8 %collective-permute-start.6 = (f32[32]{0:T(128)S(1)}, f32[32]{0:T(128)S(1)}, u32[]{:S(2)}, u32[]{:S(2)}) collective-permute-start(f32[32]{0:T(128)S(1)} %exponential_reduce_fusion), channel_id=1, source_target_pairs={{0,16},{16,0},{32,48},{48,32},{64,80},{80,64},{96,112},{112,96},{1... | collective-permute-start | bytes 392 | tf_op jit(solution)/shard_map/ppermute | solution.py:21
  262.5 4.3 %collective-permute-start.7 = (f32[32]{0:T(128)S(1)}, f32[32]{0:T(128)S(1)}, u32[]{:S(2)}, u32[]{:S(2)}) collective-permute-start(f32[32]{0:T(128)S(1)} %add.106), channel_id=1, source_target_pairs={{0,32},{16,48},{32,0},{48,16},{64,96},{80,112},{96,64},{112,80},{1... | collective-permute-start | bytes 392 | tf_op jit(solution)/shard_map/ppermute | solution.py:21
  266.8 5.8 %collective-permute-start.8 = (f32[32]{0:T(128)S(1)}, f32[32]{0:T(128)S(1)}, u32[]{:S(2)}, u32[]{:S(2)}) collective-permute-start(f32[32]{0:T(128)S(1)} %add.107), channel_id=1, source_target_pairs={{0,64},{16,80},{32,96},{48,112},{64,0},{80,16},{96,32},{112,48},{1... | collective-permute-start | bytes 392 | tf_op jit(solution)/shard_map/ppermute | solution.py:21
  272.7 4.3 %collective-permute-start.9 = (f32[32]{0:T(128)S(1)}, f32[32]{0:T(128)S(1)}, u32[]{:S(2)}, u32[]{:S(2)}) collective-permute-start(f32[32]{0:T(128)S(1)} %add.108), channel_id=1, source_target_pairs={{0,128},{16,144},{32,160},{48,176},{64,192},{80,208},{96,224},{112... | collective-permute-start | bytes 392 | tf_op jit(solution)/shard_map/ppermute | solution.py:21
  277.0 5.8 %collective-permute-start.10 = (f32[32]{0:T(128)S(1)}, f32[32]{0:T(128)S(1)}, u32[]{:S(2)}, u32[]{:S(2)}) collective-permute-start(f32[32]{0:T(128)S(1)} %add.109), channel_id=1, source_target_pairs={{0,256},{16,272},{32,288},{48,304},{64,320},{80,336},{96,352},{112... | collective-permute-start | bytes 392 | tf_op jit(solution)/shard_map/ppermute | solution.py:21
Sparse Core Ops, SparseCore 0:
  109.3 60.9 all-gather.1
  177.9 69.6 reduce-scatter.1

commit v2 on v0

--- a/solution.py
+++ b/solution.py
@@ -11,6 +11,21 @@
     mask = 2**distance
     pairs = [(source, source ^ mask) for source in range(lax.axis_size(axis))]
     return lax.ppermute(value, axis, pairs)
+
+
+def gather_from_all(value, axis):
+    size = lax.axis_size(axis)
+    copies = jnp.broadcast_to(value[None], (size,) + value.shape)
+    got = lax.all_to_all(copies, axis, 0, 0, tiled=True)
+    return got.reshape((size * value.shape[0],) + value.shape[1:])
+
+
+def split_three(value):
+    high = value.astype(jnp.bfloat16)
+    rest = value - high.astype(jnp.float32)
+    middle = rest.astype(jnp.bfloat16)
+    low = (rest - middle.astype(jnp.float32)).astype(jnp.bfloat16)
+    return jnp.stack([high, middle, low], axis=-1)
 
 
 def count_before(sources):
@@ -82,10 +97,9 @@
     rank_in = count_before(source)
     slot_index = source * slot_cap + rank_in
     slot_range = jnp.arange(slot_cap, dtype=jnp.int32)
-    all_parents, all_lengths = (
-        lax.all_gather(parents, "row", axis=0, tiled=True),
-        lax.all_gather(lengths, "row", axis=0, tiled=True),
-    )
+    id_table = gather_from_all(jnp.stack([parents, lengths])[None], "row")
+    all_parents = id_table[:, 0].reshape(-1)
+    all_lengths = id_table[:, 1].reshape(-1)
     parent_table = all_parents.reshape(row_count, beam_count)
     sources_all = parent_table // beam_count
     offsets_all = parent_table % beam_count
@@ -103,21 +117,26 @@
     kept_values = got_values.reshape(row_count * slot_cap, context, panel_width)[slot_index]
     attended = attend(queries, kept_keys, kept_values, new_keys, new_values, all_lengths[parents])
     stream = residual.astype(jnp.float32) + attended.astype(jnp.float32)
-    square_sums = lax.psum(jnp.sum(stream * stream, axis=(1, 2)), "col")
-    scaling = lax.rsqrt(square_sums / D + 1e-05)
-    normed = (stream * norm_gain.astype(jnp.float32)[None] * scaling[:, None, None]).astype(
-        jnp.bfloat16
-    )
-    gathered = lax.all_gather(normed, "row", axis=0, tiled=True)
-    flat_rows = gathered.reshape(gathered.shape[0], group_size * panel_width)
+    square_part = jnp.sum(stream * stream, axis=(1, 2))
+    unscaled = (stream * norm_gain.astype(jnp.float32)[None]).astype(jnp.bfloat16)
+    pieces = split_three(square_part)
+    extra = jnp.zeros((beam_count, 1, panel_width), jnp.bfloat16).at[:, 0, :3].set(pieces)
+    gathered = gather_from_all(jnp.concatenate([unscaled, extra], axis=1), "row")
+    flat_rows = gathered[:, :group_size, :].reshape(gathered.shape[0], group_size * panel_width)
+    square_all = jnp.sum(gathered[:, group_size, :3].astype(jnp.float32), axis=1)
     flat_weight = vocab_weight.reshape(group_size * panel_width, vocab_weight.shape[2])
-    logits = lax.psum_scatter(
-        jnp.dot(flat_rows, flat_weight, preferred_element_type=jnp.float32),
+    partial = jnp.dot(flat_rows, flat_weight, preferred_element_type=jnp.float32)
+    reduced = lax.psum_scatter(
+        jnp.concatenate([partial, square_all[:, None]], axis=1),
         "col",
         scatter_dimension=0,
         tiled=True,
     )
-    totals = lax.psum(jnp.sum(jnp.exp(logits), axis=1), "row")
+    vocab_here = vocab_weight.shape[2]
+    scaling = lax.rsqrt(reduced[:, vocab_here] / D + 1e-05)
+    logits = reduced[:, :vocab_here] * scaling[:, None]
+    exp_sums = gather_from_all(jnp.sum(jnp.exp(logits), axis=1)[None], "row")
+    totals = jnp.sum(exp_sums, axis=0)
     return logits - jnp.log(totals)[:, None]
 
 

time: 323 us -> 221 us (0.68)
  blocking collectives: 114 us -> 47.8 us
  waiting for transfers between devices: 153 us -> 102 us
  local copies, waits for them, and re-layouts: 8.63 us -> 20.2 us
  other arithmetic: 4.38 us -> 7.81 us
  starting transfers between devices: 20.3 us -> 23.6 us
    psum x2 -> x0, blocking collectives: 99.2 us -> none  [the longest x1 73.2 us: body(): totals = lax.psum(jnp.sum(jnp.exp(logits), axis=1), 'row')]
    all_gather x1 -> x0, waiting for transfers between devices: 58.6 us -> none  [body(): gathered = lax.all_gather(normed, 'row', axis=0, tiled=True)]
    all_to_all x0 -> x2, blocking collectives: none -> 47.8 us  [gather_from_all(): got = lax.all_to_all(copies, axis, 0, 0, tiled=True)]
    unnamed x1 -> x0, blocking collectives: 14.4 us -> none
    all_to_all x0 -> x1, starting transfers between devices: none -> 10.3 us  [gather_from_all(): got = lax.all_to_all(copies, axis, 0, 0, tiled=True)]
    unnamed x21 -> x23, local copies, waits for them, and re-layouts: 3.04 us -> 13.1 us
    all_to_all x0 -> x1, waiting for transfers between devices: none -> 7.35 us  [gather_from_all(): got = lax.all_to_all(copies, axis, 0, 0, tiled=True)]
    all_to_all x1, starting transfers between devices: 11 us -> 3.98 us  [body(): lax.all_to_all(cache_keys[rows_sent], 'row', split_axis=0, concat_axis=0,...]
  transfers between devices with their start and end apart: 6 -> 6, of which waited for: 4 -> 4; matrix products, arithmetic and copies ran while one was open for 1% -> 2% of each run, Pallas kernels for 0% -> 0%
where the time goes in v2:
time: 221 us; the launch traced here: 220 us
  waiting for transfers between devices  102 us (46%)
  blocking collectives  47.8 us (22%)
  starting transfers between devices  23.6 us (11%)
  local copies, waits for them, and re-layouts  20.2 us (9%)
  between operations  13.8 us (6%)
  other arithmetic  7.81 us (4%)
  matrix products  5.29 us (2%)
    reduce_scatter x1, waiting for transfers between devices, body(): lax.psum_scatter(jnp.concatenate([partial, square_all[:, None]], axis=1),...  69.3 us
    all_to_all x2, blocking collectives, gather_from_all(): got = lax.all_to_all(copies, axis, 0, 0, tiled=True)  47.8 us
    all_to_all x1, waiting for transfers between devices, body(): lax.all_to_all(cache_keys[rows_sent], 'row', split_axis=0, concat_axis=0,...  15.4 us
    unnamed x23, local copies, waits for them, and re-layouts  13.1 us
    all_to_all x1, starting transfers between devices, gather_from_all(): got = lax.all_to_all(copies, axis, 0, 0, tiled=True)  10.3 us
    all_to_all x1, waiting for transfers between devices, body(): lax.all_to_all(cache_values[rows_sent], 'row', split_axis=0, concat_axis=...  9.74 us
    all_to_all x1, waiting for transfers between devices, gather_from_all(): got = lax.all_to_all(copies, axis, 0, 0, tiled=True)  7.35 us
    ppermute x2, starting transfers between devices, from_partner(): return lax.ppermute(value, axis, pairs)  5.29 us
  transfers between devices with their start and end apart: 6, of which 4 were waited for; matrix products, arithmetic and copies ran while one was open for 2% of the time, Pallas kernels for 0%

profile of v2, /device:TPU:1, one launch (start us, length us, event | category | flops | bytes accessed | tf_op | source)
XLA Modules:
  0.0 220.2 jit_solution(14912016511862020106)
XLA Ops:
  6.5 0.7 pad_add_fusion
  7.3 0.6 broadcast_in_dim.33
  7.9 10.3 %all-to-all-start = ((s32[32,1,2,16]{3,2,1,0:T(2,128)}), s32[32,1,2,16]{3,2,1,0:T(2,128)S(1)}, u32[]{:S(2)}, u32[]{:S(2)}) async-start(s32[32,1,2,16]{3,2,1,0:T(2,128)} %broadcast_in_dim.33), calls=%async_computation | async-start | bytes 65536 | tf_op jit(solution)/shard_map/all_to_all | solution.py:19
  18.3 7.3 %all-to-all-done = s32[32,1,2,16]{3,2,1,0:T(2,128)S(1)} async-done(((s32[32,1,2,16]{3,2,1,0:T(2,128)}), s32[32,1,2,16]{3,2,1,0:T(2,128)S(1)}, u32[]{:S(2)}, u32[]{:S(2)}) %all-to-all-start) | async-done | bytes 4128 | tf_op jit(solution)/shard_map/all_to_all | solution.py:19
  25.6 0.1 copy.54
  25.7 0.1 convert_reduce_fusion.1
  25.9 0.1 copy.55
  26.0 0.1 reshape.223
  26.1 0.0 copy-start.1
  26.1 1.7 gather_fusion.3
  27.8 4.0 %all-to-all-start.2 = ((bf16[32,2,128,64]{2,3,1,0:T(8,128)(2,1)}), bf16[32,2,128,64]{2,3,1,0:T(8,128)(2,1)S(1)}, u32[]{:S(2)}, u32[]{:S(2)}) async-start(bf16[32,2,128,64]{2,3,1,0:T(8,128)(2,1)} %bitcast.10), calls=%async_computation.2 | async-start | bytes 2097152 | tf_op jit(solution)/shard_map/all_to_all | solution.py:112
  31.8 0.0 copy-start.5
  31.8 1.7 gather_fusion
  33.5 15.4 %all-to-all-done.2 = bf16[32,2,128,64]{2,3,1,0:T(8,128)(2,1)S(1)} async-done(((bf16[32,2,128,64]{2,3,1,0:T(8,128)(2,1)}), bf16[32,2,128,64]{2,3,1,0:T(8,128)(2,1)S(1)}, u32[]{:S(2)}, u32[]{:S(2)}) %all-to-all-start.2) | async-done | bytes 1048608 | tf_op jit(solution)/shard_map/all_to_all | solution.py:112
  48.9 4.0 %all-to-all-start.1 = ((bf16[32,2,128,64]{2,3,1,0:T(8,128)(2,1)}), bf16[32,2,128,64]{2,3,1,0:T(8,128)(2,1)S(1)}, u32[]{:S(2)}, u32[]{:S(2)}) async-start(bf16[32,2,128,64]{2,3,1,0:T(8,128)(2,1)} %bitcast.8), calls=%async_computation.1 | async-start | bytes 2097152 | tf_op jit(solution)/shard_map/all_to_all | solution.py:113
  52.9 0.0 reduce-scatter.4.cloned.1.call-start
  53.0 0.2 convert_reduce_fusion.2
  53.2 0.6 gather_fusion.4
  53.8 0.2 convolution_bitcast_fusion.1
  54.0 1.9 collective-permute-start
  56.0 0.1 fusion.21
  56.1 3.4 %collective-permute-start.1 = (f32[16,16,1]{1,0,2:T(8,128)S(1)}, f32[16,16,1]{1,0,2:T(8,128)S(1)}, u32[]{:S(2)}, u32[]{:S(2)}) collective-permute-start(f32[16,16,1]{1,0,2:T(8,128)S(1)} %bitcast.132), channel_id=1, source_target_pairs={{0,1},{1,0},{2,3},{3,2},{4,5},{5,4},{6,7},{7,6},{8,9},{9,8},{10,11... | collective-permute-start | bytes 3080 | tf_op jit(solution)/shard_map/ppermute | solution.py:13
  59.5 0.1 copy.56
  59.6 0.1 reshape_squeeze.3
  59.7 0.7 gather_fusion.2
  60.3 9.7 %all-to-all-done.1 = bf16[32,2,128,64]{2,3,1,0:T(8,128)(2,1)S(1)} async-done(((bf16[32,2,128,64]{2,3,1,0:T(8,128)(2,1)}), bf16[32,2,128,64]{2,3,1,0:T(8,128)(2,1)S(1)}, u32[]{:S(2)}, u32[]{:S(2)}) %all-to-all-start.1) | async-done | bytes 1048608 | tf_op jit(solution)/shard_map/all_to_all | solution.py:113
  70.1 0.6 gather_fusion.1
  70.7 0.2 select_reduce_fusion
  70.9 0.2 fusion.8
  71.2 0.4 multiply_convert_fusion
  71.6 0.1 copy.57
  71.8 0.3 broadcast_bitcast_fusion
  72.1 2.2 reshape.271
  74.3 23.1 %all_to_all.25 = bf16[32,2,8704]{2,1,0:T(2,128)(2,1)} all-to-all(bf16[32,2,8704]{2,1,0:T(2,128)(2,1)} %reshape.271), channel_id=1, replica_groups=mesh['row'=32,'col'=16] {'row'}, dimensions={0} | all-to-all | bytes 2228224 | tf_op jit(solution)/shard_map/all_to_all | solution.py:19
  97.4 3.8 %reshape.272 = bf16[32,17,16,64]{3,2,1,0:T(8,128)(2,1)S(1)} reshape(bf16[32,2,8704]{2,1,0:T(2,128)(2,1)} %all_to_all.25) | data formatting | bytes 2228224
  101.2 0.6 copy.59
  101.8 0.1 convert_reduce_fusion
  102.0 1.5 copy-done.6
  103.4 4.5 %convolution_bitcast_fusion = f32[512,2004]{0,1:T(8,128)S(1)} fusion(bf16[512,17,64]{2,0,1:T(8,128)(2,1)S(1)} %bitcast.125, bf16[16,64,2004]{2,1,0:T(8,128)(2,1)S(1)} %copy-done.6), kind=kOutput, calls=%fused_computation.6 | convolution fusion | flops 2101346304 | bytes 9322496 | tf_op jit(solution)/shard_map/dot_general | solution.py:128
  108.0 2.3 %pad_maximum_fusion = f32[512,2005]{0,1:T(8,128)} fusion(f32[512,1]{0,1:T(1,128)S(1)} %bitcast.135, f32[512,2004]{0,1:T(8,128)S(1)} %convolution_bitcast_fusion), kind=kLoop, calls=%fused_computation.5 | loop fusion | flops 1026560 | bytes 8212480 | tf_op jit(solution)/shard_map/concatenate | solution.py:130
  110.3 5.3 %copy.65 = f32[512,2005]{1,0:T(8,128)} copy(f32[512,2005]{0,1:T(8,128)} %pad_maximum_fusion) | data formatting | bytes 8212480
  115.6 0.0 reduce-scatter.4.cloned.1.call-update
  115.6 69.3 %reduce-scatter.4.cloned.1.call-done = f32[32,2005]{1,0:T(8,128)} async-done(((f32[512,2005]{1,0:T(8,128)}), f32[32,2005]{1,0:T(8,128)}) %reduce-scatter.4.cloned.1.call-update) | async-done | bytes 256656 | tf_op jit(solution)/shard_map/reduce_scatter | solution.py:129
  184.9 0.8 add_rsqrt_fusion
  185.7 0.1 copy.69
  185.8 1.2 exponential_reduce_fusion
  187.0 24.6 %all_to_all.26 = f32[32,1,32]{2,1,0:T(1,128)S(1)} all-to-all(f32[32,1,32]{2,1,0:T(1,128)S(1)} %broadcast_in_dim.44), channel_id=1, replica_groups=mesh['row'=32,'col'=16] {'row'}, dimensions={0} | all-to-all | bytes 8192 | tf_op jit(solution)/shard_map/all_to_all | solution.py:19
  211.6 1.7 fusion.6
  (41 shorter events, 0.3 us)
Async XLA Ops:
  6.5 19.6 %copy-start = (bf16[16,128,64]{1,2,0:T(8,128)(2,1)S(1)}, bf16[16,128,64]{1,2,0:T(8,128)(2,1)}, u32[]{:S(2)}) copy-start(bf16[16,128,64]{1,2,0:T(8,128)(2,1)} %param.15) | copy-start | bytes 786436
  7.9 17.7 %all-to-all-start = ((s32[32,1,2,16]{3,2,1,0:T(2,128)}), s32[32,1,2,16]{3,2,1,0:T(2,128)S(1)}, u32[]{:S(2)}, u32[]{:S(2)}) async-start(s32[32,1,2,16]{3,2,1,0:T(2,128)} %broadcast_in_dim.33), calls=%async_computation | async-start | bytes 65536 | tf_op jit(solution)/shard_map/all_to_all | solution.py:19
  26.1 5.7 %copy-start.1 = (bf16[16,128,64]{1,2,0:T(8,128)(2,1)S(1)}, bf16[16,128,64]{1,2,0:T(8,128)(2,1)}, u32[]{:S(2)}) copy-start(bf16[16,128,64]{1,2,0:T(8,128)(2,1)} %param.16) | copy-start | bytes 786436
  27.8 21.1 %all-to-all-start.2 = ((bf16[32,2,128,64]{2,3,1,0:T(8,128)(2,1)}), bf16[32,2,128,64]{2,3,1,0:T(8,128)(2,1)S(1)}, u32[]{:S(2)}, u32[]{:S(2)}) async-start(bf16[32,2,128,64]{2,3,1,0:T(8,128)(2,1)} %bitcast.10), calls=%async_computation.2 | async-start | bytes 2097152 | tf_op jit(solution)/shard_map/all_to_all | solution.py:112
  31.8 21.2 %copy-start.5 = (s32[16]{0:T(128)S(1)}, s32[16]{0:T(128)}, u32[]{:S(2)}) copy-start(s32[16]{0:T(128)} %param.18) | copy-start | bytes 196
  33.5 20.3 %copy-start.2 = (bf16[16,16,64]{2,1,0:T(8,128)(2,1)S(1)}, bf16[16,16,64]{2,1,0:T(8,128)(2,1)}, u32[]{:S(2)}) copy-start(bf16[16,16,64]{2,1,0:T(8,128)(2,1)} %param.12) | copy-start | bytes 98308
  33.5 22.4 %copy-start.8 = (bf16[16,64]{1,0:T(8,128)(2,1)S(1)}, bf16[16,64]{1,0:T(8,128)(2,1)}, u32[]{:S(2)}) copy-start(bf16[16,64]{1,0:T(8,128)(2,1)} %param.13) | copy-start | bytes 6148
  33.5 25.9 %copy-start.3 = (bf16[16,64]{1,0:T(8,128)(2,1)S(1)}, bf16[16,64]{1,0:T(8,128)(2,1)}, u32[]{:S(2)}) copy-start(bf16[16,64]{1,0:T(8,128)(2,1)} %param.14) | copy-start | bytes 6148
  33.5 26.0 %copy-start.4 = (bf16[16,64]{1,0:T(8,128)(2,1)S(1)}, bf16[16,64]{1,0:T(8,128)(2,1)}, u32[]{:S(2)}) copy-start(bf16[16,64]{1,0:T(8,128)(2,1)} %param.20) | copy-start | bytes 6148
  48.9 21.1 %all-to-all-start.1 = ((bf16[32,2,128,64]{2,3,1,0:T(8,128)(2,1)}), bf16[32,2,128,64]{2,3,1,0:T(8,128)(2,1)S(1)}, u32[]{:S(2)}, u32[]{:S(2)}) async-start(bf16[32,2,128,64]{2,3,1,0:T(8,128)(2,1)} %bitcast.8), calls=%async_computation.1 | async-start | bytes 2097152 | tf_op jit(solution)/shard_map/all_to_all | solution.py:113
  52.9 18.2 %copy-start.7 = (bf16[16,16,64]{2,1,0:T(8,128)(2,1)S(1)}, bf16[16,16,64]{2,1,0:T(8,128)(2,1)}, u32[]{:S(2)}) copy-start(bf16[16,16,64]{2,1,0:T(8,128)(2,1)} %param.19) | copy-start | bytes 98308
  52.9 132.0 %reduce-scatter.4.cloned.1.call-start = ((), (), s32[]{:S(2)}) async-start(), calls=%async_computation.6 | async-start | bytes 4456448 | tf_op jit(solution)/shard_map/reduce_scatter | solution.py:129
  54.0 16.7 %collective-permute-start = (f32[16,16,1,128]{3,1,0,2:T(8,128)S(1)}, f32[16,16,1,128]{3,1,0,2:T(8,128)S(1)}, u32[]{:S(2)}, u32[]{:S(2)}) collective-permute-start(f32[16,16,1,128]{3,1,0,2:T(8,128)S(1)} %convolution_bitcast_fusion.1), channel_id=1, source_target_pairs={{0,1},{1,0},{2,3},{3,2},{4,5},{5,4},{6,7},{7,6},{8,9},{9,8},{10,11... | collective-permute-start | bytes 393224 | tf_op jit(solution)/shard_map/ppermute | solution.py:13
  56.1 14.8 %collective-permute-start.1 = (f32[16,16,1]{1,0,2:T(8,128)S(1)}, f32[16,16,1]{1,0,2:T(8,128)S(1)}, u32[]{:S(2)}, u32[]{:S(2)}) collective-permute-start(f32[16,16,1]{1,0,2:T(8,128)S(1)} %bitcast.132), channel_id=1, source_target_pairs={{0,1},{1,0},{2,3},{3,2},{4,5},{5,4},{6,7},{7,6},{8,9},{9,8},{10,11... | collective-permute-start | bytes 3080 | tf_op jit(solution)/shard_map/ppermute | solution.py:13
  101.2 2.2 copy-start.6
Sparse Core Ops, SparseCore 0:
  115.7 69.1 reduce-scatter.3

commit v3 on v2

--- a/solution.py
+++ b/solution.py
@@ -108,13 +108,11 @@
         ranks_all[:, None, :] == slot_range[None, :, None]
     )
     rows_sent = jnp.sum(jnp.where(chosen, offsets_all[:, None, :], 0), axis=2)
-    got_keys, got_values = (
-        lax.all_to_all(cache_keys[rows_sent], "row", split_axis=0, concat_axis=0, tiled=True),
-        lax.all_to_all(cache_values[rows_sent], "row", split_axis=0, concat_axis=0, tiled=True),
-    )
+    sent = jnp.stack([cache_keys[rows_sent], cache_values[rows_sent]], axis=2)
+    got = lax.all_to_all(sent, "row", split_axis=0, concat_axis=0, tiled=True)
     context = cache_keys.shape[1]
-    kept_keys = got_keys.reshape(row_count * slot_cap, context, panel_width)[slot_index]
-    kept_values = got_values.reshape(row_count * slot_cap, context, panel_width)[slot_index]
+    kept_keys = got[:, :, 0].reshape(row_count * slot_cap, context, panel_width)[slot_index]
+    kept_values = got[:, :, 1].reshape(row_count * slot_cap, context, panel_width)[slot_index]
     attended = attend(queries, kept_keys, kept_values, new_keys, new_values, all_lengths[parents])
     stream = residual.astype(jnp.float32) + attended.astype(jnp.float32)
     square_part = jnp.sum(stream * stream, axis=(1, 2))
@@ -126,15 +124,13 @@
     square_all = jnp.sum(gathered[:, group_size, :3].astype(jnp.float32), axis=1)
     flat_weight = vocab_weight.reshape(group_size * panel_width, vocab_weight.shape[2])
     partial = jnp.dot(flat_rows, flat_weight, preferred_element_type=jnp.float32)
-    reduced = lax.psum_scatter(
-        jnp.concatenate([partial, square_all[:, None]], axis=1),
-        "col",
-        scatter_dimension=0,
-        tiled=True,
+    reduced = lax.psum_scatter(partial, "col", scatter_dimension=0, tiled=True)
+    col_count = lax.axis_size("col")
+    square_parts = lax.all_to_all(
+        square_all.reshape(col_count, -1), "col", split_axis=0, concat_axis=0, tiled=True
     )
-    vocab_here = vocab_weight.shape[2]
-    scaling = lax.rsqrt(reduced[:, vocab_here] / D + 1e-05)
-    logits = reduced[:, :vocab_here] * scaling[:, None]
+    scaling = lax.rsqrt(jnp.sum(square_parts, axis=0) / D + 1e-05)
+    logits = reduced * scaling[:, None]
     exp_sums = gather_from_all(jnp.sum(jnp.exp(logits), axis=1)[None], "row")
     totals = jnp.sum(exp_sums, axis=0)
     return logits - jnp.log(totals)[:, None]

time: 221 us -> 217 us (0.982)
  blocking collectives: 47.8 us -> 75.4 us
  waiting for transfers between devices: 102 us -> 79.1 us
  local copies, waits for them, and re-layouts: 20.2 us -> 16.4 us
  starting transfers between devices: 23.6 us -> 19.9 us
    reduce_scatter x1, waiting for transfers between devices: 69.3 us -> 43.7 us  [body(): reduced = lax.psum_scatter(partial, 'col', scatter_dimension=0, tiled=True)]
    all_to_all x0 -> x1, blocking collectives: none -> 25.2 us  [body(): lax.all_to_all(square_all.reshape(col_count, -1), 'col', split_axis=0, co...]
    unnamed x23, local copies, waits for them, and re-layouts: 13.1 us -> 8.73 us
    all_to_all x2 -> x1, starting transfers between devices: 7.96 us -> 4.19 us  [body(): got = lax.all_to_all(sent, 'row', split_axis=0, concat_axis=0, tiled=True)]
    all_to_all x2 -> x1, waiting for transfers between devices: 25.2 us -> 28 us  [body(): got = lax.all_to_all(sent, 'row', split_axis=0, concat_axis=0, tiled=True)]
    all_to_all x2, blocking collectives: 47.8 us -> 50.2 us  [gather_from_all(): got = lax.all_to_all(copies, axis, 0, 0, tiled=True)]
    concatenate x1 -> x0, other arithmetic: 2.35 us -> none  [body(): jnp.concatenate([partial, square_all[:, None]], axis=1)]
  transfers between devices with their start and end apart: 6 -> 5, of which waited for: 4 -> 3; matrix products, arithmetic and copies ran while one was open for 2% -> 1% of each run, Pallas kernels for 0% -> 0%
where the time goes in v3:
time: 217 us; the launch traced here: 216 us
  waiting for transfers between devices  79.1 us (36%)
  blocking collectives  75.4 us (35%)
  starting transfers between devices  19.9 us (9%)
  local copies, waits for them, and re-layouts  16.4 us (8%)
  between operations  13.8 us (6%)
  other arithmetic  7.12 us (3%)
  matrix products  4.72 us (2%)
    all_to_all x2, blocking collectives, gather_from_all(): got = lax.all_to_all(copies, axis, 0, 0, tiled=True)  50.2 us
    reduce_scatter x1, waiting for transfers between devices, body(): reduced = lax.psum_scatter(partial, 'col', scatter_dimension=0, tiled=True)  43.7 us
    all_to_all x1, waiting for transfers between devices, body(): got = lax.all_to_all(sent, 'row', split_axis=0, concat_axis=0, tiled=True)  28 us
    all_to_all x1, blocking collectives, body(): lax.all_to_all(square_all.reshape(col_count, -1), 'col', split_axis=0, co...  25.2 us
    all_to_all x1, starting transfers between devices, gather_from_all(): got = lax.all_to_all(copies, axis, 0, 0, tiled=True)  10.3 us
    unnamed x23, local copies, waits for them, and re-layouts  8.73 us
    all_to_all x1, waiting for transfers between devices, gather_from_all(): got = lax.all_to_all(copies, axis, 0, 0, tiled=True)  7.34 us
    ppermute x2, starting transfers between devices, from_partner(): return lax.ppermute(value, axis, pairs)  5.29 us
  transfers between devices with their start and end apart: 5, of which 3 were waited for; matrix products, arithmetic and copies ran while one was open for 1% of the time, Pallas kernels for 0%

profile of v3, /device:TPU:1, one launch (start us, length us, event | category | flops | bytes accessed | tf_op | source)
XLA Modules:
  0.0 216.3 jit_solution(14217077998953982297)
XLA Ops:
  6.5 0.7 pad_add_fusion
  7.3 0.6 broadcast_in_dim.30
  7.9 10.3 %all-to-all-start = ((s32[32,1,2,16]{3,2,1,0:T(2,128)}), s32[32,1,2,16]{3,2,1,0:T(2,128)S(1)}, u32[]{:S(2)}, u32[]{:S(2)}) async-start(s32[32,1,2,16]{3,2,1,0:T(2,128)} %broadcast_in_dim.30), calls=%async_computation | async-start | bytes 65536 | tf_op jit(solution)/shard_map/all_to_all | solution.py:19
  18.2 0.0 copy-start.1
  18.3 7.3 %all-to-all-done = s32[32,1,2,16]{3,2,1,0:T(2,128)S(1)} async-done(((s32[32,1,2,16]{3,2,1,0:T(2,128)}), s32[32,1,2,16]{3,2,1,0:T(2,128)S(1)}, u32[]{:S(2)}, u32[]{:S(2)}) %all-to-all-start) | async-done | bytes 4128 | tf_op jit(solution)/shard_map/all_to_all | solution.py:19
  25.6 0.1 copy.41
  25.7 0.1 convert_reduce_fusion.1
  25.9 0.1 copy.42
  26.0 0.1 reshape.224
  26.1 0.7 gather_fusion.1
  26.9 0.7 gather_fusion
  27.6 1.5 pad_maximum_fusion
  29.2 4.2 %all-to-all-start.1 = ((bf16[32,2,2,128,64]{3,4,1,2,0:T(8,128)(2,1)}), bf16[32,2,2,128,64]{3,4,1,2,0:T(8,128)(2,1)S(1)}, u32[]{:S(2)}, u32[]{:S(2)}) async-start(bf16[32,2,2,128,64]{3,4,1,2,0:T(8,128)(2,1)} %pad_maximum_fusion), calls=%async_computation.1 | async-start | bytes 4194304 | tf_op jit(solution)/shard_map/all_to_all | solution.py:112
  33.4 0.0 reduce-scatter.2.cloned.1.call-start
  33.5 0.2 convert_reduce_fusion.2
  33.7 0.0 copy-start.3
  33.7 0.0 copy-start.9
  33.7 28.0 %all-to-all-done.1 = bf16[32,2,2,128,64]{3,4,1,2,0:T(8,128)(2,1)S(1)} async-done(((bf16[32,2,2,128,64]{3,4,1,2,0:T(8,128)(2,1)}), bf16[32,2,2,128,64]{3,4,1,2,0:T(8,128)(2,1)S(1)}, u32[]{:S(2)}, u32[]{:S(2)}) %all-to-all-start.1) | async-done | bytes 2097184 | tf_op jit(solution)/shard_map/all_to_all | solution.py:112
  61.7 1.2 fusion.31
  62.9 1.9 gather_fusion.4
  64.8 0.2 convolution_bitcast_fusion.1
  65.0 1.9 collective-permute-start
  66.9 0.1 fusion.20
  67.0 3.4 %collective-permute-start.1 = (f32[16,16,1]{1,0,2:T(8,128)S(1)}, f32[16,16,1]{1,0,2:T(8,128)S(1)}, u32[]{:S(2)}, u32[]{:S(2)}) collective-permute-start(f32[16,16,1]{1,0,2:T(8,128)S(1)} %bitcast.133), channel_id=1, source_target_pairs={{0,1},{1,0},{2,3},{3,2},{4,5},{5,4},{6,7},{7,6},{8,9},{9,8},{10,11... | collective-permute-start | bytes 3080 | tf_op jit(solution)/shard_map/ppermute | solution.py:13
  70.5 0.1 copy.43
  70.6 0.1 reshape_squeeze.10
  70.6 0.7 gather_fusion.3
  71.3 0.6 gather_fusion.2
  71.9 0.2 select_reduce_fusion
  72.1 0.2 fusion.7
  72.4 0.4 multiply_convert_fusion
  72.8 0.1 copy.44
  73.0 0.3 broadcast_bitcast_fusion
  73.3 2.2 %reshape.272 = bf16[32,2,8704]{2,1,0:T(2,128)(2,1)} reshape(bf16[32,17,16,64]{3,2,1,0:T(8,128)(2,1)S(1)} %broadcast_bitcast_fusion) | data formatting | bytes 2228224
  75.5 25.4 %all_to_all.29 = bf16[32,2,8704]{2,1,0:T(2,128)(2,1)} all-to-all(bf16[32,2,8704]{2,1,0:T(2,128)(2,1)} %reshape.272), channel_id=1, replica_groups=mesh['row'=32,'col'=16] {'row'}, dimensions={0} | all-to-all | bytes 2228224 | tf_op jit(solution)/shard_map/all_to_all | solution.py:19
  100.9 3.8 %reshape.273 = bf16[32,17,16,64]{3,2,1,0:T(8,128)(2,1)S(1)} reshape(bf16[32,2,8704]{2,1,0:T(2,128)(2,1)} %all_to_all.29) | data formatting | bytes 2228224
  104.8 0.6 copy.46
  105.4 1.4 copy-done.2
  106.7 1.0 copy-done.7
  107.7 4.0 %convolution_bitcast_fusion = f32[512,2004]{1,0:T(8,128)} fusion(bf16[512,17,64]{2,0,1:T(8,128)(2,1)S(1)} %bitcast.124, bf16[16,64,2004]{2,1,0:T(8,128)(2,1)S(1)} %copy-done.7), kind=kOutput, calls=%fused_computation.5 | convolution fusion | flops 2101346304 | bytes 9322496 | tf_op jit(solution)/shard_map/dot_general | solution.py:126
  111.7 0.0 reduce-scatter.2.cloned.1.call-update
  111.7 1.0 convert_reduce_fusion
  112.8 0.1 all_to_all.21
  112.8 25.2 %all_to_all.30 = f32[16,1,32]{2,1,0:T(1,128)S(1)} all-to-all(f32[16,1,32]{2,1,0:T(1,128)S(1)} %all_to_all.21), channel_id=1, replica_groups=mesh['row'=32,'col'=16] {'col'}, dimensions={0} | all-to-all | bytes 4096 | tf_op jit(solution)/shard_map/all_to_all | solution.py:129
  138.1 43.7 %reduce-scatter.2.cloned.1.call-done = f32[32,2004]{1,0:T(8,128)} async-done(((f32[512,2004]{1,0:T(8,128)}), f32[32,2004]{1,0:T(8,128)}) %reduce-scatter.2.cloned.1.call-update) | async-done | bytes 256528 | tf_op jit(solution)/shard_map/reduce_scatter | solution.py:127
  181.8 1.2 exponential_reduce_fusion
  183.0 24.7 %all_to_all.31 = f32[32,1,32]{2,1,0:T(1,128)S(1)} all-to-all(f32[32,1,32]{2,1,0:T(1,128)S(1)} %broadcast_in_dim.41), channel_id=1, replica_groups=mesh['row'=32,'col'=16] {'row'}, dimensions={0} | all-to-all | bytes 8192 | tf_op jit(solution)/shard_map/all_to_all | solution.py:19
  207.7 1.7 multiply_subtract_fusion
  (43 shorter events, 0.3 us)
Async XLA Ops:
  6.5 19.6 %copy-start = (bf16[16,128,64]{1,2,0:T(8,128)(2,1)S(1)}, bf16[16,128,64]{1,2,0:T(8,128)(2,1)}, u32[]{:S(2)}) copy-start(bf16[16,128,64]{1,2,0:T(8,128)(2,1)} %param.16) | copy-start | bytes 786436
  7.9 17.7 %all-to-all-start = ((s32[32,1,2,16]{3,2,1,0:T(2,128)}), s32[32,1,2,16]{3,2,1,0:T(2,128)S(1)}, u32[]{:S(2)}, u32[]{:S(2)}) async-start(s32[32,1,2,16]{3,2,1,0:T(2,128)} %broadcast_in_dim.30), calls=%async_computation | async-start | bytes 65536 | tf_op jit(solution)/shard_map/all_to_all | solution.py:19
  18.2 8.6 %copy-start.1 = (bf16[16,128,64]{1,2,0:T(8,128)(2,1)S(1)}, bf16[16,128,64]{1,2,0:T(8,128)(2,1)}, u32[]{:S(2)}) copy-start(bf16[16,128,64]{1,2,0:T(8,128)(2,1)} %param.15) | copy-start | bytes 786436
  29.2 4.3 %copy-start.6 = (s32[16]{0:T(128)S(1)}, s32[16]{0:T(128)}, u32[]{:S(2)}) copy-start(s32[16]{0:T(128)} %param.18) | copy-start | bytes 196
  29.2 32.5 %all-to-all-start.1 = ((bf16[32,2,2,128,64]{3,4,1,2,0:T(8,128)(2,1)}), bf16[32,2,2,128,64]{3,4,1,2,0:T(8,128)(2,1)S(1)}, u32[]{:S(2)}, u32[]{:S(2)}) async-start(bf16[32,2,2,128,64]{3,4,1,2,0:T(8,128)(2,1)} %pad_maximum_fusion), calls=%async_computation.1 | async-start | bytes 4194304 | tf_op jit(solution)/shard_map/all_to_all | solution.py:112
  33.4 148.4 %reduce-scatter.2.cloned.1.call-start = ((), (), s32[]{:S(2)}) async-start(), calls=%async_computation.6 | async-start | bytes 4456448 | tf_op jit(solution)/shard_map/reduce_scatter | solution.py:127
  33.7 31.1 %copy-start.3 = (bf16[16,16,64]{2,1,0:T(8,128)(2,1)S(1)}, bf16[16,16,64]{2,1,0:T(8,128)(2,1)}, u32[]{:S(2)}) copy-start(bf16[16,16,64]{2,1,0:T(8,128)(2,1)} %param.12) | copy-start | bytes 98308
  33.7 33.2 %copy-start.9 = (bf16[16,64]{1,0:T(8,128)(2,1)S(1)}, bf16[16,64]{1,0:T(8,128)(2,1)}, u32[]{:S(2)}) copy-start(bf16[16,64]{1,0:T(8,128)(2,1)} %param.13) | copy-start | bytes 6148
  33.7 36.7 %copy-start.4 = (bf16[16,64]{1,0:T(8,128)(2,1)S(1)}, bf16[16,64]{1,0:T(8,128)(2,1)}, u32[]{:S(2)}) copy-start(bf16[16,64]{1,0:T(8,128)(2,1)} %param.14) | copy-start | bytes 6148
  33.7 36.8 %copy-start.5 = (bf16[16,64]{1,0:T(8,128)(2,1)S(1)}, bf16[16,64]{1,0:T(8,128)(2,1)}, u32[]{:S(2)}) copy-start(bf16[16,64]{1,0:T(8,128)(2,1)} %param.20) | copy-start | bytes 6148
  62.9 9.5 %copy-start.8 = (bf16[16,16,64]{2,1,0:T(8,128)(2,1)S(1)}, bf16[16,16,64]{2,1,0:T(8,128)(2,1)}, u32[]{:S(2)}) copy-start(bf16[16,16,64]{2,1,0:T(8,128)(2,1)} %param.19) | copy-start | bytes 98308
  65.0 6.9 %collective-permute-start = (f32[16,16,1,128]{3,1,0,2:T(8,128)S(1)}, f32[16,16,1,128]{3,1,0,2:T(8,128)S(1)}, u32[]{:S(2)}, u32[]{:S(2)}) collective-permute-start(f32[16,16,1,128]{3,1,0,2:T(8,128)S(1)} %convolution_bitcast_fusion.1), channel_id=1, source_target_pairs={{0,1},{1,0},{2,3},{3,2},{4,5},{5,4},{6,7},{7,6},{8,9},{9,8},{10,11... | collective-permute-start | bytes 393224 | tf_op jit(solution)/shard_map/ppermute | solution.py:13
  67.0 5.1 %collective-permute-start.1 = (f32[16,16,1]{1,0,2:T(8,128)S(1)}, f32[16,16,1]{1,0,2:T(8,128)S(1)}, u32[]{:S(2)}, u32[]{:S(2)}) collective-permute-start(f32[16,16,1]{1,0,2:T(8,128)S(1)} %bitcast.133), channel_id=1, source_target_pairs={{0,1},{1,0},{2,3},{3,2},{4,5},{5,4},{6,7},{7,6},{8,9},{9,8},{10,11... | collective-permute-start | bytes 3080 | tf_op jit(solution)/shard_map/ppermute | solution.py:13
  104.8 3.0 %copy-start.7 = (bf16[16,64,2004]{2,1,0:T(8,128)(2,1)S(1)}, bf16[16,64,2004]{2,1,0:T(8,128)(2,1)}, u32[]{:S(2)}) copy-start(bf16[16,64,2004]{2,1,0:T(8,128)(2,1)} %param.21) | copy-start | bytes 12312580
  105.3 1.4 copy-start.2
Sparse Core Ops, SparseCore 0:
  111.9 69.8 reduce-scatter.1

commit v4 on v3

--- a/solution.py
+++ b/solution.py
@@ -116,19 +116,25 @@
     attended = attend(queries, kept_keys, kept_values, new_keys, new_values, all_lengths[parents])
     stream = residual.astype(jnp.float32) + attended.astype(jnp.float32)
     square_part = jnp.sum(stream * stream, axis=(1, 2))
+    width = group_size * panel_width
     unscaled = (stream * norm_gain.astype(jnp.float32)[None]).astype(jnp.bfloat16)
-    pieces = split_three(square_part)
-    extra = jnp.zeros((beam_count, 1, panel_width), jnp.bfloat16).at[:, 0, :3].set(pieces)
-    gathered = gather_from_all(jnp.concatenate([unscaled, extra], axis=1), "row")
-    flat_rows = gathered[:, :group_size, :].reshape(gathered.shape[0], group_size * panel_width)
-    square_all = jnp.sum(gathered[:, group_size, :3].astype(jnp.float32), axis=1)
-    flat_weight = vocab_weight.reshape(group_size * panel_width, vocab_weight.shape[2])
-    partial = jnp.dot(flat_rows, flat_weight, preferred_element_type=jnp.float32)
-    reduced = lax.psum_scatter(partial, "col", scatter_dimension=0, tiled=True)
+    extra = jnp.zeros((beam_count, 128), jnp.bfloat16).at[:, :3].set(split_three(square_part))
+    packed = jnp.concatenate([unscaled.reshape(beam_count, width), extra], axis=1)
+    flat_weight = vocab_weight.reshape(width, vocab_weight.shape[2])
     col_count = lax.axis_size("col")
-    square_parts = lax.all_to_all(
-        square_all.reshape(col_count, -1), "col", split_axis=0, concat_axis=0, tiled=True
-    )
+    chunks = 2
+    step = beam_count // chunks
+    reduced_parts, square_chunks = [], []
+    for chunk in range(chunks):
+        gathered = gather_from_all(packed[chunk * step : (chunk + 1) * step], "row")
+        partial = jnp.dot(gathered[:, :width], flat_weight, preferred_element_type=jnp.float32)
+        reduced = lax.psum_scatter(partial, "col", scatter_dimension=0, tiled=True)
+        reduced_parts.append(reduced.reshape(-1, step, reduced.shape[-1]))
+        squares = jnp.sum(gathered[:, width : width + 3].astype(jnp.float32), axis=1)
+        square_chunks.append(squares.reshape(col_count, -1, step))
+    reduced = jnp.stack(reduced_parts, axis=1).reshape(-1, flat_weight.shape[1])
+    square_all = jnp.stack(square_chunks, axis=2).reshape(col_count, -1)
+    square_parts = lax.all_to_all(square_all, "col", split_axis=0, concat_axis=0, tiled=True)
     scaling = lax.rsqrt(jnp.sum(square_parts, axis=0) / D + 1e-05)
     logits = reduced * scaling[:, None]
     exp_sums = gather_from_all(jnp.sum(jnp.exp(logits), axis=1)[None], "row")

time: 217 us -> 269 us (1.24)
  waiting for transfers between devices: 79.1 us -> 133 us
  starting transfers between devices: 19.9 us -> 37.9 us
  blocking collectives: 75.4 us -> 58 us
  local copies, waits for them, and re-layouts: 16.4 us -> 8.8 us
  matrix products: 4.72 us -> 10.3 us
    reduce_scatter x1 -> x2, waiting for transfers between devices: 43.7 us -> 91.3 us  [body(): reduced = lax.psum_scatter(partial, 'col', scatter_dimension=0, tiled=True)]
    all_to_all x1 -> x2, starting transfers between devices: 10.3 us -> 28.4 us  [gather_from_all(): got = lax.all_to_all(copies, axis, 0, 0, tiled=True)]
    all_to_all x2, blocking collectives: 50.2 us -> 33.3 us  [gather_from_all(): got = lax.all_to_all(copies, axis, 0, 0, tiled=True)]
    unnamed x23 -> x19, local copies, waits for them, and re-layouts: 8.73 us -> 0.49 us
    all_to_all x1 -> x2, waiting for transfers between devices: 7.34 us -> 14.2 us  [gather_from_all(): got = lax.all_to_all(copies, axis, 0, 0, tiled=True)]
    dot_general x1 -> x2, matrix products: 3.97 us -> 9.53 us  [body(): jnp.dot(gathered[:, :width], flat_weight, preferred_element_type=jnp.floa...]
  transfers between devices with their start and end apart: 5 -> 7, of which waited for: 3 -> 5; matrix products, arithmetic and copies ran while one was open for 1% -> 3% of each run, Pallas kernels for 0% -> 0%
where the time goes in v4:
time: 269 us
  waiting for transfers between devices  133 us (49%)
  blocking collectives  58 us (22%)
  starting transfers between devices  37.9 us (14%)
  between operations  13.8 us (5%)
  matrix products  10.3 us (4%)
  local copies, waits for them, and re-layouts  8.8 us (3%)
  other arithmetic  6.51 us (2%)
    reduce_scatter x2, waiting for transfers between devices, body(): reduced = lax.psum_scatter(partial, 'col', scatter_dimension=0, tiled=True)  91.3 us
    all_to_all x2, blocking collectives, gather_from_all(): got = lax.all_to_all(copies, axis, 0, 0, tiled=True)  33.3 us
    all_to_all x2, starting transfers between devices, gather_from_all(): got = lax.all_to_all(copies, axis, 0, 0, tiled=True)  28.4 us
    all_to_all x1, waiting for transfers between devices, body(): got = lax.all_to_all(sent, 'row', split_axis=0, concat_axis=0, tiled=True)  28 us
    all_to_all x1, blocking collectives, body(): lax.all_to_all(square_all, 'col', split_axis=0, concat_axis=0, tiled=True)  24.7 us
    all_to_all x2, waiting for transfers between devices, gather_from_all(): got = lax.all_to_all(copies, axis, 0, 0, tiled=True)  14.2 us
    dot_general x2, matrix products, body(): jnp.dot(gathered[:, :width], flat_weight, preferred_element_type=jnp.floa...  9.53 us
  transfers between devices with their start and end apart: 7, of which 5 were waited for; matrix products, arithmetic and copies ran while one was open for 3% of the time, Pallas kernels for 0%

profile of v4, /device:TPU:1, one launch (start us, length us, event | category | flops | bytes accessed | tf_op | source)
XLA Modules:
  0.0 268.8 jit_solution(11953502437589972609)
XLA Ops:
  6.5 0.7 pad_add_fusion
  7.3 0.6 broadcast_in_dim.36
  7.9 10.3 %all-to-all-start = ((s32[32,1,2,16]{3,2,1,0:T(2,128)}), s32[32,1,2,16]{3,2,1,0:T(2,128)S(1)}, u32[]{:S(2)}, u32[]{:S(2)}) async-start(s32[32,1,2,16]{3,2,1,0:T(2,128)} %broadcast_in_dim.36), calls=%async_computation | async-start | bytes 65536 | tf_op jit(solution)/shard_map/all_to_all | solution.py:19
  18.3 7.3 %all-to-all-done = s32[32,1,2,16]{3,2,1,0:T(2,128)S(1)} async-done(((s32[32,1,2,16]{3,2,1,0:T(2,128)}), s32[32,1,2,16]{3,2,1,0:T(2,128)S(1)}, u32[]{:S(2)}, u32[]{:S(2)}) %all-to-all-start) | async-done | bytes 4128 | tf_op jit(solution)/shard_map/all_to_all | solution.py:19
  25.7 0.1 convert_reduce_fusion
  25.9 0.1 copy.73
  26.0 0.1 reshape.238
  26.1 0.7 gather_fusion
  26.9 0.2 copy-done.1
  27.1 0.7 gather_fusion.1
  27.8 1.5 pad_maximum_fusion
  29.4 4.2 %all-to-all-start.1 = ((bf16[32,2,2,128,64]{3,4,1,2,0:T(8,128)(2,1)}), bf16[32,2,2,128,64]{3,4,1,2,0:T(8,128)(2,1)S(1)}, u32[]{:S(2)}, u32[]{:S(2)}) async-start(bf16[32,2,2,128,64]{3,4,1,2,0:T(8,128)(2,1)} %pad_maximum_fusion), calls=%async_computation.1 | async-start | bytes 4194304 | tf_op jit(solution)/shard_map/all_to_all | solution.py:112
  33.6 0.2 convert_reduce_fusion.1
  33.9 28.0 %all-to-all-done.1 = bf16[32,2,2,128,64]{3,4,1,2,0:T(8,128)(2,1)S(1)} async-done(((bf16[32,2,2,128,64]{3,4,1,2,0:T(8,128)(2,1)}), bf16[32,2,2,128,64]{3,4,1,2,0:T(8,128)(2,1)S(1)}, u32[]{:S(2)}, u32[]{:S(2)}) %all-to-all-start.1) | async-done | bytes 2097184 | tf_op jit(solution)/shard_map/all_to_all | solution.py:112
  61.9 1.2 fusion.36
  63.1 1.9 gather_fusion.4
  65.0 0.2 convolution_bitcast_fusion
  65.2 1.9 collective-permute-start
  67.1 0.1 fusion.25
  67.2 3.4 %collective-permute-start.1 = (f32[16,16,1]{1,0,2:T(8,128)S(1)}, f32[16,16,1]{1,0,2:T(8,128)S(1)}, u32[]{:S(2)}, u32[]{:S(2)}) collective-permute-start(f32[16,16,1]{1,0,2:T(8,128)S(1)} %bitcast.137), channel_id=1, source_target_pairs={{0,1},{1,0},{2,3},{3,2},{4,5},{5,4},{6,7},{7,6},{8,9},{9,8},{10,11... | collective-permute-start | bytes 3080 | tf_op jit(solution)/shard_map/ppermute | solution.py:13
  70.7 0.6 compare_reduce_fusion
  71.4 0.1 reshape_squeeze.10
  71.5 0.7 gather_fusion.3
  72.1 0.6 gather_fusion.2
  72.7 0.2 select_reduce_fusion
  72.9 0.2 fusion.11
  73.2 0.4 multiply_convert_fusion
  73.6 0.1 reshape.229
  73.8 0.7 maximum_select_fusion
  74.4 0.1 copy.88
  74.6 17.6 %all_to_all.34 = bf16[32,8,1152]{2,1,0:T(8,128)(2,1)S(1)} all-to-all(bf16[32,8,1152]{2,1,0:T(8,128)(2,1)S(1)} %broadcast_in_dim.44), channel_id=1, replica_groups=mesh['row'=32,'col'=16] {'row'}, dimensions={0} | all-to-all | bytes 1179648 | tf_op jit(solution)/shard_map/all_to_all | solution.py:19
  92.2 4.8 %fusion.8 = f32[256,2004]{1,0:T(8,128)} fusion(bf16[1024,2004]{1,0:T(8,128)(2,1)} %bitcast.142, bf16[256,1152]{1,0:T(8,128)(2,1)S(1)} %bitcast.126), kind=kOutput, calls=%fused_computation.16 | convolution fusion | flops 1050673152 | bytes 6680576 | tf_op jit(solution)/shard_map/dot_general | solution.py:130
  97.1 15.8 %all_to_all.35 = bf16[32,8,1152]{2,1,0:T(8,128)(2,1)S(1)} all-to-all(bf16[32,8,1152]{2,1,0:T(8,128)(2,1)S(1)} %broadcast_in_dim.45), channel_id=1, replica_groups=mesh['row'=32,'col'=16] {'row'}, dimensions={0} | all-to-all | bytes 1179648 | tf_op jit(solution)/shard_map/all_to_all | solution.py:19
  112.9 4.7 %fusion.6 = f32[256,2004]{1,0:T(8,128)} fusion(bf16[1024,2004]{1,0:T(8,128)(2,1)} %bitcast.143, bf16[256,1152]{1,0:T(8,128)(2,1)S(1)} %bitcast.128), kind=kOutput, calls=%fused_computation.14 | convolution fusion | flops 1050673152 | bytes 6680576 | tf_op jit(solution)/shard_map/dot_general | solution.py:130
  117.6 0.1 copy.86
  117.8 0.1 stack_reshape.14
  117.9 0.1 copy.87
  118.0 0.1 stack_reshape.15
  118.3 24.7 %all_to_all.36 = f32[16,1,32]{2,1,0:T(1,128)S(1)} all-to-all(f32[16,1,32]{2,1,0:T(1,128)S(1)} %copy.80), channel_id=1, replica_groups=mesh['row'=32,'col'=16] {'col'}, dimensions={0} | all-to-all | bytes 4096 | tf_op jit(solution)/shard_map/all_to_all | solution.py:137
  143.0 0.1 rsqrt.12
  143.1 17.1 %reduce-scatter.3.cloned.1.call-done = f32[16,2004]{1,0:T(8,128)} async-done(((f32[256,2004]{1,0:T(8,128)}), f32[16,2004]{1,0:T(8,128)}) %reduce-scatter.3.cloned.1.call-update) | async-done | bytes 128272 | tf_op jit(solution)/shard_map/reduce_scatter | solution.py:131
  160.2 74.1 %reduce-scatter.5.cloned.1.call-done = f32[16,2004]{1,0:T(8,128)} async-done(((f32[256,2004]{1,0:T(8,128)}), f32[16,2004]{1,0:T(8,128)}) %reduce-scatter.5.cloned.1.call-update) | async-done | bytes 128272 | tf_op jit(solution)/shard_map/reduce_scatter | solution.py:131
  234.3 1.2 exponential_reduce_fusion
  235.5 0.1 broadcast_in_dim.46
  235.6 0.6 broadcast_in_dim.47
  236.2 18.0 %all-to-all-start.5 = ((f32[32,1,32]{2,1,0:T(1,128)}), f32[32,1,32]{2,1,0:T(1,128)S(1)}, u32[]{:S(2)}, u32[]{:S(2)}) async-start(f32[32,1,32]{2,1,0:T(1,128)} %broadcast_in_dim.47), calls=%async_computation.7 | async-start | bytes 32768 | tf_op jit(solution)/shard_map/all_to_all | solution.py:19
  254.3 6.9 %all-to-all-done.5 = f32[32,1,32]{2,1,0:T(1,128)S(1)} async-done(((f32[32,1,32]{2,1,0:T(1,128)}), f32[32,1,32]{2,1,0:T(1,128)S(1)}, u32[]{:S(2)}, u32[]{:S(2)}) %all-to-all-start.5) | async-done | bytes 4128 | tf_op jit(solution)/shard_map/all_to_all | solution.py:19
  261.2 0.8 fusion.10
  (59 shorter events, 0.9 us)
Async XLA Ops:
  6.5 19.6 %copy-start = (bf16[16,128,64]{1,2,0:T(8,128)(2,1)S(1)}, bf16[16,128,64]{1,2,0:T(8,128)(2,1)}, u32[]{:S(2)}) copy-start(bf16[16,128,64]{1,2,0:T(8,128)(2,1)} %param.15) | copy-start | bytes 786436
  7.9 17.7 %all-to-all-start = ((s32[32,1,2,16]{3,2,1,0:T(2,128)}), s32[32,1,2,16]{3,2,1,0:T(2,128)S(1)}, u32[]{:S(2)}, u32[]{:S(2)}) async-start(s32[32,1,2,16]{3,2,1,0:T(2,128)} %broadcast_in_dim.36), calls=%async_computation | async-start | bytes 65536 | tf_op jit(solution)/shard_map/all_to_all | solution.py:19
  26.1 1.0 copy-start.1
  29.4 4.3 %copy-start.5 = (s32[16]{0:T(128)S(1)}, s32[16]{0:T(128)}, u32[]{:S(2)}) copy-start(s32[16]{0:T(128)} %param.18) | copy-start | bytes 196
  29.4 32.5 %all-to-all-start.1 = ((bf16[32,2,2,128,64]{3,4,1,2,0:T(8,128)(2,1)}), bf16[32,2,2,128,64]{3,4,1,2,0:T(8,128)(2,1)S(1)}, u32[]{:S(2)}, u32[]{:S(2)}) async-start(bf16[32,2,2,128,64]{3,4,1,2,0:T(8,128)(2,1)} %pad_maximum_fusion), calls=%async_computation.1 | async-start | bytes 4194304 | tf_op jit(solution)/shard_map/all_to_all | solution.py:112
  33.6 126.7 %reduce-scatter.3.cloned.1.call-start = ((), (), s32[]{:S(2)}) async-start(), calls=%async_computation.8 | async-start | bytes 2228224 | tf_op jit(solution)/shard_map/reduce_scatter | solution.py:131
  33.8 31.1 %copy-start.2 = (bf16[16,16,64]{2,1,0:T(8,128)(2,1)S(1)}, bf16[16,16,64]{2,1,0:T(8,128)(2,1)}, u32[]{:S(2)}) copy-start(bf16[16,16,64]{2,1,0:T(8,128)(2,1)} %param.12) | copy-start | bytes 98308
  33.9 33.2 %copy-start.7 = (bf16[16,64]{1,0:T(8,128)(2,1)S(1)}, bf16[16,64]{1,0:T(8,128)(2,1)}, u32[]{:S(2)}) copy-start(bf16[16,64]{1,0:T(8,128)(2,1)} %param.13) | copy-start | bytes 6148
  33.9 36.7 %copy-start.3 = (bf16[16,64]{1,0:T(8,128)(2,1)S(1)}, bf16[16,64]{1,0:T(8,128)(2,1)}, u32[]{:S(2)}) copy-start(bf16[16,64]{1,0:T(8,128)(2,1)} %param.14) | copy-start | bytes 6148
  33.9 36.8 %copy-start.4 = (bf16[16,64]{1,0:T(8,128)(2,1)S(1)}, bf16[16,64]{1,0:T(8,128)(2,1)}, u32[]{:S(2)}) copy-start(bf16[16,64]{1,0:T(8,128)(2,1)} %param.20) | copy-start | bytes 6148
  63.1 10.1 %copy-start.6 = (bf16[16,16,64]{2,1,0:T(8,128)(2,1)S(1)}, bf16[16,16,64]{2,1,0:T(8,128)(2,1)}, u32[]{:S(2)}) copy-start(bf16[16,16,64]{2,1,0:T(8,128)(2,1)} %param.19) | copy-start | bytes 98308
  65.2 7.6 %collective-permute-start = (f32[16,16,1,128]{3,1,0,2:T(8,128)S(1)}, f32[16,16,1,128]{3,1,0,2:T(8,128)S(1)}, u32[]{:S(2)}, u32[]{:S(2)}) collective-permute-start(f32[16,16,1,128]{3,1,0,2:T(8,128)S(1)} %convolution_bitcast_fusion), channel_id=1, source_target_pairs={{0,1},{1,0},{2,3},{3,2},{4,5},{5,4},{6,7},{7,6},{8,9},{9,8},{10,11... | collective-permute-start | bytes 393224 | tf_op jit(solution)/shard_map/ppermute | solution.py:13
  67.2 5.7 %collective-permute-start.1 = (f32[16,16,1]{1,0,2:T(8,128)S(1)}, f32[16,16,1]{1,0,2:T(8,128)S(1)}, u32[]{:S(2)}, u32[]{:S(2)}) collective-permute-start(f32[16,16,1]{1,0,2:T(8,128)S(1)} %bitcast.137), channel_id=1, source_target_pairs={{0,1},{1,0},{2,3},{3,2},{4,5},{5,4},{6,7},{7,6},{8,9},{9,8},{10,11... | collective-permute-start | bytes 3080 | tf_op jit(solution)/shard_map/ppermute | solution.py:13
  97.0 137.3 %reduce-scatter.5.cloned.1.call-start = ((), (), s32[]{:S(2)}) async-start(), calls=%async_computation.9 | async-start | bytes 2228224 | tf_op jit(solution)/shard_map/reduce_scatter | solution.py:131
  236.2 24.9 %all-to-all-start.5 = ((f32[32,1,32]{2,1,0:T(1,128)}), f32[32,1,32]{2,1,0:T(1,128)S(1)}, u32[]{:S(2)}, u32[]{:S(2)}) async-start(f32[32,1,32]{2,1,0:T(1,128)} %broadcast_in_dim.47), calls=%async_computation.7 | async-start | bytes 32768 | tf_op jit(solution)/shard_map/all_to_all | solution.py:19
Sparse Core Ops, SparseCore 0:
  97.1 63.0 reduce-scatter.2
  163.0 71.2 reduce-scatter.4

commit v5 on v3

--- a/solution.py
+++ b/solution.py
@@ -90,30 +90,37 @@
     row_count = lax.axis_size("row")
     beam_count = parents.shape[0]
     slot_cap = max(2, (2 * beam_count + row_count - 1) // row_count)
-    my_row = lax.axis_index("row")
     group_size = queries.shape[1]
     panel_width = queries.shape[2]
     source = parents // beam_count
     rank_in = count_before(source)
-    slot_index = source * slot_cap + rank_in
-    slot_range = jnp.arange(slot_cap, dtype=jnp.int32)
-    id_table = gather_from_all(jnp.stack([parents, lengths])[None], "row")
-    all_parents = id_table[:, 0].reshape(-1)
-    all_lengths = id_table[:, 1].reshape(-1)
-    parent_table = all_parents.reshape(row_count, beam_count)
-    sources_all = parent_table // beam_count
-    offsets_all = parent_table % beam_count
-    ranks_all = count_before(sources_all)
-    chosen = (sources_all[:, None, :] == my_row) & (
-        ranks_all[:, None, :] == slot_range[None, :, None]
+    offset_row = jnp.broadcast_to(
+        (parents % beam_count).astype(jnp.bfloat16)[:, None, None], (beam_count, 1, panel_width)
     )
-    rows_sent = jnp.sum(jnp.where(chosen, offsets_all[:, None, :], 0), axis=2)
-    sent = jnp.stack([cache_keys[rows_sent], cache_values[rows_sent]], axis=2)
-    got = lax.all_to_all(sent, "row", split_axis=0, concat_axis=0, tiled=True)
-    context = cache_keys.shape[1]
-    kept_keys = got[:, :, 0].reshape(row_count * slot_cap, context, panel_width)[slot_index]
-    kept_values = got[:, :, 1].reshape(row_count * slot_cap, context, panel_width)[slot_index]
-    attended = attend(queries, kept_keys, kept_values, new_keys, new_values, all_lengths[parents])
+    message = jnp.concatenate(
+        [queries, new_keys[:, None, :], new_values[:, None, :], offset_row], axis=1
+    )
+    outgoing = jnp.zeros((row_count, slot_cap) + message.shape[1:], message.dtype)
+    outgoing = outgoing.at[source, rank_in].set(message)
+    incoming = lax.all_to_all(outgoing, "row", split_axis=0, concat_axis=0, tiled=True)
+    incoming = incoming.reshape((row_count * slot_cap,) + message.shape[1:])
+    offsets = incoming[:, group_size + 2, 0].astype(jnp.int32)
+    served = attend(
+        incoming[:, :group_size],
+        cache_keys[offsets],
+        cache_values[offsets],
+        incoming[:, group_size],
+        incoming[:, group_size + 1],
+        lengths[offsets],
+    )
+    returned = lax.all_to_all(
+        served.reshape((row_count, slot_cap) + served.shape[1:]),
+        "row",
+        split_axis=0,
+        concat_axis=0,
+        tiled=True,
+    )
+    attended = returned[source, rank_in]
     stream = residual.astype(jnp.float32) + attended.astype(jnp.float32)
     square_part = jnp.sum(stream * stream, axis=(1, 2))
     unscaled = (stream * norm_gain.astype(jnp.float32)[None]).astype(jnp.bfloat16)

time: 217 us -> 205 us (0.945)
  waiting for transfers between devices: 79.1 us -> 60.2 us
  blocking collectives: 75.4 us -> 89.8 us
  starting transfers between devices: 19.9 us -> 10 us
    all_to_all x2 -> x1, waiting for transfers between devices: 35.3 us -> 7.64 us  [body(): lax.all_to_all(served.reshape((row_count, slot_cap) + served.shape[1:]),...]
    all_to_all x0 -> x1, blocking collectives: none -> 17.5 us  [body(): lax.all_to_all(outgoing, 'row', split_axis=0, concat_axis=0, tiled=True)]
    all_to_all x2 -> x1, starting transfers between devices: 14.5 us -> 4.69 us  [body(): lax.all_to_all(served.reshape((row_count, slot_cap) + served.shape[1:]),...]
    ppermute x2, waiting for transfers between devices: 0.01 us -> 8.32 us  [from_partner(): return lax.ppermute(value, axis, pairs)]
    all_to_all x2, blocking collectives: 50.2 us -> 47.3 us  [gather_from_all(): got = lax.all_to_all(copies, axis, 0, 0, tiled=True)]
    another operation x3 -> x1, other arithmetic: 2.27 us -> 0.01 us  [the longest x1 1.54 us: body(): sent = jnp.stack([cache_keys[rows_sent], cache_values[rows_sent]], axis=2)]
    gather x5 -> x4, local copies, waits for them, and re-layouts: 4.62 us -> 2.89 us  [the longest x1 0.78 us: body(): lengths[offsets]]
    unnamed x23 -> x21, local copies, waits for them, and re-layouts: 8.73 us -> 10.3 us
  transfers between devices with their start and end apart: 5 -> 4, of which waited for: 3 -> 4; matrix products, arithmetic and copies ran while one was open for 1% -> 2% of each run, Pallas kernels for 0% -> 0%
where the time goes in v5:
time: 205 us; the launch traced here: 204 us
  blocking collectives  89.8 us (44%)
  waiting for transfers between devices  60.2 us (29%)
  local copies, waits for them, and re-layouts  17.1 us (8%)
  between operations  13.7 us (7%)
  starting transfers between devices  10 us (5%)
  other arithmetic  8.08 us (4%)
  matrix products  5.53 us (3%)
    all_to_all x2, blocking collectives, gather_from_all(): got = lax.all_to_all(copies, axis, 0, 0, tiled=True)  47.3 us
    reduce_scatter x1, waiting for transfers between devices, body(): reduced = lax.psum_scatter(partial, 'col', scatter_dimension=0, tiled=True)  44.2 us
    all_to_all x1, blocking collectives, body(): lax.all_to_all(square_all.reshape(col_count, -1), 'col', split_axis=0, co...  25 us
    all_to_all x1, blocking collectives, body(): lax.all_to_all(outgoing, 'row', split_axis=0, concat_axis=0, tiled=True)  17.5 us
    unnamed x21, local copies, waits for them, and re-layouts  10.3 us
    ppermute x2, waiting for transfers between devices, from_partner(): return lax.ppermute(value, axis, pairs)  8.32 us
    all_to_all x1, waiting for transfers between devices, body(): lax.all_to_all(served.reshape((row_count, slot_cap) + served.shape[1:]),...  7.64 us
    ppermute x2, starting transfers between devices, from_partner(): return lax.ppermute(value, axis, pairs)  5.29 us
  transfers between devices with their start and end apart: 4, of which 4 were waited for; matrix products, arithmetic and copies ran while one was open for 2% of the time, Pallas kernels for 0%

profile of v5, /device:TPU:1, one launch (start us, length us, event | category | flops | bytes accessed | tf_op | source)
XLA Modules:
  0.0 204.4 jit_solution(13761929719873443552)
XLA Ops:
  6.5 0.7 fusion.20
  7.2 0.2 convert_reduce_fusion.1
  7.4 0.7 copy.36
  8.1 0.7 copy.37
  8.8 0.1 broadcast_in_dim.26
  8.9 0.9 pad_maximum_fusion
  9.8 0.1 broadcast_in_dim.22
  9.9 1.2 scatter_fusion
  11.1 0.2 copy.50
  11.4 0.3 reshape.250
  11.6 17.5 %all_to_all.29 = bf16[32,2,1216]{2,1,0:T(2,128)(2,1)S(1)} all-to-all(bf16[32,2,1216]{2,1,0:T(2,128)(2,1)S(1)} %reshape.250), channel_id=1, replica_groups=mesh['row'=32,'col'=16] {'row'}, dimensions={0} | all-to-all | bytes 311296 | tf_op jit(solution)/shard_map/all_to_all | solution.py:105
  29.1 0.3 reshape.251
  29.4 0.1 copy.39
  29.5 1.2 fusion.15
  30.8 0.7 gather_fusion.2
  31.5 0.4 convolution_bitcast_fusion.1
  31.9 2.3 %collective-permute-start = (f32[64,16,1,128]{3,1,0,2:T(8,128)S(1)}, f32[64,16,1,128]{3,1,0,2:T(8,128)S(1)}, u32[]{:S(2)}, u32[]{:S(2)}) collective-permute-start(f32[64,16,1,128]{3,1,0,2:T(8,128)S(1)} %convolution_bitcast_fusion.1), channel_id=1, source_target_pairs={{0,1},{1,0},{2,3},{3,2},{4,5},{5,4},{6,7},{7,6},{8,9},{9,8},{10,11... | collective-permute-start | bytes 1572872 | tf_op jit(solution)/shard_map/ppermute | solution.py:13
  34.3 0.8 gather_fusion.1
  35.1 0.2 fusion.10
  35.3 3.0 %collective-permute-start.1 = (f32[64,16,1]{1,0,2:T(8,128)S(1)}, f32[64,16,1]{1,0,2:T(8,128)S(1)}, u32[]{:S(2)}, u32[]{:S(2)}) collective-permute-start(f32[64,16,1]{1,0,2:T(8,128)S(1)} %bitcast.119), channel_id=1, source_target_pairs={{0,1},{1,0},{2,3},{3,2},{4,5},{5,4},{6,7},{7,6},{8,9},{9,8},{10,11... | collective-permute-start | bytes 12296 | tf_op jit(solution)/shard_map/ppermute | solution.py:13
  38.3 0.7 gather_fusion
  39.1 7.9 %collective-permute-done = f32[64,16,1,128]{3,1,0,2:T(8,128)S(1)} collective-permute-done((f32[64,16,1,128]{3,1,0,2:T(8,128)S(1)}, f32[64,16,1,128]{3,1,0,2:T(8,128)S(1)}, u32[]{:S(2)}, u32[]{:S(2)}) %collective-permute-start) | collective-permute-done | bytes 524320 | tf_op jit(solution)/shard_map/ppermute | solution.py:13
  47.0 0.3 select_reduce_fusion
  47.3 0.4 collective-permute-done.1
  47.7 0.4 fusion.3
  48.2 0.9 fusion.2
  49.1 0.8 reshape.252
  50.0 4.7 %all-to-all-start.1 = ((bf16[32,2,1024]{2,1,0:T(2,128)(2,1)}), bf16[32,2,1024]{2,1,0:T(2,128)(2,1)S(1)}, u32[]{:S(2)}, u32[]{:S(2)}) async-start(bf16[32,2,1024]{2,1,0:T(2,128)(2,1)} %reshape.252), calls=%async_computation.1 | async-start | bytes 262144 | tf_op jit(solution)/shard_map/all_to_all | solution.py:116
  54.8 7.6 %all-to-all-done.1 = bf16[32,2,1024]{2,1,0:T(2,128)(2,1)S(1)} async-done(((bf16[32,2,1024]{2,1,0:T(2,128)(2,1)}), bf16[32,2,1024]{2,1,0:T(2,128)(2,1)S(1)}, u32[]{:S(2)}, u32[]{:S(2)}) %all-to-all-start.1) | async-done | bytes 131104 | tf_op jit(solution)/shard_map/all_to_all | solution.py:116
  62.4 0.2 reshape.253
  62.6 0.6 gather_fusion.3
  63.2 0.2 multiply_convert_fusion
  63.5 0.1 copy.40
  63.6 0.3 broadcast_bitcast_fusion
  63.9 2.2 %reshape.254 = bf16[32,2,8704]{2,1,0:T(2,128)(2,1)} reshape(bf16[32,17,16,64]{3,2,1,0:T(8,128)(2,1)S(1)} %broadcast_bitcast_fusion) | data formatting | bytes 2228224
  66.1 23.1 %all_to_all.30 = bf16[32,2,8704]{2,1,0:T(2,128)(2,1)} all-to-all(bf16[32,2,8704]{2,1,0:T(2,128)(2,1)} %reshape.254), channel_id=1, replica_groups=mesh['row'=32,'col'=16] {'row'}, dimensions={0} | all-to-all | bytes 2228224 | tf_op jit(solution)/shard_map/all_to_all | solution.py:19
  89.3 3.8 %reshape.255 = bf16[32,17,16,64]{3,2,1,0:T(8,128)(2,1)S(1)} reshape(bf16[32,2,8704]{2,1,0:T(2,128)(2,1)} %all_to_all.30) | data formatting | bytes 2228224
  93.1 0.6 copy.42
  93.7 1.4 copy-done.3
  95.0 1.0 copy-done.6
  96.1 4.0 %convolution_bitcast_fusion = f32[512,2004]{1,0:T(8,128)} fusion(bf16[512,17,64]{2,0,1:T(8,128)(2,1)S(1)} %bitcast.110, bf16[16,64,2004]{2,1,0:T(8,128)(2,1)S(1)} %copy-done.6), kind=kOutput, calls=%fused_computation.5 | convolution fusion | flops 2101346304 | bytes 9322496 | tf_op jit(solution)/shard_map/dot_general | solution.py:133
  100.1 1.0 convert_reduce_fusion
  101.1 0.1 all_to_all.21
  101.2 25.0 %all_to_all.31 = f32[16,1,32]{2,1,0:T(1,128)S(1)} all-to-all(f32[16,1,32]{2,1,0:T(1,128)S(1)} %all_to_all.21), channel_id=1, replica_groups=mesh['row'=32,'col'=16] {'col'}, dimensions={0} | all-to-all | bytes 4096 | tf_op jit(solution)/shard_map/all_to_all | solution.py:136
  126.2 44.2 %reduce-scatter.2.cloned.1.call-done = f32[32,2004]{1,0:T(8,128)} async-done(((f32[512,2004]{1,0:T(8,128)}), f32[32,2004]{1,0:T(8,128)}) %reduce-scatter.2.cloned.1.call-update) | async-done | bytes 256528 | tf_op jit(solution)/shard_map/reduce_scatter | solution.py:134
  170.5 1.2 exponential_reduce_fusion
  171.7 24.1 %all_to_all.32 = f32[32,1,32]{2,1,0:T(1,128)S(1)} all-to-all(f32[32,1,32]{2,1,0:T(1,128)S(1)} %broadcast_in_dim.30), channel_id=1, replica_groups=mesh['row'=32,'col'=16] {'row'}, dimensions={0} | all-to-all | bytes 8192 | tf_op jit(solution)/shard_map/all_to_all | solution.py:19
  195.8 1.7 multiply_subtract_fusion
  (32 shorter events, 0.3 us)
Async XLA Ops:
  6.5 24.2 %copy-start = (bf16[16,128,64]{1,2,0:T(8,128)(2,1)S(1)}, bf16[16,128,64]{1,2,0:T(8,128)(2,1)}, u32[]{:S(2)}) copy-start(bf16[16,128,64]{1,2,0:T(8,128)(2,1)} %param.15) | copy-start | bytes 786436
  30.8 3.5 %copy-start.1 = (s32[16]{0:T(128)S(1)}, s32[16]{0:T(128)}, u32[]{:S(2)}) copy-start(s32[16]{0:T(128)} %param.17) | copy-start | bytes 196
  31.5 6.7 %copy-start.2 = (bf16[16,128,64]{1,2,0:T(8,128)(2,1)S(1)}, bf16[16,128,64]{1,2,0:T(8,128)(2,1)}, u32[]{:S(2)}) copy-start(bf16[16,128,64]{1,2,0:T(8,128)(2,1)} %param.16) | copy-start | bytes 786436
  31.9 15.0 %collective-permute-start = (f32[64,16,1,128]{3,1,0,2:T(8,128)S(1)}, f32[64,16,1,128]{3,1,0,2:T(8,128)S(1)}, u32[]{:S(2)}, u32[]{:S(2)}) collective-permute-start(f32[64,16,1,128]{3,1,0,2:T(8,128)S(1)} %convolution_bitcast_fusion.1), channel_id=1, source_target_pairs={{0,1},{1,0},{2,3},{3,2},{4,5},{5,4},{6,7},{7,6},{8,9},{9,8},{10,11... | collective-permute-start | bytes 1572872 | tf_op jit(solution)/shard_map/ppermute | solution.py:13
  35.3 12.4 %collective-permute-start.1 = (f32[64,16,1]{1,0,2:T(8,128)S(1)}, f32[64,16,1]{1,0,2:T(8,128)S(1)}, u32[]{:S(2)}, u32[]{:S(2)}) collective-permute-start(f32[64,16,1]{1,0,2:T(8,128)S(1)} %bitcast.119), channel_id=1, source_target_pairs={{0,1},{1,0},{2,3},{3,2},{4,5},{5,4},{6,7},{7,6},{8,9},{9,8},{10,11... | collective-permute-start | bytes 12296 | tf_op jit(solution)/shard_map/ppermute | solution.py:13
  48.2 6.6 %copy-start.5 = (bf16[16,64]{1,0:T(8,128)(2,1)S(1)}, bf16[16,64]{1,0:T(8,128)(2,1)}, u32[]{:S(2)}) copy-start(bf16[16,64]{1,0:T(8,128)(2,1)} %param.20) | copy-start | bytes 6148
  48.2 15.1 %copy-start.4 = (bf16[16,16,64]{2,1,0:T(8,128)(2,1)S(1)}, bf16[16,16,64]{2,1,0:T(8,128)(2,1)}, u32[]{:S(2)}) copy-start(bf16[16,16,64]{2,1,0:T(8,128)(2,1)} %param.19) | copy-start | bytes 98308
  50.0 12.4 %all-to-all-start.1 = ((bf16[32,2,1024]{2,1,0:T(2,128)(2,1)}), bf16[32,2,1024]{2,1,0:T(2,128)(2,1)S(1)}, u32[]{:S(2)}, u32[]{:S(2)}) async-start(bf16[32,2,1024]{2,1,0:T(2,128)(2,1)} %reshape.252), calls=%async_computation.1 | async-start | bytes 262144 | tf_op jit(solution)/shard_map/all_to_all | solution.py:116
  54.7 115.8 %reduce-scatter.2.cloned.1.call-start = ((), (), s32[]{:S(2)}) async-start(), calls=%async_computation.6 | async-start | bytes 4456448 | tf_op jit(solution)/shard_map/reduce_scatter | solution.py:134
  93.1 3.0 %copy-start.6 = (bf16[16,64,2004]{2,1,0:T(8,128)(2,1)S(1)}, bf16[16,64,2004]{2,1,0:T(8,128)(2,1)}, u32[]{:S(2)}) copy-start(bf16[16,64,2004]{2,1,0:T(8,128)(2,1)} %param.21) | copy-start | bytes 12312580
  93.7 1.4 copy-start.3
Sparse Core Ops, SparseCore 0:
  100.2 70.2 reduce-scatter.1

commit v6 on v5

--- a/solution.py
+++ b/solution.py
@@ -123,13 +123,14 @@
     attended = returned[source, rank_in]
     stream = residual.astype(jnp.float32) + attended.astype(jnp.float32)
     square_part = jnp.sum(stream * stream, axis=(1, 2))
+    width = group_size * panel_width
     unscaled = (stream * norm_gain.astype(jnp.float32)[None]).astype(jnp.bfloat16)
-    pieces = split_three(square_part)
-    extra = jnp.zeros((beam_count, 1, panel_width), jnp.bfloat16).at[:, 0, :3].set(pieces)
-    gathered = gather_from_all(jnp.concatenate([unscaled, extra], axis=1), "row")
-    flat_rows = gathered[:, :group_size, :].reshape(gathered.shape[0], group_size * panel_width)
-    square_all = jnp.sum(gathered[:, group_size, :3].astype(jnp.float32), axis=1)
-    flat_weight = vocab_weight.reshape(group_size * panel_width, vocab_weight.shape[2])
+    extra = jnp.zeros((beam_count, 128), jnp.bfloat16).at[:, :3].set(split_three(square_part))
+    packed = jnp.concatenate([unscaled.reshape(beam_count, width), extra], axis=1)
+    gathered = gather_from_all(packed, "row")
+    flat_rows = gathered[:, :width]
+    square_all = jnp.sum(gathered[:, width : width + 3].astype(jnp.float32), axis=1)
+    flat_weight = vocab_weight.reshape(width, vocab_weight.shape[2])
     partial = jnp.dot(flat_rows, flat_weight, preferred_element_type=jnp.float32)
     reduced = lax.psum_scatter(partial, "col", scatter_dimension=0, tiled=True)
     col_count = lax.axis_size("col")

time: 205 us -> 199 us (0.971)
  local copies, waits for them, and re-layouts: 17.1 us -> 8.1 us
  matrix products: 5.53 us -> 8.01 us
    unnamed x21 -> x16, local copies, waits for them, and re-layouts: 10.3 us -> 1.85 us
    dot_general x1, matrix products: 3.97 us -> 6.45 us  [body(): jnp.dot(flat_rows, flat_weight, preferred_element_type=jnp.float32)]
  transfers between devices with their start and end apart: 4 -> 4, of which waited for: 4 -> 4; matrix products, arithmetic and copies ran while one was open for 2% -> 1% of each run, Pallas kernels for 0% -> 0%
where the time goes in v6:
time: 199 us; the launch traced here: 198 us
  blocking collectives  90 us (45%)
  waiting for transfers between devices  59.9 us (30%)
  between operations  13.7 us (7%)
  starting transfers between devices  10 us (5%)
  other arithmetic  8.48 us (4%)
  local copies, waits for them, and re-layouts  8.1 us (4%)
  matrix products  8.01 us (4%)
    all_to_all x2, blocking collectives, gather_from_all(): got = lax.all_to_all(copies, axis, 0, 0, tiled=True)  47.5 us
    reduce_scatter x1, waiting for transfers between devices, body(): reduced = lax.psum_scatter(partial, 'col', scatter_dimension=0, tiled=True)  44.7 us
    all_to_all x1, blocking collectives, body(): lax.all_to_all(square_all.reshape(col_count, -1), 'col', split_axis=0, co...  25 us
    all_to_all x1, blocking collectives, body(): lax.all_to_all(outgoing, 'row', split_axis=0, concat_axis=0, tiled=True)  17.5 us
    ppermute x2, waiting for transfers between devices, from_partner(): return lax.ppermute(value, axis, pairs)  8.32 us
    all_to_all x1, waiting for transfers between devices, body(): lax.all_to_all(served.reshape((row_count, slot_cap) + served.shape[1:]),...  6.92 us
    dot_general x1, matrix products, body(): jnp.dot(flat_rows, flat_weight, preferred_element_type=jnp.float32)  6.45 us
    ppermute x2, starting transfers between devices, from_partner(): return lax.ppermute(value, axis, pairs)  5.29 us
  transfers between devices with their start and end apart: 4, of which 4 were waited for; matrix products, arithmetic and copies ran while one was open for 1% of the time, Pallas kernels for 0%

profile of v6, /device:TPU:1, one launch (start us, length us, event | category | flops | bytes accessed | tf_op | source)
XLA Modules:
  0.0 198.2 jit_solution(751560841295062818)
XLA Ops:
  6.5 0.7 fusion.22
  7.2 0.2 convert_reduce_fusion.1
  7.4 0.7 copy.42
  8.1 0.7 copy.43
  8.8 0.1 broadcast_in_dim.26
  8.9 0.9 pad_maximum_fusion
  9.8 0.1 broadcast_in_dim.22
  9.9 1.2 scatter_fusion
  11.1 0.2 copy.55
  11.4 0.3 reshape.241
  11.6 17.5 %all_to_all.29 = bf16[32,2,1216]{2,1,0:T(2,128)(2,1)S(1)} all-to-all(bf16[32,2,1216]{2,1,0:T(2,128)(2,1)S(1)} %reshape.241), channel_id=1, replica_groups=mesh['row'=32,'col'=16] {'row'}, dimensions={0} | all-to-all | bytes 311296 | tf_op jit(solution)/shard_map/all_to_all | solution.py:105
  29.1 0.3 reshape.242
  29.4 0.1 copy.45
  29.5 1.2 fusion.17
  30.8 0.7 gather_fusion.2
  31.5 0.4 convolution_bitcast_fusion
  31.9 2.3 %collective-permute-start = (f32[64,16,1,128]{3,1,0,2:T(8,128)S(1)}, f32[64,16,1,128]{3,1,0,2:T(8,128)S(1)}, u32[]{:S(2)}, u32[]{:S(2)}) collective-permute-start(f32[64,16,1,128]{3,1,0,2:T(8,128)S(1)} %convolution_bitcast_fusion), channel_id=1, source_target_pairs={{0,1},{1,0},{2,3},{3,2},{4,5},{5,4},{6,7},{7,6},{8,9},{9,8},{10,11... | collective-permute-start | bytes 1572872 | tf_op jit(solution)/shard_map/ppermute | solution.py:13
  34.3 0.8 gather_fusion.1
  35.1 0.2 fusion.12
  35.3 3.0 %collective-permute-start.1 = (f32[64,16,1]{1,0,2:T(8,128)S(1)}, f32[64,16,1]{1,0,2:T(8,128)S(1)}, u32[]{:S(2)}, u32[]{:S(2)}) collective-permute-start(f32[64,16,1]{1,0,2:T(8,128)S(1)} %bitcast.111), channel_id=1, source_target_pairs={{0,1},{1,0},{2,3},{3,2},{4,5},{5,4},{6,7},{7,6},{8,9},{9,8},{10,11... | collective-permute-start | bytes 12296 | tf_op jit(solution)/shard_map/ppermute | solution.py:13
  38.3 0.8 gather_fusion
  39.1 7.9 %collective-permute-done = f32[64,16,1,128]{3,1,0,2:T(8,128)S(1)} collective-permute-done((f32[64,16,1,128]{3,1,0,2:T(8,128)S(1)}, f32[64,16,1,128]{3,1,0,2:T(8,128)S(1)}, u32[]{:S(2)}, u32[]{:S(2)}) %collective-permute-start) | collective-permute-done | bytes 524320 | tf_op jit(solution)/shard_map/ppermute | solution.py:13
  47.0 0.3 select_reduce_fusion
  47.3 0.4 collective-permute-done.1
  47.7 0.4 fusion.5
  48.2 0.9 fusion.2
  49.1 0.8 reshape.243
  50.0 4.7 %all-to-all-start.1 = ((bf16[32,2,1024]{2,1,0:T(2,128)(2,1)}), bf16[32,2,1024]{2,1,0:T(2,128)(2,1)S(1)}, u32[]{:S(2)}, u32[]{:S(2)}) async-start(bf16[32,2,1024]{2,1,0:T(2,128)(2,1)} %reshape.243), calls=%async_computation.1 | async-start | bytes 262144 | tf_op jit(solution)/shard_map/all_to_all | solution.py:116
  54.7 0.0 reduce-scatter.2.cloned.1.call-start
  54.8 0.7 compare_reduce_fusion
  55.5 6.9 %all-to-all-done.1 = bf16[32,2,1024]{2,1,0:T(2,128)(2,1)S(1)} async-done(((bf16[32,2,1024]{2,1,0:T(2,128)(2,1)}), bf16[32,2,1024]{2,1,0:T(2,128)(2,1)S(1)}, u32[]{:S(2)}, u32[]{:S(2)}) %all-to-all-start.1) | async-done | bytes 131104 | tf_op jit(solution)/shard_map/all_to_all | solution.py:116
  62.4 0.2 reshape.244
  62.6 0.6 gather_fusion.3
  63.2 0.2 multiply_convert_fusion
  63.5 0.1 reshape.195
  63.6 0.7 maximum_select_fusion
  64.3 0.1 copy.53
  64.4 0.1 broadcast_in_dim.29
  64.5 22.5 %all_to_all.30 = bf16[32,16,1152]{2,1,0:T(8,128)(2,1)S(1)} all-to-all(bf16[32,16,1152]{2,1,0:T(8,128)(2,1)S(1)} %broadcast_in_dim.29), channel_id=1, replica_groups=mesh['row'=32,'col'=16] {'row'}, dimensions={0} | all-to-all | bytes 2359296 | tf_op jit(solution)/shard_map/all_to_all | solution.py:19
  87.0 6.4 %fusion.3 = f32[512,2004]{1,0:T(8,128)} fusion(bf16[1024,2004]{1,0:T(8,128)(2,1)} %bitcast.119, bf16[512,1152]{1,0:T(8,128)(2,1)S(1)} %bitcast.102), kind=kOutput, calls=%fused_computation.10 | convolution fusion | flops 2101346304 | bytes 9256960 | tf_op jit(solution)/shard_map/dot_general | solution.py:134
  93.4 0.0 reduce-scatter.2.cloned.1.call-update
  93.5 0.1 copy.52
  93.6 0.1 all_to_all.21
  93.7 25.0 %all_to_all.31 = f32[16,1,32]{2,1,0:T(1,128)S(1)} all-to-all(f32[16,1,32]{2,1,0:T(1,128)S(1)} %all_to_all.21), channel_id=1, replica_groups=mesh['row'=32,'col'=16] {'col'}, dimensions={0} | all-to-all | bytes 4096 | tf_op jit(solution)/shard_map/all_to_all | solution.py:137
  118.7 44.7 %reduce-scatter.2.cloned.1.call-done = f32[32,2004]{1,0:T(8,128)} async-done(((f32[512,2004]{1,0:T(8,128)}), f32[32,2004]{1,0:T(8,128)}) %reduce-scatter.2.cloned.1.call-update) | async-done | bytes 256528 | tf_op jit(solution)/shard_map/reduce_scatter | solution.py:135
  163.4 1.2 exponential_reduce_fusion
  164.6 25.0 %all_to_all.32 = f32[32,1,32]{2,1,0:T(1,128)S(1)} all-to-all(f32[32,1,32]{2,1,0:T(1,128)S(1)} %broadcast_in_dim.30), channel_id=1, replica_groups=mesh['row'=32,'col'=16] {'row'}, dimensions={0} | all-to-all | bytes 8192 | tf_op jit(solution)/shard_map/all_to_all | solution.py:19
  189.6 1.7 multiply_subtract_fusion
  (28 shorter events, 0.3 us)
Async XLA Ops:
  6.5 24.2 %copy-start = (bf16[16,128,64]{1,2,0:T(8,128)(2,1)S(1)}, bf16[16,128,64]{1,2,0:T(8,128)(2,1)}, u32[]{:S(2)}) copy-start(bf16[16,128,64]{1,2,0:T(8,128)(2,1)} %param.15) | copy-start | bytes 786436
  30.8 3.5 %copy-start.1 = (s32[16]{0:T(128)S(1)}, s32[16]{0:T(128)}, u32[]{:S(2)}) copy-start(s32[16]{0:T(128)} %param.17) | copy-start | bytes 196
  31.5 6.7 %copy-start.2 = (bf16[16,128,64]{1,2,0:T(8,128)(2,1)S(1)}, bf16[16,128,64]{1,2,0:T(8,128)(2,1)}, u32[]{:S(2)}) copy-start(bf16[16,128,64]{1,2,0:T(8,128)(2,1)} %param.16) | copy-start | bytes 786436
  31.9 15.0 %collective-permute-start = (f32[64,16,1,128]{3,1,0,2:T(8,128)S(1)}, f32[64,16,1,128]{3,1,0,2:T(8,128)S(1)}, u32[]{:S(2)}, u32[]{:S(2)}) collective-permute-start(f32[64,16,1,128]{3,1,0,2:T(8,128)S(1)} %convolution_bitcast_fusion), channel_id=1, source_target_pairs={{0,1},{1,0},{2,3},{3,2},{4,5},{5,4},{6,7},{7,6},{8,9},{9,8},{10,11... | collective-permute-start | bytes 1572872 | tf_op jit(solution)/shard_map/ppermute | solution.py:13
  35.3 12.4 %collective-permute-start.1 = (f32[64,16,1]{1,0,2:T(8,128)S(1)}, f32[64,16,1]{1,0,2:T(8,128)S(1)}, u32[]{:S(2)}, u32[]{:S(2)}) collective-permute-start(f32[64,16,1]{1,0,2:T(8,128)S(1)} %bitcast.111), channel_id=1, source_target_pairs={{0,1},{1,0},{2,3},{3,2},{4,5},{5,4},{6,7},{7,6},{8,9},{9,8},{10,11... | collective-permute-start | bytes 12296 | tf_op jit(solution)/shard_map/ppermute | solution.py:13
  48.2 6.6 %copy-start.4 = (bf16[16,64]{1,0:T(8,128)(2,1)S(1)}, bf16[16,64]{1,0:T(8,128)(2,1)}, u32[]{:S(2)}) copy-start(bf16[16,64]{1,0:T(8,128)(2,1)} %param.20) | copy-start | bytes 6148
  48.2 15.1 %copy-start.3 = (bf16[16,16,64]{2,1,0:T(8,128)(2,1)S(1)}, bf16[16,16,64]{2,1,0:T(8,128)(2,1)}, u32[]{:S(2)}) copy-start(bf16[16,16,64]{2,1,0:T(8,128)(2,1)} %param.19) | copy-start | bytes 98308
  50.0 12.4 %all-to-all-start.1 = ((bf16[32,2,1024]{2,1,0:T(2,128)(2,1)}), bf16[32,2,1024]{2,1,0:T(2,128)(2,1)S(1)}, u32[]{:S(2)}, u32[]{:S(2)}) async-start(bf16[32,2,1024]{2,1,0:T(2,128)(2,1)} %reshape.243), calls=%async_computation.1 | async-start | bytes 262144 | tf_op jit(solution)/shard_map/all_to_all | solution.py:116
  54.7 108.7 %reduce-scatter.2.cloned.1.call-start = ((), (), s32[]{:S(2)}) async-start(), calls=%async_computation.6 | async-start | bytes 4456448 | tf_op jit(solution)/shard_map/reduce_scatter | solution.py:135
Sparse Core Ops, SparseCore 0:
  93.6 69.7 reduce-scatter.1

commit v7 on v6

--- a/solution.py
+++ b/solution.py
@@ -35,44 +35,25 @@
     return jnp.sum(matching & earlier, axis=-1)
 
 
-def attend(queries_in, key_cache, value_cache, key_new, value_new, live_rows):
-    leading = queries_in.shape[:-2]
-    group_size = queries_in.shape[-2]
-    panel_width = queries_in.shape[-1]
-    head_part = min(panel_width, HEAD_DIM)
-    heads_here = panel_width // head_part
-    context = key_cache.shape[-2]
-    query_heads = queries_in.reshape(leading + (group_size, heads_here, head_part))
-    key_heads = key_cache.reshape(leading + (context, heads_here, head_part))
-    value_heads = value_cache.reshape(leading + (context, heads_here, head_part))
-    fresh_key = key_new.reshape(leading + (heads_here, head_part))
-    fresh_value = value_new.reshape(leading + (1, heads_here, head_part)).astype(jnp.float32)
+def attend(query_full, key_full, value_half, key_new, value_new, live_rows):
+    scale_factor = HEAD_DIM ** (-0.5)
     cached = jnp.einsum(
-        "...jhe,...the->...jht", query_heads, key_heads, preferred_element_type=jnp.float32
-    )
+        "sjd,std->sjt", query_full, key_full, preferred_element_type=jnp.float32
+    ) * scale_factor
     own_score = jnp.einsum(
-        "...jhe,...he->...jh", query_heads, fresh_key, preferred_element_type=jnp.float32
-    )
-    other_cached, other_own = from_partner((cached, own_score), "col", 0)
-    cached = cached + other_cached
-    own_score = own_score + other_own
-    scale_factor = HEAD_DIM ** (-0.5)
-    cached = cached * scale_factor
-    own_score = own_score * scale_factor
+        "sjd,sd->sj", query_full, key_new, preferred_element_type=jnp.float32
+    ) * scale_factor
     positions = lax.broadcasted_iota(jnp.int32, cached.shape, cached.ndim - 1)
-    visible = positions < live_rows.reshape(leading + (1, 1, 1))
+    visible = positions < live_rows[:, None, None]
     peak_score = jnp.maximum(jnp.max(jnp.where(visible, cached, -jnp.inf), axis=-1), own_score)
     weight = jnp.where(visible, jnp.exp(cached - peak_score[..., None]), jnp.float32(0.0))
     weight_own = jnp.exp(own_score - peak_score)
     weight_sum = jnp.sum(weight, axis=-1) + weight_own
     rounded = weight.astype(jnp.bfloat16)
     rounded_own = lax.optimization_barrier(weight_own.astype(jnp.bfloat16)).astype(jnp.float32)
-    summed = jnp.einsum(
-        "...jht,...the->...jhe", rounded, value_heads, preferred_element_type=jnp.float32
-    )
-    own_part = rounded_own[..., None] * fresh_value
-    result = (summed + own_part) / weight_sum[..., None]
-    return result.reshape(leading + (group_size, panel_width)).astype(jnp.bfloat16)
+    summed = jnp.einsum("sjt,ste->sje", rounded, value_half, preferred_element_type=jnp.float32)
+    own_part = rounded_own[..., None] * value_new.astype(jnp.float32)[:, None, :]
+    return ((summed + own_part) / weight_sum[..., None]).astype(jnp.bfloat16)
 
 
 def body(
@@ -94,23 +75,32 @@
     panel_width = queries.shape[2]
     source = parents // beam_count
     rank_in = count_before(source)
-    offset_row = jnp.broadcast_to(
-        (parents % beam_count).astype(jnp.bfloat16)[:, None, None], (beam_count, 1, panel_width)
+    other_queries, other_new_keys, other_keys = from_partner(
+        (queries, new_keys, cache_keys), "col", 0
+    )
+    offset_part = jnp.broadcast_to(
+        (parents % beam_count).astype(jnp.bfloat16)[:, None], (beam_count, panel_width)
     )
     message = jnp.concatenate(
-        [queries, new_keys[:, None, :], new_values[:, None, :], offset_row], axis=1
+        [
+            jnp.concatenate([queries, other_queries], axis=-1),
+            jnp.concatenate([new_keys, other_new_keys], axis=-1)[:, None, :],
+            jnp.concatenate([new_values, offset_part], axis=-1)[:, None, :],
+        ],
+        axis=1,
     )
     outgoing = jnp.zeros((row_count, slot_cap) + message.shape[1:], message.dtype)
     outgoing = outgoing.at[source, rank_in].set(message)
     incoming = lax.all_to_all(outgoing, "row", split_axis=0, concat_axis=0, tiled=True)
     incoming = incoming.reshape((row_count * slot_cap,) + message.shape[1:])
-    offsets = incoming[:, group_size + 2, 0].astype(jnp.int32)
+    offsets = incoming[:, group_size + 1, panel_width].astype(jnp.int32)
+    whole_keys = jnp.concatenate([cache_keys, other_keys], axis=-1)
     served = attend(
         incoming[:, :group_size],
-        cache_keys[offsets],
+        whole_keys[offsets],
         cache_values[offsets],
         incoming[:, group_size],
-        incoming[:, group_size + 1],
+        incoming[:, group_size + 1, :panel_width],
         lengths[offsets],
     )
     returned = lax.all_to_all(

time: 199 us -> 196 us (0.985)
  blocking collectives: 90 us -> 72.4 us
  starting transfers between devices: 10 us -> 22.1 us
    all_to_all x1 -> x0, blocking collectives: 17.5 us -> none  [body(): lax.all_to_all(outgoing, 'row', split_axis=0, concat_axis=0, tiled=True)]
    all_to_all x0 -> x1, waiting for transfers between devices: none -> 9.13 us  [body(): lax.all_to_all(outgoing, 'row', split_axis=0, concat_axis=0, tiled=True)]
    all_to_all x0 -> x1, starting transfers between devices: none -> 8.6 us  [body(): lax.all_to_all(outgoing, 'row', split_axis=0, concat_axis=0, tiled=True)]
    ppermute x2 -> x3, waiting for transfers between devices: 8.32 us -> 0.01 us  [from_partner(): return lax.ppermute(value, axis, pairs)]
    ppermute x2 -> x3, starting transfers between devices: 5.29 us -> 9.77 us  [from_partner(): return lax.ppermute(value, axis, pairs)]
  transfers between devices with their start and end apart: 4 -> 6, of which waited for: 4 -> 3; matrix products, arithmetic and copies ran while one was open for 1% -> 3% of each run, Pallas kernels for 0% -> 0%
where the time goes in v7:
time: 196 us; the launch traced here: 195 us
  blocking collectives  72.4 us (37%)
  waiting for transfers between devices  60.8 us (31%)
  starting transfers between devices  22.1 us (11%)
  between operations  13.7 us (7%)
  other arithmetic  9.83 us (5%)
  matrix products  8.36 us (4%)
  local copies, waits for them, and re-layouts  7.98 us (4%)
    all_to_all x2, blocking collectives, gather_from_all(): got = lax.all_to_all(copies, axis, 0, 0, tiled=True)  47.1 us
    reduce_scatter x1, waiting for transfers between devices, body(): reduced = lax.psum_scatter(partial, 'col', scatter_dimension=0, tiled=True)  44.8 us
    all_to_all x1, blocking collectives, body(): lax.all_to_all(square_all.reshape(col_count, -1), 'col', split_axis=0, co...  25.3 us
    ppermute x3, starting transfers between devices, from_partner(): return lax.ppermute(value, axis, pairs)  9.77 us
    all_to_all x1, waiting for transfers between devices, body(): lax.all_to_all(outgoing, 'row', split_axis=0, concat_axis=0, tiled=True)  9.13 us
    all_to_all x1, starting transfers between devices, body(): lax.all_to_all(outgoing, 'row', split_axis=0, concat_axis=0, tiled=True)  8.6 us
    all_to_all x1, waiting for transfers between devices, body(): lax.all_to_all(served.reshape((row_count, slot_cap) + served.shape[1:]),...  6.88 us
    dot_general x1, matrix products, body(): jnp.dot(flat_rows, flat_weight, preferred_element_type=jnp.float32)  6.45 us
  transfers between devices with their start and end apart: 6, of which 3 were waited for; matrix products, arithmetic and copies ran while one was open for 3% of the time, Pallas kernels for 0%

profile of v7, /device:TPU:1, one launch (start us, length us, event | category | flops | bytes accessed | tf_op | source)
XLA Modules:
  0.0 195.2 jit_solution(17584968011152181898)
XLA Ops:
  6.5 4.5 %collective-permute-start.1 = (bf16[16,64]{1,0:T(8,128)(2,1)}, bf16[16,64]{1,0:T(8,128)(2,1)S(1)}, u32[]{:S(2)}, u32[]{:S(2)}) collective-permute-start(bf16[16,64]{1,0:T(8,128)(2,1)} %param.13), channel_id=1, source_target_pairs={{0,1},{1,0},{2,3},{3,2},{4,5},{5,4},{6,7},{7,6},{8,9},{9,8},{10,11... | collective-permute-start | bytes 6152 | tf_op jit(solution)/shard_map/ppermute | solution.py:13
  11.0 1.9 collective-permute-start
  13.0 3.4 %collective-permute-start.2 = (bf16[16,128,64]{1,2,0:T(8,128)(2,1)}, bf16[16,128,64]{1,2,0:T(8,128)(2,1)S(1)}, u32[]{:S(2)}, u32[]{:S(2)}) collective-permute-start(bf16[16,128,64]{1,2,0:T(8,128)(2,1)} %param.15), channel_id=1, source_target_pairs={{0,1},{1,0},{2,3},{3,2},{4,5},{5,4},{6,7},{7,6},{8,9},{9,8},{10,11... | collective-permute-start | bytes 786440 | tf_op jit(solution)/shard_map/ppermute | solution.py:13
  16.3 0.7 fusion.20
  17.0 0.2 convert_reduce_fusion.1
  17.2 0.1 broadcast_in_dim.25
  17.3 0.8 maximum_bitcast_fusion.1
  18.1 0.8 maximum_bitcast_fusion
  18.8 0.9 pad_maximum_fusion.1
  19.8 0.0 copy-start.1
  19.8 0.1 broadcast_in_dim.21
  19.9 1.2 scatter_fusion
  21.1 0.9 copy.50
  22.0 8.6 %all-to-all-start = ((bf16[32,2,18,128]{3,1,2,0:T(2,128)(2,1)}), bf16[32,2,18,128]{3,1,2,0:T(2,128)(2,1)S(1)}, u32[]{:S(2)}, u32[]{:S(2)}) async-start(bf16[32,2,18,128]{3,1,2,0:T(2,128)(2,1)} %copy.50), calls=%async_computation | async-start | bytes 589824 | tf_op jit(solution)/shard_map/all_to_all | solution.py:94
  30.7 9.1 %all-to-all-done = bf16[32,2,18,128]{3,1,2,0:T(2,128)(2,1)S(1)} async-done(((bf16[32,2,18,128]{3,1,2,0:T(2,128)(2,1)}), bf16[32,2,18,128]{3,1,2,0:T(2,128)(2,1)S(1)}, u32[]{:S(2)}, u32[]{:S(2)}) %all-to-all-start) | async-done | bytes 294944 | tf_op jit(solution)/shard_map/all_to_all | solution.py:94
  39.8 0.1 copy.51
  39.9 1.3 fusion.15
  41.2 0.2 fusion.10
  41.5 0.8 gather_fusion
  42.3 1.7 gather_fusion.2
  44.0 0.9 gather_fusion.1
  44.9 0.7 select_reduce_fusion
  45.7 0.4 fusion.4
  46.2 0.0 copy-start.5
  46.2 0.0 copy-start.4
  46.2 0.9 fusion.1
  47.1 0.8 reshape.180
  48.0 3.7 %all-to-all-start.1 = ((bf16[32,2,1024]{2,1,0:T(2,128)(2,1)}), bf16[32,2,1024]{2,1,0:T(2,128)(2,1)S(1)}, u32[]{:S(2)}, u32[]{:S(2)}) async-start(bf16[32,2,1024]{2,1,0:T(2,128)(2,1)} %reshape.180), calls=%async_computation.1 | async-start | bytes 262144 | tf_op jit(solution)/shard_map/all_to_all | solution.py:106
  51.7 0.0 reduce-scatter.2.cloned.1.call-start
  51.8 0.7 compare_reduce_fusion
  52.5 6.9 %all-to-all-done.1 = bf16[32,2,1024]{2,1,0:T(2,128)(2,1)S(1)} async-done(((bf16[32,2,1024]{2,1,0:T(2,128)(2,1)}), bf16[32,2,1024]{2,1,0:T(2,128)(2,1)S(1)}, u32[]{:S(2)}, u32[]{:S(2)}) %all-to-all-start.1) | async-done | bytes 131104 | tf_op jit(solution)/shard_map/all_to_all | solution.py:106
  59.4 0.2 reshape.181
  59.6 0.6 gather_fusion.3
  60.2 0.2 multiply_convert_fusion
  60.5 0.1 reshape.135
  60.6 0.7 maximum_select_fusion
  61.3 0.1 copy.61
  61.4 0.1 broadcast_in_dim.29
  61.5 22.5 %all_to_all.29 = bf16[32,16,1152]{2,1,0:T(8,128)(2,1)S(1)} all-to-all(bf16[32,16,1152]{2,1,0:T(8,128)(2,1)S(1)} %broadcast_in_dim.29), channel_id=1, replica_groups=mesh['row'=32,'col'=16] {'row'}, dimensions={0} | all-to-all | bytes 2359296 | tf_op jit(solution)/shard_map/all_to_all | solution.py:19
  84.0 6.4 %fusion.2 = f32[512,2004]{1,0:T(8,128)} fusion(bf16[1024,2004]{1,0:T(8,128)(2,1)} %bitcast.73, bf16[512,1152]{1,0:T(8,128)(2,1)S(1)} %bitcast.61), kind=kOutput, calls=%fused_computation.9 | convolution fusion | flops 2101346304 | bytes 9256960 | tf_op jit(solution)/shard_map/dot_general | solution.py:124
  90.4 0.0 reduce-scatter.2.cloned.1.call-update
  90.4 0.1 copy.60
  90.6 0.1 all_to_all.21
  90.7 25.3 %all_to_all.30 = f32[16,1,32]{2,1,0:T(1,128)S(1)} all-to-all(f32[16,1,32]{2,1,0:T(1,128)S(1)} %all_to_all.21), channel_id=1, replica_groups=mesh['row'=32,'col'=16] {'col'}, dimensions={0} | all-to-all | bytes 4096 | tf_op jit(solution)/shard_map/all_to_all | solution.py:127
  116.0 44.8 %reduce-scatter.2.cloned.1.call-done = f32[32,2004]{1,0:T(8,128)} async-done(((f32[512,2004]{1,0:T(8,128)}), f32[32,2004]{1,0:T(8,128)}) %reduce-scatter.2.cloned.1.call-update) | async-done | bytes 256528 | tf_op jit(solution)/shard_map/reduce_scatter | solution.py:125
  160.8 1.2 exponential_reduce_fusion
  162.0 24.6 %all_to_all.31 = f32[32,1,32]{2,1,0:T(1,128)S(1)} all-to-all(f32[32,1,32]{2,1,0:T(1,128)S(1)} %broadcast_in_dim.30), channel_id=1, replica_groups=mesh['row'=32,'col'=16] {'row'}, dimensions={0} | all-to-all | bytes 8192 | tf_op jit(solution)/shard_map/all_to_all | solution.py:19
  186.6 1.7 multiply_subtract_fusion
  (33 shorter events, 0.3 us)
Async XLA Ops:
  6.5 35.7 %copy-start = (bf16[16,128,64]{1,2,0:T(8,128)(2,1)S(1)}, bf16[16,128,64]{1,2,0:T(8,128)(2,1)}, u32[]{:S(2)}) copy-start(bf16[16,128,64]{1,2,0:T(8,128)(2,1)} %param.16) | copy-start | bytes 786436
  6.5 24.1 %copy-start.3 = (bf16[16,128,64]{1,2,0:T(8,128)(2,1)S(1)}, bf16[16,128,64]{1,2,0:T(8,128)(2,1)}, u32[]{:S(2)}) copy-start(bf16[16,128,64]{1,2,0:T(8,128)(2,1)} %param.15) | copy-start | bytes 786436
  6.5 11.5 %collective-permute-start.1 = (bf16[16,64]{1,0:T(8,128)(2,1)}, bf16[16,64]{1,0:T(8,128)(2,1)S(1)}, u32[]{:S(2)}, u32[]{:S(2)}) collective-permute-start(bf16[16,64]{1,0:T(8,128)(2,1)} %param.13), channel_id=1, source_target_pairs={{0,1},{1,0},{2,3},{3,2},{4,5},{5,4},{6,7},{7,6},{8,9},{9,8},{10,11... | collective-permute-start | bytes 6152 | tf_op jit(solution)/shard_map/ppermute | solution.py:13
  11.0 7.8 %collective-permute-start = (bf16[16,16,64]{2,1,0:T(8,128)(2,1)}, bf16[16,16,64]{2,1,0:T(8,128)(2,1)S(1)}, u32[]{:S(2)}, u32[]{:S(2)}) collective-permute-start(bf16[16,16,64]{2,1,0:T(8,128)(2,1)} %param.12), channel_id=1, source_target_pairs={{0,1},{1,0},{2,3},{3,2},{4,5},{5,4},{6,7},{7,6},{8,9},{9,8},{10,11... | collective-permute-start | bytes 98312 | tf_op jit(solution)/shard_map/ppermute | solution.py:13
  13.0 17.7 %collective-permute-start.2 = (bf16[16,128,64]{1,2,0:T(8,128)(2,1)}, bf16[16,128,64]{1,2,0:T(8,128)(2,1)S(1)}, u32[]{:S(2)}, u32[]{:S(2)}) collective-permute-start(bf16[16,128,64]{1,2,0:T(8,128)(2,1)} %param.15), channel_id=1, source_target_pairs={{0,1},{1,0},{2,3},{3,2},{4,5},{5,4},{6,7},{7,6},{8,9},{9,8},{10,11... | collective-permute-start | bytes 786440 | tf_op jit(solution)/shard_map/ppermute | solution.py:13
  19.8 21.7 %copy-start.1 = (s32[16]{0:T(128)S(1)}, s32[16]{0:T(128)}, u32[]{:S(2)}) copy-start(s32[16]{0:T(128)} %param.17) | copy-start | bytes 196
  22.0 17.8 %all-to-all-start = ((bf16[32,2,18,128]{3,1,2,0:T(2,128)(2,1)}), bf16[32,2,18,128]{3,1,2,0:T(2,128)(2,1)S(1)}, u32[]{:S(2)}, u32[]{:S(2)}) async-start(bf16[32,2,18,128]{3,1,2,0:T(2,128)(2,1)} %copy.50), calls=%async_computation | async-start | bytes 589824 | tf_op jit(solution)/shard_map/all_to_all | solution.py:94
  44.9 1.2 copy-start.2
  46.2 5.6 %copy-start.5 = (bf16[16,64]{1,0:T(8,128)(2,1)S(1)}, bf16[16,64]{1,0:T(8,128)(2,1)}, u32[]{:S(2)}) copy-start(bf16[16,64]{1,0:T(8,128)(2,1)} %param.20) | copy-start | bytes 6148
  46.2 14.1 %copy-start.4 = (bf16[16,16,64]{2,1,0:T(8,128)(2,1)S(1)}, bf16[16,16,64]{2,1,0:T(8,128)(2,1)}, u32[]{:S(2)}) copy-start(bf16[16,16,64]{2,1,0:T(8,128)(2,1)} %param.19) | copy-start | bytes 98308
  48.0 11.4 %all-to-all-start.1 = ((bf16[32,2,1024]{2,1,0:T(2,128)(2,1)}), bf16[32,2,1024]{2,1,0:T(2,128)(2,1)S(1)}, u32[]{:S(2)}, u32[]{:S(2)}) async-start(bf16[32,2,1024]{2,1,0:T(2,128)(2,1)} %reshape.180), calls=%async_computation.1 | async-start | bytes 262144 | tf_op jit(solution)/shard_map/all_to_all | solution.py:106
  51.7 109.1 %reduce-scatter.2.cloned.1.call-start = ((), (), s32[]{:S(2)}) async-start(), calls=%async_computation.6 | async-start | bytes 4456448 | tf_op jit(solution)/shard_map/reduce_scatter | solution.py:125
Sparse Core Ops, SparseCore 0:
  90.5 70.1 reduce-scatter.1

commit v8 on v7

--- a/solution.py
+++ b/solution.py
@@ -4,6 +4,7 @@
 from jax.sharding import PartitionSpec as P
 
 HEAD_DIM = 128
+COL = ("high", "low")
 D = 16384
 
 
@@ -76,7 +77,7 @@
     source = parents // beam_count
     rank_in = count_before(source)
     other_queries, other_new_keys, other_keys = from_partner(
-        (queries, new_keys, cache_keys), "col", 0
+        (queries, new_keys, cache_keys), "low", 0
     )
     offset_part = jnp.broadcast_to(
         (parents % beam_count).astype(jnp.bfloat16)[:, None], (beam_count, panel_width)
@@ -122,10 +123,14 @@
     square_all = jnp.sum(gathered[:, width : width + 3].astype(jnp.float32), axis=1)
     flat_weight = vocab_weight.reshape(width, vocab_weight.shape[2])
     partial = jnp.dot(flat_rows, flat_weight, preferred_element_type=jnp.float32)
-    reduced = lax.psum_scatter(partial, "col", scatter_dimension=0, tiled=True)
-    col_count = lax.axis_size("col")
+    high_count, low_count = lax.axis_size("high"), lax.axis_size("low")
+    col_count = high_count * low_count
+    blocks = partial.reshape(high_count, low_count, -1, partial.shape[1])
+    by_low = jnp.swapaxes(blocks, 0, 1).reshape(partial.shape)
+    reduced = lax.psum_scatter(by_low, "low", scatter_dimension=0, tiled=True)
+    reduced = lax.psum_scatter(reduced, "high", scatter_dimension=0, tiled=True)
     square_parts = lax.all_to_all(
-        square_all.reshape(col_count, -1), "col", split_axis=0, concat_axis=0, tiled=True
+        square_all.reshape(col_count, -1), COL, split_axis=0, concat_axis=0, tiled=True
     )
     scaling = lax.rsqrt(jnp.sum(square_parts, axis=0) / D + 1e-05)
     logits = reduced * scaling[:, None]
@@ -135,18 +140,20 @@
 
 
 def solution(mesh):
+    rows, cols = mesh.devices.shape
+    split = jax.sharding.Mesh(mesh.devices.reshape(rows, 4, cols // 4), ("row",) + COL)
     placed = (
-        P("row", None, "col"),
-        P("row", "col"),
-        P("row", "col"),
-        P("row", None, "col"),
-        P("row", None, "col"),
+        P("row", None, COL),
+        P("row", COL),
+        P("row", COL),
+        P("row", None, COL),
+        P("row", None, COL),
         P("row"),
         P("row"),
-        P("row", None, "col"),
-        P(None, "col"),
-        P(None, "col", "row"),
+        P("row", None, COL),
+        P(None, COL),
+        P(None, COL, "row"),
     )
     return jax.shard_map(
-        body, mesh=mesh, in_specs=placed, out_specs=P("col", "row"), check_vma=False
+        body, mesh=split, in_specs=placed, out_specs=P(COL, "row"), check_vma=False
     )

time: 196 us -> 266 us (1.36)
  waiting for transfers between devices: 60.8 us -> 145 us
  blocking collectives: 72.4 us -> 60.4 us
  matrix products: 8.36 us -> 4.27 us
    reduce_scatter x1 -> x2, waiting for transfers between devices: 44.8 us -> 129 us  [the longest x1 86.5 us: body(): reduced = lax.psum_scatter(by_low, 'low', scatter_dimension=0, tiled=True)]
    all_to_all x2, blocking collectives: 47.1 us -> 37.5 us  [gather_from_all(): got = lax.all_to_all(copies, axis, 0, 0, tiled=True)]
    dot_general x1, matrix products: 6.45 us -> 2.36 us  [body(): jnp.dot(flat_rows, flat_weight, preferred_element_type=jnp.float32)]
  transfers between devices with their start and end apart: 6 -> 7, of which waited for: 3 -> 4; matrix products, arithmetic and copies ran while one was open for 3% -> 2% of each run, Pallas kernels for 0% -> 0%
where the time goes in v8:
time: 266 us
  waiting for transfers between devices  145 us (55%)
  blocking collectives  60.4 us (23%)
  starting transfers between devices  22.2 us (8%)
  between operations  13.7 us (5%)
  local copies, waits for them, and re-layouts  10.2 us (4%)
  other arithmetic  9.92 us (4%)
  matrix products  4.27 us (2%)
    reduce_scatter x1, waiting for transfers between devices, body(): reduced = lax.psum_scatter(by_low, 'low', scatter_dimension=0, tiled=True)  86.5 us
    reduce_scatter x1, waiting for transfers between devices, body(): reduced = lax.psum_scatter(reduced, 'high', scatter_dimension=0, tiled=True)  42.3 us
    all_to_all x2, blocking collectives, gather_from_all(): got = lax.all_to_all(copies, axis, 0, 0, tiled=True)  37.5 us
    all_to_all x1, blocking collectives, body(): lax.all_to_all(square_all.reshape(col_count, -1), COL, split_axis=0, conc...  22.9 us
    ppermute x3, starting transfers between devices, from_partner(): return lax.ppermute(value, axis, pairs)  9.77 us
    all_to_all x1, waiting for transfers between devices, body(): lax.all_to_all(outgoing, 'row', split_axis=0, concat_axis=0, tiled=True)  9.13 us
    all_to_all x1, starting transfers between devices, body(): lax.all_to_all(outgoing, 'row', split_axis=0, concat_axis=0, tiled=True)  8.6 us
    all_to_all x1, waiting for transfers between devices, body(): lax.all_to_all(served.reshape((row_count, slot_cap) + served.shape[1:]),...  6.88 us
  transfers between devices with their start and end apart: 7, of which 4 were waited for; matrix products, arithmetic and copies ran while one was open for 2% of the time, Pallas kernels for 0%

profile of v8, /device:TPU:1, one launch (start us, length us, event | category | flops | bytes accessed | tf_op | source)
XLA Modules:
  0.0 265.5 jit_solution(1454109420464479015)
XLA Ops:
  6.5 4.5 %collective-permute-start.1 = (bf16[16,64]{1,0:T(8,128)(2,1)}, bf16[16,64]{1,0:T(8,128)(2,1)S(1)}, u32[]{:S(2)}, u32[]{:S(2)}) collective-permute-start(bf16[16,64]{1,0:T(8,128)(2,1)} %param.13), channel_id=1, source_target_pairs={{0,1},{1,0},{2,3},{3,2},{4,5},{5,4},{6,7},{7,6},{8,9},{9,8},{10,11... | collective-permute-start | bytes 6152 | tf_op jit(solution)/shard_map/ppermute | solution.py:14
  11.0 1.9 collective-permute-start
  13.0 3.4 %collective-permute-start.2 = (bf16[16,128,64]{1,2,0:T(8,128)(2,1)}, bf16[16,128,64]{1,2,0:T(8,128)(2,1)S(1)}, u32[]{:S(2)}, u32[]{:S(2)}) collective-permute-start(bf16[16,128,64]{1,2,0:T(8,128)(2,1)} %param.15), channel_id=1, source_target_pairs={{0,1},{1,0},{2,3},{3,2},{4,5},{5,4},{6,7},{7,6},{8,9},{9,8},{10,11... | collective-permute-start | bytes 786440 | tf_op jit(solution)/shard_map/ppermute | solution.py:14
  16.3 0.7 fusion.18
  17.0 0.2 convert_reduce_fusion.1
  17.2 0.1 broadcast_in_dim.25
  17.3 0.8 maximum_bitcast_fusion.1
  18.1 0.8 maximum_bitcast_fusion
  18.8 0.9 pad_maximum_fusion.1
  19.8 0.1 broadcast_in_dim.21
  19.9 1.2 scatter_fusion
  21.1 0.9 copy.40
  22.0 8.6 %all-to-all-start = ((bf16[32,2,18,128]{3,1,2,0:T(2,128)(2,1)}), bf16[32,2,18,128]{3,1,2,0:T(2,128)(2,1)S(1)}, u32[]{:S(2)}, u32[]{:S(2)}) async-start(bf16[32,2,18,128]{3,1,2,0:T(2,128)(2,1)} %copy.40), calls=%async_computation | async-start | bytes 589824 | tf_op jit(solution)/shard_map/all_to_all | solution.py:95
  30.7 9.1 %all-to-all-done = bf16[32,2,18,128]{3,1,2,0:T(2,128)(2,1)S(1)} async-done(((bf16[32,2,18,128]{3,1,2,0:T(2,128)(2,1)}), bf16[32,2,18,128]{3,1,2,0:T(2,128)(2,1)S(1)}, u32[]{:S(2)}, u32[]{:S(2)}) %all-to-all-start) | async-done | bytes 294944 | tf_op jit(solution)/shard_map/all_to_all | solution.py:95
  39.8 0.1 copy.41
  39.9 1.3 fusion.13
  41.2 0.2 fusion.8
  41.5 0.8 gather_fusion
  42.3 1.7 gather_fusion.2
  44.0 0.9 gather_fusion.1
  44.9 0.7 select_reduce_fusion
  45.7 0.4 fusion.2
  46.2 0.9 fusion.1
  47.1 0.8 reshape.187
  48.0 3.7 %all-to-all-start.1 = ((bf16[32,2,1024]{2,1,0:T(2,128)(2,1)}), bf16[32,2,1024]{2,1,0:T(2,128)(2,1)S(1)}, u32[]{:S(2)}, u32[]{:S(2)}) async-start(bf16[32,2,1024]{2,1,0:T(2,128)(2,1)} %reshape.187), calls=%async_computation.1 | async-start | bytes 262144 | tf_op jit(solution)/shard_map/all_to_all | solution.py:107
  51.7 0.0 reduce-scatter.3.cloned.1.call-start
  51.8 0.7 compare_reduce_fusion
  52.5 6.9 %all-to-all-done.1 = bf16[32,2,1024]{2,1,0:T(2,128)(2,1)S(1)} async-done(((bf16[32,2,1024]{2,1,0:T(2,128)(2,1)}), bf16[32,2,1024]{2,1,0:T(2,128)(2,1)S(1)}, u32[]{:S(2)}, u32[]{:S(2)}) %all-to-all-start.1) | async-done | bytes 131104 | tf_op jit(solution)/shard_map/all_to_all | solution.py:107
  59.4 0.2 reshape.188
  59.6 0.6 gather_fusion.3
  60.2 0.2 multiply_convert_fusion
  60.5 0.1 reshape.140
  60.6 0.7 maximum_select_fusion
  61.3 0.1 copy.53
  61.4 0.1 broadcast_in_dim.29
  61.5 22.7 %all_to_all.29 = bf16[32,16,1152]{2,1,0:T(8,128)(2,1)S(1)} all-to-all(bf16[32,16,1152]{2,1,0:T(8,128)(2,1)S(1)} %broadcast_in_dim.29), channel_id=1, replica_groups=mesh['row'=32,'high'=4,'low'=4] {'row'}, dimensions={0} | all-to-all | bytes 2359296 | tf_op jit(solution)/shard_map/all_to_all | solution.py:20
  84.2 0.1 slice.54
  84.4 2.4 convolution_bitcast_fusion
  86.7 2.2 copy.45
  89.0 0.0 reduce-scatter.5.cloned.1.call-start
  89.0 86.5 %reduce-scatter.3.cloned.1.call-done = f32[128,2004]{1,0:T(8,128)} async-done(((f32[512,2004]{1,0:T(8,128)}), f32[128,2004]{1,0:T(8,128)}) %reduce-scatter.3.cloned.1.call-update) | async-done | bytes 1026064 | tf_op jit(solution)/shard_map/reduce_scatter | solution.py:130
  175.5 0.1 convert_reduce_fusion
  175.6 0.1 all_to_all.21
  175.7 22.9 %all_to_all.30 = f32[16,1,32]{2,1,0:T(1,128)S(1)} all-to-all(f32[16,1,32]{2,1,0:T(1,128)S(1)} %all_to_all.21), channel_id=1, replica_groups=mesh['row'=32,'high'=4,'low'=4] {'high','low'}, dimensions={0} | all-to-all | bytes 4096 | tf_op jit(solution)/shard_map/all_to_all | solution.py:132
  198.7 42.3 %reduce-scatter.5.cloned.1.call-done = f32[32,2004]{1,0:T(8,128)} async-done(((f32[128,2004]{1,0:T(8,128)}), f32[32,2004]{1,0:T(8,128)}) %reduce-scatter.5.cloned.1.call-update) | async-done | bytes 256528 | tf_op jit(solution)/shard_map/reduce_scatter | solution.py:131
  241.0 1.2 exponential_reduce_fusion
  242.2 14.8 %all_to_all.31 = f32[32,1,32]{2,1,0:T(1,128)S(1)} all-to-all(f32[32,1,32]{2,1,0:T(1,128)S(1)} %broadcast_in_dim.30), channel_id=1, replica_groups=mesh['row'=32,'high'=4,'low'=4] {'row'}, dimensions={0} | all-to-all | bytes 8192 | tf_op jit(solution)/shard_map/all_to_all | solution.py:20
  257.0 1.7 multiply_subtract_fusion
  (38 shorter events, 0.3 us)
Async XLA Ops:
  6.5 35.7 %copy-start = (bf16[16,128,64]{1,2,0:T(8,128)(2,1)S(1)}, bf16[16,128,64]{1,2,0:T(8,128)(2,1)}, u32[]{:S(2)}) copy-start(bf16[16,128,64]{1,2,0:T(8,128)(2,1)} %param.16) | copy-start | bytes 786436
  6.5 24.1 %copy-start.3 = (bf16[16,128,64]{1,2,0:T(8,128)(2,1)S(1)}, bf16[16,128,64]{1,2,0:T(8,128)(2,1)}, u32[]{:S(2)}) copy-start(bf16[16,128,64]{1,2,0:T(8,128)(2,1)} %param.15) | copy-start | bytes 786436
  6.5 11.5 %collective-permute-start.1 = (bf16[16,64]{1,0:T(8,128)(2,1)}, bf16[16,64]{1,0:T(8,128)(2,1)S(1)}, u32[]{:S(2)}, u32[]{:S(2)}) collective-permute-start(bf16[16,64]{1,0:T(8,128)(2,1)} %param.13), channel_id=1, source_target_pairs={{0,1},{1,0},{2,3},{3,2},{4,5},{5,4},{6,7},{7,6},{8,9},{9,8},{10,11... | collective-permute-start | bytes 6152 | tf_op jit(solution)/shard_map/ppermute | solution.py:14
  11.0 7.8 %collective-permute-start = (bf16[16,16,64]{2,1,0:T(8,128)(2,1)}, bf16[16,16,64]{2,1,0:T(8,128)(2,1)S(1)}, u32[]{:S(2)}, u32[]{:S(2)}) collective-permute-start(bf16[16,16,64]{2,1,0:T(8,128)(2,1)} %param.12), channel_id=1, source_target_pairs={{0,1},{1,0},{2,3},{3,2},{4,5},{5,4},{6,7},{7,6},{8,9},{9,8},{10,11... | collective-permute-start | bytes 98312 | tf_op jit(solution)/shard_map/ppermute | solution.py:14
  13.0 17.7 %collective-permute-start.2 = (bf16[16,128,64]{1,2,0:T(8,128)(2,1)}, bf16[16,128,64]{1,2,0:T(8,128)(2,1)S(1)}, u32[]{:S(2)}, u32[]{:S(2)}) collective-permute-start(bf16[16,128,64]{1,2,0:T(8,128)(2,1)} %param.15), channel_id=1, source_target_pairs={{0,1},{1,0},{2,3},{3,2},{4,5},{5,4},{6,7},{7,6},{8,9},{9,8},{10,11... | collective-permute-start | bytes 786440 | tf_op jit(solution)/shard_map/ppermute | solution.py:14
  19.8 21.7 %copy-start.1 = (s32[16]{0:T(128)S(1)}, s32[16]{0:T(128)}, u32[]{:S(2)}) copy-start(s32[16]{0:T(128)} %param.17) | copy-start | bytes 196
  22.0 17.8 %all-to-all-start = ((bf16[32,2,18,128]{3,1,2,0:T(2,128)(2,1)}), bf16[32,2,18,128]{3,1,2,0:T(2,128)(2,1)S(1)}, u32[]{:S(2)}, u32[]{:S(2)}) async-start(bf16[32,2,18,128]{3,1,2,0:T(2,128)(2,1)} %copy.40), calls=%async_computation | async-start | bytes 589824 | tf_op jit(solution)/shard_map/all_to_all | solution.py:95
  44.9 1.2 copy-start.2
  46.2 5.6 %copy-start.5 = (bf16[16,64]{1,0:T(8,128)(2,1)S(1)}, bf16[16,64]{1,0:T(8,128)(2,1)}, u32[]{:S(2)}) copy-start(bf16[16,64]{1,0:T(8,128)(2,1)} %param.20) | copy-start | bytes 6148
  46.2 14.1 %copy-start.4 = (bf16[16,16,64]{2,1,0:T(8,128)(2,1)S(1)}, bf16[16,16,64]{2,1,0:T(8,128)(2,1)}, u32[]{:S(2)}) copy-start(bf16[16,16,64]{2,1,0:T(8,128)(2,1)} %param.19) | copy-start | bytes 98308
  48.0 11.4 %all-to-all-start.1 = ((bf16[32,2,1024]{2,1,0:T(2,128)(2,1)}), bf16[32,2,1024]{2,1,0:T(2,128)(2,1)S(1)}, u32[]{:S(2)}, u32[]{:S(2)}) async-start(bf16[32,2,1024]{2,1,0:T(2,128)(2,1)} %reshape.187), calls=%async_computation.1 | async-start | bytes 262144 | tf_op jit(solution)/shard_map/all_to_all | solution.py:107
  51.7 123.7 %reduce-scatter.3.cloned.1.call-start = ((), (), s32[]{:S(2)}) async-start(), calls=%async_computation.7 | async-start | bytes 5242880 | tf_op jit(solution)/shard_map/reduce_scatter | solution.py:130
  61.5 22.9 %copy-start.6 = (bf16[16,64,2004]{2,1,0:T(8,128)(2,1)S(1)}, bf16[16,64,2004]{2,1,0:T(8,128)(2,1)}, u32[]{:S(2)}) copy-start(bf16[16,64,2004]{2,1,0:T(8,128)(2,1)} %param.21) | copy-start | bytes 12312580
  89.0 152.0 %reduce-scatter.5.cloned.1.call-start = ((), (), s32[]{:S(2)}) async-start(), calls=%async_computation.8 | async-start | bytes 1310720 | tf_op jit(solution)/shard_map/reduce_scatter | solution.py:131
Sparse Core Ops, SparseCore 0:
  89.1 86.3 reduce-scatter.2
  178.3 62.6 reduce-scatter.4

commit v9 on v7

--- a/solution.py
+++ b/solution.py
@@ -18,6 +18,25 @@
     copies = jnp.broadcast_to(value[None], (size,) + value.shape)
     got = lax.all_to_all(copies, axis, 0, 0, tiled=True)
     return got.reshape((size * value.shape[0],) + value.shape[1:])
+
+
+def ring_reduce_scatter(value, axis):
+    size = lax.axis_size(axis)
+    me = lax.axis_index(axis)
+    rows = value.shape[0] // size
+    half = value.shape[1] // 2
+    lanes = (value[:, :half], value[:, half:])
+    shifts = (1, size - 1)
+    moving = [None, None]
+    for step in range(size):
+        for lane in range(2):
+            block = (me - shifts[lane] * (step + 1)) % size
+            own = lax.dynamic_slice_in_dim(lanes[lane], block * rows, rows, axis=0)
+            moving[lane] = own if step == 0 else moving[lane] + own
+            if step < size - 1:
+                pairs = [(source, (source + shifts[lane]) % size) for source in range(size)]
+                moving[lane] = lax.ppermute(moving[lane], axis, pairs)
+    return jnp.concatenate(moving, axis=1)
 
 
 def split_three(value):
@@ -122,8 +141,8 @@
     square_all = jnp.sum(gathered[:, width : width + 3].astype(jnp.float32), axis=1)
     flat_weight = vocab_weight.reshape(width, vocab_weight.shape[2])
     partial = jnp.dot(flat_rows, flat_weight, preferred_element_type=jnp.float32)
-    reduced = lax.psum_scatter(partial, "col", scatter_dimension=0, tiled=True)
     col_count = lax.axis_size("col")
+    reduced = ring_reduce_scatter(partial, "col")
     square_parts = lax.all_to_all(
         square_all.reshape(col_count, -1), "col", split_axis=0, concat_axis=0, tiled=True
     )

time: 196 us -> 350 us (1.79)
  starting transfers between devices: 22.1 us -> 146 us
  waiting for transfers between devices: 60.8 us -> 137 us
  blocking collectives: 72.4 us -> 27.8 us
  between operations: 13.7 us -> 1.47 us
  other arithmetic: 9.83 us -> 17 us
  local copies, waits for them, and re-layouts: 7.98 us -> 12.2 us
    ppermute x0 -> x30, starting transfers between devices: none -> 106 us  [ring_reduce_scatter(): moving[lane] = lax.ppermute(moving[lane], axis, pairs)]
    ppermute x0 -> x30, waiting for transfers between devices: none -> 103 us  [ring_reduce_scatter(): moving[lane] = lax.ppermute(moving[lane], axis, pairs)]
    reduce_scatter x1 -> x0, waiting for transfers between devices: 44.8 us -> none  [body(): reduced = lax.psum_scatter(partial, 'col', scatter_dimension=0, tiled=True)]
    all_to_all x1 -> x0, blocking collectives: 25.3 us -> none  [body(): lax.all_to_all(square_all.reshape(col_count, -1), 'col', split_axis=0, co...]
    all_to_all x2 -> x1, blocking collectives: 47.1 us -> 27.8 us  [gather_from_all(): got = lax.all_to_all(copies, axis, 0, 0, tiled=True)]
    all_to_all x0 -> x2, starting transfers between devices: none -> 18 us  [the longest x1 14 us: body(): lax.all_to_all(square_all.reshape(col_count, -1), 'col', split_axis=0, co...]
    all_to_all x0 -> x2, waiting for transfers between devices: none -> 18 us  [the longest x1 18 us: gather_from_all(): got = lax.all_to_all(copies, axis, 0, 0, tiled=True)]
    add x0 -> x30, other arithmetic: none -> 9.17 us  [ring_reduce_scatter(): moving[lane] = own if step == 0 else moving[lane] + own]
  transfers between devices with their start and end apart: 6 -> 37, of which waited for: 3 -> 30; matrix products, arithmetic and copies ran while one was open for 3% -> 6% of each run, Pallas kernels for 0% -> 0%
where the time goes in v9:
time: 350 us; the launch traced here: 349 us
  starting transfers between devices  146 us (42%)
  waiting for transfers between devices  137 us (39%)
  blocking collectives  27.8 us (8%)
  other arithmetic  17 us (5%)
  local copies, waits for them, and re-layouts  12.2 us (3%)
  matrix products  6.49 us (2%)
    ppermute x30, starting transfers between devices, ring_reduce_scatter(): moving[lane] = lax.ppermute(moving[lane], axis, pairs)  106 us
    ppermute x30, waiting for transfers between devices, ring_reduce_scatter(): moving[lane] = lax.ppermute(moving[lane], axis, pairs)  103 us
    all_to_all x1, blocking collectives, gather_from_all(): got = lax.all_to_all(copies, axis, 0, 0, tiled=True)  27.8 us
    all_to_all x1, waiting for transfers between devices, gather_from_all(): got = lax.all_to_all(copies, axis, 0, 0, tiled=True)  18 us
    all_to_all x1, starting transfers between devices, body(): lax.all_to_all(square_all.reshape(col_count, -1), 'col', split_axis=0, co...  14 us
    ppermute x3, starting transfers between devices, from_partner(): return lax.ppermute(value, axis, pairs)  9.77 us
    add x30, other arithmetic, ring_reduce_scatter(): moving[lane] = own if step == 0 else moving[lane] + own  9.17 us
    all_to_all x1, waiting for transfers between devices, body(): lax.all_to_all(outgoing, 'row', split_axis=0, concat_axis=0, tiled=True)  9.13 us
  transfers between devices with their start and end apart: 37, of which 30 were waited for; matrix products, arithmetic and copies ran while one was open for 6% of the time, Pallas kernels for 0%

profile of v9, /device:TPU:1, one launch (start us, length us, event | category | flops | bytes accessed | tf_op | source)
XLA Modules:
  0.0 348.6 jit_solution(4377055627341351442)
XLA Ops:
  0.0 4.5 %collective-permute-start.1 = (bf16[16,64]{1,0:T(8,128)(2,1)}, bf16[16,64]{1,0:T(8,128)(2,1)S(1)}, u32[]{:S(2)}, u32[]{:S(2)}) collective-permute-start(bf16[16,64]{1,0:T(8,128)(2,1)} %param.13), channel_id=1, source_target_pairs={{0,1},{1,0},{2,3},{3,2},{4,5},{5,4},{6,7},{7,6},{8,9},{9,8},{10,11... | collective-permute-start | bytes 6152 | tf_op jit(solution)/shard_map/ppermute | solution.py:13
  4.5 1.9 collective-permute-start
  6.4 3.4 collective-permute-start.2
  15.5 8.6 %all-to-all-start = ((bf16[32,2,18,128]{3,1,2,0:T(2,128)(2,1)}), bf16[32,2,18,128]{3,1,2,0:T(2,128)(2,1)S(1)}, u32[]{:S(2)}, u32[]{:S(2)}) async-start(bf16[32,2,18,128]{3,1,2,0:T(2,128)(2,1)} %copy.60), calls=%async_computation | async-start | bytes 589824 | tf_op jit(solution)/shard_map/all_to_all | solution.py:113
  24.2 9.1 %all-to-all-done = bf16[32,2,18,128]{3,1,2,0:T(2,128)(2,1)S(1)} async-done(((bf16[32,2,18,128]{3,1,2,0:T(2,128)(2,1)}), bf16[32,2,18,128]{3,1,2,0:T(2,128)(2,1)S(1)}, u32[]{:S(2)}, u32[]{:S(2)}) %all-to-all-start) | async-done | bytes 294944 | tf_op jit(solution)/shard_map/all_to_all | solution.py:113
  41.5 3.7 %all-to-all-start.1 = ((bf16[32,2,1024]{2,1,0:T(2,128)(2,1)}), bf16[32,2,1024]{2,1,0:T(2,128)(2,1)S(1)}, u32[]{:S(2)}, u32[]{:S(2)}) async-start(bf16[32,2,1024]{2,1,0:T(2,128)(2,1)} %reshape.180), calls=%async_computation.1 | async-start | bytes 262144 | tf_op jit(solution)/shard_map/all_to_all | solution.py:125
  45.9 7.0 %all-to-all-done.1 = bf16[32,2,1024]{2,1,0:T(2,128)(2,1)S(1)} async-done(((bf16[32,2,1024]{2,1,0:T(2,128)(2,1)}), bf16[32,2,1024]{2,1,0:T(2,128)(2,1)S(1)}, u32[]{:S(2)}, u32[]{:S(2)}) %all-to-all-start.1) | async-done | bytes 131104 | tf_op jit(solution)/shard_map/all_to_all | solution.py:125
  55.9 4.0 %all-to-all-start.2 = ((bf16[32,16,1152]{2,1,0:T(8,128)(2,1)}), bf16[32,16,1152]{2,1,0:T(8,128)(2,1)S(1)}, u32[]{:S(2)}, u32[]{:S(2)}) async-start(bf16[32,16,1152]{2,1,0:T(8,128)(2,1)} %broadcast_in_dim.29), calls=%async_computation.2 | async-start | bytes 2359296 | tf_op jit(solution)/shard_map/all_to_all | solution.py:19
  60.5 18.0 %all-to-all-done.2 = bf16[32,16,1152]{2,1,0:T(8,128)(2,1)S(1)} async-done(((bf16[32,16,1152]{2,1,0:T(8,128)(2,1)}), bf16[32,16,1152]{2,1,0:T(8,128)(2,1)S(1)}, u32[]{:S(2)}, u32[]{:S(2)}) %all-to-all-start.2) | async-done | bytes 1179680 | tf_op jit(solution)/shard_map/all_to_all | solution.py:19
  79.4 14.0 %all-to-all-start.3 = ((f32[16,1,32]{2,1,0:T(1,128)}), f32[16,1,32]{2,1,0:T(1,128)S(1)}, u32[]{:S(2)}, u32[]{:S(2)}) async-start(f32[16,1,32]{2,1,0:T(1,128)} %all_to_all.21), calls=%async_computation.3 | async-start | bytes 16384 | tf_op jit(solution)/shard_map/all_to_all | solution.py:146
  93.4 4.6 %fusion.2 = f32[512,2004]{0,1:T(8,128)S(1)} fusion(bf16[1024,2004]{1,0:T(8,128)(2,1)} %bitcast.73, bf16[512,1152]{1,0:T(8,128)(2,1)S(1)} %bitcast.62), kind=kOutput, calls=%fused_computation.9 | convolution fusion | flops 2101346304 | bytes 9256960 | tf_op jit(solution)/shard_map/dot_general | solution.py:143
  100.0 4.5 %collective-permute-start.18 = (f32[32,1002]{0,1:T(8,128)S(1)}, f32[32,1002]{0,1:T(8,128)}, u32[]{:S(2)}, u32[]{:S(2)}) collective-permute-start(f32[32,1002]{0,1:T(8,128)S(1)} %constant_dynamic-slice_fusion), channel_id=1, source_target_pairs={{0,15},{1,0},{2,1},{3,2},{4,3},{5,4},{6,5},{7,6},{8,7},{9,8},{10,9... | collective-permute-start | bytes 384776 | tf_op jit(solution)/shard_map/ppermute | solution.py:38
  104.7 1.9 collective-permute-start.3
  106.7 7.9 %collective-permute-done.18 = f32[32,1002]{0,1:T(8,128)} collective-permute-done((f32[32,1002]{0,1:T(8,128)S(1)}, f32[32,1002]{0,1:T(8,128)}, u32[]{:S(2)}, u32[]{:S(2)}) %collective-permute-start.18) | collective-permute-done | bytes 128288 | tf_op jit(solution)/shard_map/ppermute | solution.py:38
  116.0 5.4 %collective-permute-start.19 = (f32[32,1002]{0,1:T(8,128)S(1)}, f32[32,1002]{0,1:T(8,128)S(1)}, u32[]{:S(2)}, u32[]{:S(2)}) collective-permute-start(f32[32,1002]{0,1:T(8,128)S(1)} %dynamic-slice_add_fusion.14), channel_id=1, source_target_pairs={{0,15},{1,0},{2,1},{3,2},{4,3},{5,4},{6,5},{7,6},{8,7},{9,8},{10,9... | collective-permute-start | bytes 384776 | tf_op jit(solution)/shard_map/ppermute | solution.py:38
  122.8 2.1 collective-permute-start.4
  124.9 5.9 %collective-permute-done.19 = f32[32,1002]{0,1:T(8,128)S(1)} collective-permute-done((f32[32,1002]{0,1:T(8,128)S(1)}, f32[32,1002]{0,1:T(8,128)S(1)}, u32[]{:S(2)}, u32[]{:S(2)}) %collective-permute-start.19) | collective-permute-done | bytes 128288 | tf_op jit(solution)/shard_map/ppermute | solution.py:38
  131.0 5.3 %collective-permute-start.20 = (f32[32,1002]{0,1:T(8,128)S(1)}, f32[32,1002]{0,1:T(8,128)S(1)}, u32[]{:S(2)}, u32[]{:S(2)}) collective-permute-start(f32[32,1002]{0,1:T(8,128)S(1)} %dynamic-slice_add_fusion.13), channel_id=1, source_target_pairs={{0,15},{1,0},{2,1},{3,2},{4,3},{5,4},{6,5},{7,6},{8,7},{9,8},{10,9... | collective-permute-start | bytes 384776 | tf_op jit(solution)/shard_map/ppermute | solution.py:38
  139.2 5.5 %collective-permute-done.20 = f32[32,1002]{0,1:T(8,128)S(1)} collective-permute-done((f32[32,1002]{0,1:T(8,128)S(1)}, f32[32,1002]{0,1:T(8,128)S(1)}, u32[]{:S(2)}, u32[]{:S(2)}) %collective-permute-start.20) | collective-permute-done | bytes 128288 | tf_op jit(solution)/shard_map/ppermute | solution.py:38
  144.9 5.3 %collective-permute-start.21 = (f32[32,1002]{0,1:T(8,128)S(1)}, f32[32,1002]{0,1:T(8,128)S(1)}, u32[]{:S(2)}, u32[]{:S(2)}) collective-permute-start(f32[32,1002]{0,1:T(8,128)S(1)} %dynamic-slice_add_fusion.12), channel_id=1, source_target_pairs={{0,15},{1,0},{2,1},{3,2},{4,3},{5,4},{6,5},{7,6},{8,7},{9,8},{10,9... | collective-permute-start | bytes 384776 | tf_op jit(solution)/shard_map/ppermute | solution.py:38
  151.0 1.9 collective-permute-start.6
  152.9 4.9 %collective-permute-done.21 = f32[32,1002]{0,1:T(8,128)S(1)} collective-permute-done((f32[32,1002]{0,1:T(8,128)S(1)}, f32[32,1002]{0,1:T(8,128)S(1)}, u32[]{:S(2)}, u32[]{:S(2)}) %collective-permute-start.21) | collective-permute-done | bytes 128288 | tf_op jit(solution)/shard_map/ppermute | solution.py:38
  158.0 5.3 %collective-permute-start.22 = (f32[32,1002]{0,1:T(8,128)S(1)}, f32[32,1002]{0,1:T(8,128)S(1)}, u32[]{:S(2)}, u32[]{:S(2)}) collective-permute-start(f32[32,1002]{0,1:T(8,128)S(1)} %dynamic-slice_add_fusion.11), channel_id=1, source_target_pairs={{0,15},{1,0},{2,1},{3,2},{4,3},{5,4},{6,5},{7,6},{8,7},{9,8},{10,9... | collective-permute-start | bytes 384776 | tf_op jit(solution)/shard_map/ppermute | solution.py:38
  163.8 1.9 collective-permute-start.7
  165.7 4.4 %collective-permute-done.22 = f32[32,1002]{0,1:T(8,128)S(1)} collective-permute-done((f32[32,1002]{0,1:T(8,128)S(1)}, f32[32,1002]{0,1:T(8,128)S(1)}, u32[]{:S(2)}, u32[]{:S(2)}) %collective-permute-start.22) | collective-permute-done | bytes 128288 | tf_op jit(solution)/shard_map/ppermute | solution.py:38
  170.3 5.3 %collective-permute-start.23 = (f32[32,1002]{0,1:T(8,128)S(1)}, f32[32,1002]{0,1:T(8,128)S(1)}, u32[]{:S(2)}, u32[]{:S(2)}) collective-permute-start(f32[32,1002]{0,1:T(8,128)S(1)} %dynamic-slice_add_fusion.10), channel_id=1, source_target_pairs={{0,15},{1,0},{2,1},{3,2},{4,3},{5,4},{6,5},{7,6},{8,7},{9,8},{10,9... | collective-permute-start | bytes 384776 | tf_op jit(solution)/shard_map/ppermute | solution.py:38
  177.8 3.9 %collective-permute-done.23 = f32[32,1002]{0,1:T(8,128)S(1)} collective-permute-done((f32[32,1002]{0,1:T(8,128)S(1)}, f32[32,1002]{0,1:T(8,128)S(1)}, u32[]{:S(2)}, u32[]{:S(2)}) %collective-permute-start.23) | collective-permute-done | bytes 128288 | tf_op jit(solution)/shard_map/ppermute | solution.py:38
  181.8 5.0 %collective-permute-start.24 = (f32[32,1002]{0,1:T(8,128)S(1)}, f32[32,1002]{0,1:T(8,128)S(1)}, u32[]{:S(2)}, u32[]{:S(2)}) collective-permute-start(f32[32,1002]{0,1:T(8,128)S(1)} %dynamic-slice_add_fusion.9), channel_id=1, source_target_pairs={{0,15},{1,0},{2,1},{3,2},{4,3},{5,4},{6,5},{7,6},{8,7},{9,8},{10,9... | collective-permute-start | bytes 384776 | tf_op jit(solution)/shard_map/ppermute | solution.py:38
  189.0 3.9 %collective-permute-done.24 = f32[32,1002]{0,1:T(8,128)S(1)} collective-permute-done((f32[32,1002]{0,1:T(8,128)S(1)}, f32[32,1002]{0,1:T(8,128)S(1)}, u32[]{:S(2)}, u32[]{:S(2)}) %collective-permute-start.24) | collective-permute-done | bytes 128288 | tf_op jit(solution)/shard_map/ppermute | solution.py:38
  193.1 5.0 %collective-permute-start.25 = (f32[32,1002]{0,1:T(8,128)S(1)}, f32[32,1002]{0,1:T(8,128)S(1)}, u32[]{:S(2)}, u32[]{:S(2)}) collective-permute-start(f32[32,1002]{0,1:T(8,128)S(1)} %dynamic-slice_add_fusion.8), channel_id=1, source_target_pairs={{0,15},{1,0},{2,1},{3,2},{4,3},{5,4},{6,5},{7,6},{8,7},{9,8},{10,9... | collective-permute-start | bytes 384776 | tf_op jit(solution)/shard_map/ppermute | solution.py:38
  198.6 1.9 collective-permute-start.10
  200.5 4.7 %collective-permute-done.25 = f32[32,1002]{0,1:T(8,128)S(1)} collective-permute-done((f32[32,1002]{0,1:T(8,128)S(1)}, f32[32,1002]{0,1:T(8,128)S(1)}, u32[]{:S(2)}, u32[]{:S(2)}) %collective-permute-start.25) | collective-permute-done | bytes 128288 | tf_op jit(solution)/shard_map/ppermute | solution.py:38
  205.5 5.0 %collective-permute-start.26 = (f32[32,1002]{0,1:T(8,128)S(1)}, f32[32,1002]{0,1:T(8,128)S(1)}, u32[]{:S(2)}, u32[]{:S(2)}) collective-permute-start(f32[32,1002]{0,1:T(8,128)S(1)} %dynamic-slice_add_fusion.7), channel_id=1, source_target_pairs={{0,15},{1,0},{2,1},{3,2},{4,3},{5,4},{6,5},{7,6},{8,7},{9,8},{10,9... | collective-permute-start | bytes 384776 | tf_op jit(solution)/shard_map/ppermute | solution.py:38
  213.2 5.6 %collective-permute-done.26 = f32[32,1002]{0,1:T(8,128)S(1)} collective-permute-done((f32[32,1002]{0,1:T(8,128)S(1)}, f32[32,1002]{0,1:T(8,128)S(1)}, u32[]{:S(2)}, u32[]{:S(2)}) %collective-permute-start.26) | collective-permute-done | bytes 128288 | tf_op jit(solution)/shard_map/ppermute | solution.py:38
  219.0 5.0 %collective-permute-start.27 = (f32[32,1002]{0,1:T(8,128)S(1)}, f32[32,1002]{0,1:T(8,128)S(1)}, u32[]{:S(2)}, u32[]{:S(2)}) collective-permute-start(f32[32,1002]{0,1:T(8,128)S(1)} %dynamic-slice_add_fusion.6), channel_id=1, source_target_pairs={{0,15},{1,0},{2,1},{3,2},{4,3},{5,4},{6,5},{7,6},{8,7},{9,8},{10,9... | collective-permute-start | bytes 384776 | tf_op jit(solution)/shard_map/ppermute | solution.py:38
  227.0 6.5 %collective-permute-done.27 = f32[32,1002]{0,1:T(8,128)S(1)} collective-permute-done((f32[32,1002]{0,1:T(8,128)S(1)}, f32[32,1002]{0,1:T(8,128)S(1)}, u32[]{:S(2)}, u32[]{:S(2)}) %collective-permute-start.27) | collective-permute-done | bytes 128288 | tf_op jit(solution)/shard_map/ppermute | solution.py:38
  233.7 5.0 %collective-permute-start.28 = (f32[32,1002]{0,1:T(8,128)S(1)}, f32[32,1002]{0,1:T(8,128)S(1)}, u32[]{:S(2)}, u32[]{:S(2)}) collective-permute-start(f32[32,1002]{0,1:T(8,128)S(1)} %dynamic-slice_add_fusion.5), channel_id=1, source_target_pairs={{0,15},{1,0},{2,1},{3,2},{4,3},{5,4},{6,5},{7,6},{8,7},{9,8},{10,9... | collective-permute-start | bytes 384776 | tf_op jit(solution)/shard_map/ppermute | solution.py:38
  241.9 7.3 %collective-permute-done.28 = f32[32,1002]{0,1:T(8,128)S(1)} collective-permute-done((f32[32,1002]{0,1:T(8,128)S(1)}, f32[32,1002]{0,1:T(8,128)S(1)}, u32[]{:S(2)}, u32[]{:S(2)}) %collective-permute-start.28) | collective-permute-done | bytes 128288 | tf_op jit(solution)/shard_map/ppermute | solution.py:38
  249.5 5.0 %collective-permute-start.29 = (f32[32,1002]{0,1:T(8,128)S(1)}, f32[32,1002]{0,1:T(8,128)S(1)}, u32[]{:S(2)}, u32[]{:S(2)}) collective-permute-start(f32[32,1002]{0,1:T(8,128)S(1)} %dynamic-slice_add_fusion.4), channel_id=1, source_target_pairs={{0,15},{1,0},{2,1},{3,2},{4,3},{5,4},{6,5},{7,6},{8,7},{9,8},{10,9... | collective-permute-start | bytes 384776 | tf_op jit(solution)/shard_map/ppermute | solution.py:38
  258.0 7.9 %collective-permute-done.29 = f32[32,1002]{0,1:T(8,128)S(1)} collective-permute-done((f32[32,1002]{0,1:T(8,128)S(1)}, f32[32,1002]{0,1:T(8,128)S(1)}, u32[]{:S(2)}, u32[]{:S(2)}) %collective-permute-start.29) | collective-permute-done | bytes 128288 | tf_op jit(solution)/shard_map/ppermute | solution.py:38
  266.1 5.3 %collective-permute-start.30 = (f32[32,1002]{0,1:T(8,128)S(1)}, f32[32,1002]{0,1:T(8,128)S(1)}, u32[]{:S(2)}, u32[]{:S(2)}) collective-permute-start(f32[32,1002]{0,1:T(8,128)S(1)} %dynamic-slice_add_fusion.3), channel_id=1, source_target_pairs={{0,15},{1,0},{2,1},{3,2},{4,3},{5,4},{6,5},{7,6},{8,7},{9,8},{10,9... | collective-permute-start | bytes 384776 | tf_op jit(solution)/shard_map/ppermute | solution.py:38
  274.6 7.3 %collective-permute-done.30 = f32[32,1002]{0,1:T(8,128)S(1)} collective-permute-done((f32[32,1002]{0,1:T(8,128)S(1)}, f32[32,1002]{0,1:T(8,128)S(1)}, u32[]{:S(2)}, u32[]{:S(2)}) %collective-permute-start.30) | collective-permute-done | bytes 128288 | tf_op jit(solution)/shard_map/ppermute | solution.py:38
  282.1 5.3 %collective-permute-start.31 = (f32[32,1002]{0,1:T(8,128)S(1)}, f32[32,1002]{0,1:T(8,128)S(1)}, u32[]{:S(2)}, u32[]{:S(2)}) collective-permute-start(f32[32,1002]{0,1:T(8,128)S(1)} %dynamic-slice_add_fusion.2), channel_id=1, source_target_pairs={{0,15},{1,0},{2,1},{3,2},{4,3},{5,4},{6,5},{7,6},{8,7},{9,8},{10,9... | collective-permute-start | bytes 384776 | tf_op jit(solution)/shard_map/ppermute | solution.py:38
  290.4 6.7 %collective-permute-done.31 = f32[32,1002]{0,1:T(8,128)S(1)} collective-permute-done((f32[32,1002]{0,1:T(8,128)S(1)}, f32[32,1002]{0,1:T(8,128)S(1)}, u32[]{:S(2)}, u32[]{:S(2)}) %collective-permute-start.31) | collective-permute-done | bytes 128288 | tf_op jit(solution)/shard_map/ppermute | solution.py:38
  297.4 5.3 %collective-permute-start.32 = (f32[32,1002]{0,1:T(8,128)S(1)}, f32[32,1002]{0,1:T(8,128)S(1)}, u32[]{:S(2)}, u32[]{:S(2)}) collective-permute-start(f32[32,1002]{0,1:T(8,128)S(1)} %dynamic-slice_add_fusion.1), channel_id=1, source_target_pairs={{0,15},{1,0},{2,1},{3,2},{4,3},{5,4},{6,5},{7,6},{8,7},{9,8},{10,9... | collective-permute-start | bytes 384776 | tf_op jit(solution)/shard_map/ppermute | solution.py:38
  306.2 5.3 %collective-permute-done.32 = f32[32,1002]{0,1:T(8,128)S(1)} collective-permute-done((f32[32,1002]{0,1:T(8,128)S(1)}, f32[32,1002]{0,1:T(8,128)S(1)}, u32[]{:S(2)}, u32[]{:S(2)}) %collective-permute-start.32) | collective-permute-done | bytes 128288 | tf_op jit(solution)/shard_map/ppermute | solution.py:38
  311.9 7.4 %collective-permute-done.17 = f32[32,1002]{0,1:T(8,128)S(1)} collective-permute-done((f32[32,1002]{0,1:T(8,128)}, f32[32,1002]{0,1:T(8,128)S(1)}, u32[]{:S(2)}, u32[]{:S(2)}) %collective-permute-start.17) | collective-permute-done | bytes 128288 | tf_op jit(solution)/shard_map/ppermute | solution.py:38
  319.9 27.8 %all_to_all.29 = f32[32,1,32]{2,1,0:T(1,128)S(1)} all-to-all(f32[32,1,32]{2,1,0:T(1,128)S(1)} %broadcast_in_dim.30), channel_id=1, replica_groups=mesh['row'=32,'col'=16] {'row'}, dimensions={0} | all-to-all | bytes 8192 | tf_op jit(solution)/shard_map/all_to_all | solution.py:19
  (131 shorter events, 58.3 us)
Async XLA Ops:
  0.0 35.8 %copy-start = (bf16[16,128,64]{1,2,0:T(8,128)(2,1)S(1)}, bf16[16,128,64]{1,2,0:T(8,128)(2,1)}, u32[]{:S(2)}) copy-start(bf16[16,128,64]{1,2,0:T(8,128)(2,1)} %param.16) | copy-start | bytes 786436
  0.0 24.1 %copy-start.5 = (bf16[16,128,64]{1,2,0:T(8,128)(2,1)S(1)}, bf16[16,128,64]{1,2,0:T(8,128)(2,1)}, u32[]{:S(2)}) copy-start(bf16[16,128,64]{1,2,0:T(8,128)(2,1)} %param.15) | copy-start | bytes 786436
  0.0 11.5 %collective-permute-start.1 = (bf16[16,64]{1,0:T(8,128)(2,1)}, bf16[16,64]{1,0:T(8,128)(2,1)S(1)}, u32[]{:S(2)}, u32[]{:S(2)}) collective-permute-start(bf16[16,64]{1,0:T(8,128)(2,1)} %param.13), channel_id=1, source_target_pairs={{0,1},{1,0},{2,3},{3,2},{4,5},{5,4},{6,7},{7,6},{8,9},{9,8},{10,11... | collective-permute-start | bytes 6152 | tf_op jit(solution)/shard_map/ppermute | solution.py:13
  4.5 7.8 %collective-permute-start = (bf16[16,16,64]{2,1,0:T(8,128)(2,1)}, bf16[16,16,64]{2,1,0:T(8,128)(2,1)S(1)}, u32[]{:S(2)}, u32[]{:S(2)}) collective-permute-start(bf16[16,16,64]{2,1,0:T(8,128)(2,1)} %param.12), channel_id=1, source_target_pairs={{0,1},{1,0},{2,3},{3,2},{4,5},{5,4},{6,7},{7,6},{8,9},{9,8},{10,11... | collective-permute-start | bytes 98312 | tf_op jit(solution)/shard_map/ppermute | solution.py:13
  6.4 17.7 %collective-permute-start.2 = (bf16[16,128,64]{1,2,0:T(8,128)(2,1)}, bf16[16,128,64]{1,2,0:T(8,128)(2,1)S(1)}, u32[]{:S(2)}, u32[]{:S(2)}) collective-permute-start(bf16[16,128,64]{1,2,0:T(8,128)(2,1)} %param.15), channel_id=1, source_target_pairs={{0,1},{1,0},{2,3},{3,2},{4,5},{5,4},{6,7},{7,6},{8,9},{9,8},{10,11... | collective-permute-start | bytes 786440 | tf_op jit(solution)/shard_map/ppermute | solution.py:13
  13.2 21.7 %copy-start.1 = (s32[16]{0:T(128)S(1)}, s32[16]{0:T(128)}, u32[]{:S(2)}) copy-start(s32[16]{0:T(128)} %param.17) | copy-start | bytes 196
  15.5 17.8 %all-to-all-start = ((bf16[32,2,18,128]{3,1,2,0:T(2,128)(2,1)}), bf16[32,2,18,128]{3,1,2,0:T(2,128)(2,1)S(1)}, u32[]{:S(2)}, u32[]{:S(2)}) async-start(bf16[32,2,18,128]{3,1,2,0:T(2,128)(2,1)} %copy.60), calls=%async_computation | async-start | bytes 589824 | tf_op jit(solution)/shard_map/all_to_all | solution.py:113
  38.4 1.2 copy-start.4
  39.6 5.6 %copy-start.7 = (bf16[16,64]{1,0:T(8,128)(2,1)S(1)}, bf16[16,64]{1,0:T(8,128)(2,1)}, u32[]{:S(2)}) copy-start(bf16[16,64]{1,0:T(8,128)(2,1)} %param.20) | copy-start | bytes 6148
  39.6 14.1 %copy-start.6 = (bf16[16,16,64]{2,1,0:T(8,128)(2,1)S(1)}, bf16[16,16,64]{2,1,0:T(8,128)(2,1)}, u32[]{:S(2)}) copy-start(bf16[16,16,64]{2,1,0:T(8,128)(2,1)} %param.19) | copy-start | bytes 98308
  41.5 11.4 %all-to-all-start.1 = ((bf16[32,2,1024]{2,1,0:T(2,128)(2,1)}), bf16[32,2,1024]{2,1,0:T(2,128)(2,1)S(1)}, u32[]{:S(2)}, u32[]{:S(2)}) async-start(bf16[32,2,1024]{2,1,0:T(2,128)(2,1)} %reshape.180), calls=%async_computation.1 | async-start | bytes 262144 | tf_op jit(solution)/shard_map/all_to_all | solution.py:125
  55.9 22.7 %all-to-all-start.2 = ((bf16[32,16,1152]{2,1,0:T(8,128)(2,1)}), bf16[32,16,1152]{2,1,0:T(8,128)(2,1)S(1)}, u32[]{:S(2)}, u32[]{:S(2)}) async-start(bf16[32,16,1152]{2,1,0:T(8,128)(2,1)} %broadcast_in_dim.29), calls=%async_computation.2 | async-start | bytes 2359296 | tf_op jit(solution)/shard_map/all_to_all | solution.py:19
  79.4 27.3 %all-to-all-start.3 = ((f32[16,1,32]{2,1,0:T(1,128)}), f32[16,1,32]{2,1,0:T(1,128)S(1)}, u32[]{:S(2)}, u32[]{:S(2)}) async-start(f32[16,1,32]{2,1,0:T(1,128)} %all_to_all.21), calls=%async_computation.3 | async-start | bytes 16384 | tf_op jit(solution)/shard_map/all_to_all | solution.py:146
  98.5 1.3 copy-start.2
  100.0 14.6 %collective-permute-start.18 = (f32[32,1002]{0,1:T(8,128)S(1)}, f32[32,1002]{0,1:T(8,128)}, u32[]{:S(2)}, u32[]{:S(2)}) collective-permute-start(f32[32,1002]{0,1:T(8,128)S(1)} %constant_dynamic-slice_fusion), channel_id=1, source_target_pairs={{0,15},{1,0},{2,1},{3,2},{4,3},{5,4},{6,5},{7,6},{8,7},{9,8},{10,9... | collective-permute-start | bytes 384776 | tf_op jit(solution)/shard_map/ppermute | solution.py:38
  104.7 16.8 %collective-permute-start.3 = (f32[32,1002]{0,1:T(8,128)S(1)}, f32[32,1002]{0,1:T(8,128)}, u32[]{:S(2)}, u32[]{:S(2)}) collective-permute-start(f32[32,1002]{0,1:T(8,128)S(1)} %constant_dynamic-slice_fusion.1), channel_id=1, source_target_pairs={{0,1},{1,2},{2,3},{3,4},{4,5},{5,6},{6,7},{7,8},{8,9},{9,10},{10,1... | collective-permute-start | bytes 384776 | tf_op jit(solution)/shard_map/ppermute | solution.py:38
  106.7 24.1 %copy-start.3 = (f32[512,1002]{0,1:T(8,128)S(1)}, f32[512,1002]{0,1:T(8,128)}, u32[]{:S(2)}) copy-start(f32[512,1002]{0,1:T(8,128)} %copy-done.2) | copy-start | bytes 6156292
  116.0 14.7 %collective-permute-start.19 = (f32[32,1002]{0,1:T(8,128)S(1)}, f32[32,1002]{0,1:T(8,128)S(1)}, u32[]{:S(2)}, u32[]{:S(2)}) collective-permute-start(f32[32,1002]{0,1:T(8,128)S(1)} %dynamic-slice_add_fusion.14), channel_id=1, source_target_pairs={{0,15},{1,0},{2,1},{3,2},{4,3},{5,4},{6,5},{7,6},{8,7},{9,8},{10,9... | collective-permute-start | bytes 384776 | tf_op jit(solution)/shard_map/ppermute | solution.py:38
  122.8 14.3 %collective-permute-start.4 = (f32[32,1002]{0,1:T(8,128)S(1)}, f32[32,1002]{0,1:T(8,128)S(1)}, u32[]{:S(2)}, u32[]{:S(2)}) collective-permute-start(f32[32,1002]{0,1:T(8,128)S(1)} %dynamic-slice_add_fusion.29), channel_id=1, source_target_pairs={{0,1},{1,2},{2,3},{3,4},{4,5},{5,6},{6,7},{7,8},{8,9},{9,10},{10,1... | collective-permute-start | bytes 384776 | tf_op jit(solution)/shard_map/ppermute | solution.py:38
  131.0 13.7 %collective-permute-start.20 = (f32[32,1002]{0,1:T(8,128)S(1)}, f32[32,1002]{0,1:T(8,128)S(1)}, u32[]{:S(2)}, u32[]{:S(2)}) collective-permute-start(f32[32,1002]{0,1:T(8,128)S(1)} %dynamic-slice_add_fusion.13), channel_id=1, source_target_pairs={{0,15},{1,0},{2,1},{3,2},{4,3},{5,4},{6,5},{7,6},{8,7},{9,8},{10,9... | collective-permute-start | bytes 384776 | tf_op jit(solution)/shard_map/ppermute | solution.py:38
  137.3 13.5 %collective-permute-start.5 = (f32[32,1002]{0,1:T(8,128)S(1)}, f32[32,1002]{0,1:T(8,128)S(1)}, u32[]{:S(2)}, u32[]{:S(2)}) collective-permute-start(f32[32,1002]{0,1:T(8,128)S(1)} %dynamic-slice_add_fusion.28), channel_id=1, source_target_pairs={{0,1},{1,2},{2,3},{3,4},{4,5},{5,6},{6,7},{7,8},{8,9},{9,10},{10,1... | collective-permute-start | bytes 384776 | tf_op jit(solution)/shard_map/ppermute | solution.py:38
  144.9 12.9 %collective-permute-start.21 = (f32[32,1002]{0,1:T(8,128)S(1)}, f32[32,1002]{0,1:T(8,128)S(1)}, u32[]{:S(2)}, u32[]{:S(2)}) collective-permute-start(f32[32,1002]{0,1:T(8,128)S(1)} %dynamic-slice_add_fusion.12), channel_id=1, source_target_pairs={{0,15},{1,0},{2,1},{3,2},{4,3},{5,4},{6,5},{7,6},{8,7},{9,8},{10,9... | collective-permute-start | bytes 384776 | tf_op jit(solution)/shard_map/ppermute | solution.py:38
  151.0 12.6 %collective-permute-start.6 = (f32[32,1002]{0,1:T(8,128)S(1)}, f32[32,1002]{0,1:T(8,128)S(1)}, u32[]{:S(2)}, u32[]{:S(2)}) collective-permute-start(f32[32,1002]{0,1:T(8,128)S(1)} %dynamic-slice_add_fusion.27), channel_id=1, source_target_pairs={{0,1},{1,2},{2,3},{3,4},{4,5},{5,6},{6,7},{7,8},{8,9},{9,10},{10,1... | collective-permute-start | bytes 384776 | tf_op jit(solution)/shard_map/ppermute | solution.py:38
  158.0 12.0 %collective-permute-start.22 = (f32[32,1002]{0,1:T(8,128)S(1)}, f32[32,1002]{0,1:T(8,128)S(1)}, u32[]{:S(2)}, u32[]{:S(2)}) collective-permute-start(f32[32,1002]{0,1:T(8,128)S(1)} %dynamic-slice_add_fusion.11), channel_id=1, source_target_pairs={{0,15},{1,0},{2,1},{3,2},{4,3},{5,4},{6,5},{7,6},{8,7},{9,8},{10,9... | collective-permute-start | bytes 384776 | tf_op jit(solution)/shard_map/ppermute | solution.py:38
  163.8 11.8 %collective-permute-start.7 = (f32[32,1002]{0,1:T(8,128)S(1)}, f32[32,1002]{0,1:T(8,128)S(1)}, u32[]{:S(2)}, u32[]{:S(2)}) collective-permute-start(f32[32,1002]{0,1:T(8,128)S(1)} %dynamic-slice_add_fusion.26), channel_id=1, source_target_pairs={{0,1},{1,2},{2,3},{3,4},{4,5},{5,6},{6,7},{7,8},{8,9},{9,10},{10,1... | collective-permute-start | bytes 384776 | tf_op jit(solution)/shard_map/ppermute | solution.py:38
  170.3 11.3 %collective-permute-start.23 = (f32[32,1002]{0,1:T(8,128)S(1)}, f32[32,1002]{0,1:T(8,128)S(1)}, u32[]{:S(2)}, u32[]{:S(2)}) collective-permute-start(f32[32,1002]{0,1:T(8,128)S(1)} %dynamic-slice_add_fusion.10), channel_id=1, source_target_pairs={{0,15},{1,0},{2,1},{3,2},{4,3},{5,4},{6,5},{7,6},{8,7},{9,8},{10,9... | collective-permute-start | bytes 384776 | tf_op jit(solution)/shard_map/ppermute | solution.py:38
  175.8 11.0 %collective-permute-start.8 = (f32[32,1002]{0,1:T(8,128)S(1)}, f32[32,1002]{0,1:T(8,128)S(1)}, u32[]{:S(2)}, u32[]{:S(2)}) collective-permute-start(f32[32,1002]{0,1:T(8,128)S(1)} %dynamic-slice_add_fusion.25), channel_id=1, source_target_pairs={{0,1},{1,2},{2,3},{3,4},{4,5},{5,6},{6,7},{7,8},{8,9},{9,10},{10,1... | collective-permute-start | bytes 384776 | tf_op jit(solution)/shard_map/ppermute | solution.py:38
  181.8 11.0 %collective-permute-start.24 = (f32[32,1002]{0,1:T(8,128)S(1)}, f32[32,1002]{0,1:T(8,128)S(1)}, u32[]{:S(2)}, u32[]{:S(2)}) collective-permute-start(f32[32,1002]{0,1:T(8,128)S(1)} %dynamic-slice_add_fusion.9), channel_id=1, source_target_pairs={{0,15},{1,0},{2,1},{3,2},{4,3},{5,4},{6,5},{7,6},{8,7},{9,8},{10,9... | collective-permute-start | bytes 384776 | tf_op jit(solution)/shard_map/ppermute | solution.py:38
  187.1 11.3 %collective-permute-start.9 = (f32[32,1002]{0,1:T(8,128)S(1)}, f32[32,1002]{0,1:T(8,128)S(1)}, u32[]{:S(2)}, u32[]{:S(2)}) collective-permute-start(f32[32,1002]{0,1:T(8,128)S(1)} %dynamic-slice_add_fusion.24), channel_id=1, source_target_pairs={{0,1},{1,2},{2,3},{3,4},{4,5},{5,6},{6,7},{7,8},{8,9},{9,10},{10,1... | collective-permute-start | bytes 384776 | tf_op jit(solution)/shard_map/ppermute | solution.py:38
  193.1 12.2 %collective-permute-start.25 = (f32[32,1002]{0,1:T(8,128)S(1)}, f32[32,1002]{0,1:T(8,128)S(1)}, u32[]{:S(2)}, u32[]{:S(2)}) collective-permute-start(f32[32,1002]{0,1:T(8,128)S(1)} %dynamic-slice_add_fusion.8), channel_id=1, source_target_pairs={{0,15},{1,0},{2,1},{3,2},{4,3},{5,4},{6,5},{7,6},{8,7},{9,8},{10,9... | collective-permute-start | bytes 384776 | tf_op jit(solution)/shard_map/ppermute | solution.py:38
  198.6 12.4 %collective-permute-start.10 = (f32[32,1002]{0,1:T(8,128)S(1)}, f32[32,1002]{0,1:T(8,128)S(1)}, u32[]{:S(2)}, u32[]{:S(2)}) collective-permute-start(f32[32,1002]{0,1:T(8,128)S(1)} %dynamic-slice_add_fusion.23), channel_id=1, source_target_pairs={{0,1},{1,2},{2,3},{3,4},{4,5},{5,6},{6,7},{7,8},{8,9},{9,10},{10,1... | collective-permute-start | bytes 384776 | tf_op jit(solution)/shard_map/ppermute | solution.py:38
  205.5 13.3 %collective-permute-start.26 = (f32[32,1002]{0,1:T(8,128)S(1)}, f32[32,1002]{0,1:T(8,128)S(1)}, u32[]{:S(2)}, u32[]{:S(2)}) collective-permute-start(f32[32,1002]{0,1:T(8,128)S(1)} %dynamic-slice_add_fusion.7), channel_id=1, source_target_pairs={{0,15},{1,0},{2,1},{3,2},{4,3},{5,4},{6,5},{7,6},{8,7},{9,8},{10,9... | collective-permute-start | bytes 384776 | tf_op jit(solution)/shard_map/ppermute | solution.py:38
  211.3 13.6 %collective-permute-start.11 = (f32[32,1002]{0,1:T(8,128)S(1)}, f32[32,1002]{0,1:T(8,128)S(1)}, u32[]{:S(2)}, u32[]{:S(2)}) collective-permute-start(f32[32,1002]{0,1:T(8,128)S(1)} %dynamic-slice_add_fusion.22), channel_id=1, source_target_pairs={{0,1},{1,2},{2,3},{3,4},{4,5},{5,6},{6,7},{7,8},{8,9},{9,10},{10,1... | collective-permute-start | bytes 384776 | tf_op jit(solution)/shard_map/ppermute | solution.py:38
  219.0 14.5 %collective-permute-start.27 = (f32[32,1002]{0,1:T(8,128)S(1)}, f32[32,1002]{0,1:T(8,128)S(1)}, u32[]{:S(2)}, u32[]{:S(2)}) collective-permute-start(f32[32,1002]{0,1:T(8,128)S(1)} %dynamic-slice_add_fusion.6), channel_id=1, source_target_pairs={{0,15},{1,0},{2,1},{3,2},{4,3},{5,4},{6,5},{7,6},{8,7},{9,8},{10,9... | collective-permute-start | bytes 384776 | tf_op jit(solution)/shard_map/ppermute | solution.py:38
  225.0 14.7 %collective-permute-start.12 = (f32[32,1002]{0,1:T(8,128)S(1)}, f32[32,1002]{0,1:T(8,128)S(1)}, u32[]{:S(2)}, u32[]{:S(2)}) collective-permute-start(f32[32,1002]{0,1:T(8,128)S(1)} %dynamic-slice_add_fusion.21), channel_id=1, source_target_pairs={{0,1},{1,2},{2,3},{3,4},{4,5},{5,6},{6,7},{7,8},{8,9},{9,10},{10,1... | collective-permute-start | bytes 384776 | tf_op jit(solution)/shard_map/ppermute | solution.py:38
  233.7 15.6 %collective-permute-start.28 = (f32[32,1002]{0,1:T(8,128)S(1)}, f32[32,1002]{0,1:T(8,128)S(1)}, u32[]{:S(2)}, u32[]{:S(2)}) collective-permute-start(f32[32,1002]{0,1:T(8,128)S(1)} %dynamic-slice_add_fusion.5), channel_id=1, source_target_pairs={{0,15},{1,0},{2,1},{3,2},{4,3},{5,4},{6,5},{7,6},{8,7},{9,8},{10,9... | collective-permute-start | bytes 384776 | tf_op jit(solution)/shard_map/ppermute | solution.py:38
  240.0 15.9 %collective-permute-start.13 = (f32[32,1002]{0,1:T(8,128)S(1)}, f32[32,1002]{0,1:T(8,128)S(1)}, u32[]{:S(2)}, u32[]{:S(2)}) collective-permute-start(f32[32,1002]{0,1:T(8,128)S(1)} %dynamic-slice_add_fusion.20), channel_id=1, source_target_pairs={{0,1},{1,2},{2,3},{3,4},{4,5},{5,6},{6,7},{7,8},{8,9},{9,10},{10,1... | collective-permute-start | bytes 384776 | tf_op jit(solution)/shard_map/ppermute | solution.py:38
  249.5 16.4 %collective-permute-start.29 = (f32[32,1002]{0,1:T(8,128)S(1)}, f32[32,1002]{0,1:T(8,128)S(1)}, u32[]{:S(2)}, u32[]{:S(2)}) collective-permute-start(f32[32,1002]{0,1:T(8,128)S(1)} %dynamic-slice_add_fusion.4), channel_id=1, source_target_pairs={{0,15},{1,0},{2,1},{3,2},{4,3},{5,4},{6,5},{7,6},{8,7},{9,8},{10,9... | collective-permute-start | bytes 384776 | tf_op jit(solution)/shard_map/ppermute | solution.py:38
  256.1 16.4 %collective-permute-start.14 = (f32[32,1002]{0,1:T(8,128)S(1)}, f32[32,1002]{0,1:T(8,128)S(1)}, u32[]{:S(2)}, u32[]{:S(2)}) collective-permute-start(f32[32,1002]{0,1:T(8,128)S(1)} %dynamic-slice_add_fusion.19), channel_id=1, source_target_pairs={{0,1},{1,2},{2,3},{3,4},{4,5},{5,6},{6,7},{7,8},{8,9},{9,10},{10,1... | collective-permute-start | bytes 384776 | tf_op jit(solution)/shard_map/ppermute | solution.py:38
  266.1 15.8 %collective-permute-start.30 = (f32[32,1002]{0,1:T(8,128)S(1)}, f32[32,1002]{0,1:T(8,128)S(1)}, u32[]{:S(2)}, u32[]{:S(2)}) collective-permute-start(f32[32,1002]{0,1:T(8,128)S(1)} %dynamic-slice_add_fusion.3), channel_id=1, source_target_pairs={{0,15},{1,0},{2,1},{3,2},{4,3},{5,4},{6,5},{7,6},{8,7},{9,8},{10,9... | collective-permute-start | bytes 384776 | tf_op jit(solution)/shard_map/ppermute | solution.py:38
  272.7 15.6 %collective-permute-start.15 = (f32[32,1002]{0,1:T(8,128)S(1)}, f32[32,1002]{0,1:T(8,128)S(1)}, u32[]{:S(2)}, u32[]{:S(2)}) collective-permute-start(f32[32,1002]{0,1:T(8,128)S(1)} %dynamic-slice_add_fusion.18), channel_id=1, source_target_pairs={{0,1},{1,2},{2,3},{3,4},{4,5},{5,6},{6,7},{7,8},{8,9},{9,10},{10,1... | collective-permute-start | bytes 384776 | tf_op jit(solution)/shard_map/ppermute | solution.py:38
  282.1 15.0 %collective-permute-start.31 = (f32[32,1002]{0,1:T(8,128)S(1)}, f32[32,1002]{0,1:T(8,128)S(1)}, u32[]{:S(2)}, u32[]{:S(2)}) collective-permute-start(f32[32,1002]{0,1:T(8,128)S(1)} %dynamic-slice_add_fusion.2), channel_id=1, source_target_pairs={{0,15},{1,0},{2,1},{3,2},{4,3},{5,4},{6,5},{7,6},{8,7},{9,8},{10,9... | collective-permute-start | bytes 384776 | tf_op jit(solution)/shard_map/ppermute | solution.py:38
  288.5 14.7 %collective-permute-start.16 = (f32[32,1002]{0,1:T(8,128)S(1)}, f32[32,1002]{0,1:T(8,128)S(1)}, u32[]{:S(2)}, u32[]{:S(2)}) collective-permute-start(f32[32,1002]{0,1:T(8,128)S(1)} %dynamic-slice_add_fusion.17), channel_id=1, source_target_pairs={{0,1},{1,2},{2,3},{3,4},{4,5},{5,6},{6,7},{7,8},{8,9},{9,10},{10,1... | collective-permute-start | bytes 384776 | tf_op jit(solution)/shard_map/ppermute | solution.py:38
  297.4 14.1 %collective-permute-start.32 = (f32[32,1002]{0,1:T(8,128)S(1)}, f32[32,1002]{0,1:T(8,128)S(1)}, u32[]{:S(2)}, u32[]{:S(2)}) collective-permute-start(f32[32,1002]{0,1:T(8,128)S(1)} %dynamic-slice_add_fusion.1), channel_id=1, source_target_pairs={{0,15},{1,0},{2,1},{3,2},{4,3},{5,4},{6,5},{7,6},{8,7},{9,8},{10,9... | collective-permute-start | bytes 384776 | tf_op jit(solution)/shard_map/ppermute | solution.py:38
  304.2 15.1 %collective-permute-start.17 = (f32[32,1002]{0,1:T(8,128)}, f32[32,1002]{0,1:T(8,128)S(1)}, u32[]{:S(2)}, u32[]{:S(2)}) collective-permute-start(f32[32,1002]{0,1:T(8,128)} %dynamic-slice_add_fusion.16), channel_id=1, source_target_pairs={{0,1},{1,2},{2,3},{3,4},{4,5},{5,6},{6,7},{7,8},{8,9},{9,10},{10,1... | collective-permute-start | bytes 384776 | tf_op jit(solution)/shard_map/ppermute | solution.py:38

commit v10 on v7

--- a/solution.py
+++ b/solution.py
@@ -75,9 +75,10 @@
     panel_width = queries.shape[2]
     source = parents // beam_count
     rank_in = count_before(source)
-    other_queries, other_new_keys, other_keys = from_partner(
-        (queries, new_keys, cache_keys), "col", 0
+    other_both, other_keys = from_partner(
+        (jnp.concatenate([queries, new_keys[:, None, :]], axis=1), cache_keys), "col", 0
     )
+    other_queries, other_new_keys = other_both[:, :group_size], other_both[:, group_size]
     offset_part = jnp.broadcast_to(
         (parents % beam_count).astype(jnp.bfloat16)[:, None], (beam_count, panel_width)
     )

time: 196 us -> 194 us (0.990)
  starting transfers between devices: 22.1 us -> 20 us
    ppermute x3 -> x2, starting transfers between devices: 9.77 us -> 6.29 us  [from_partner(): return lax.ppermute(value, axis, pairs)]
  transfers between devices with their start and end apart: 6 -> 5, of which waited for: 3 -> 3; matrix products, arithmetic and copies ran while one was open for 3% -> 3% of each run, Pallas kernels for 0% -> 0%
where the time goes in v10:
time: 194 us; the launch traced here: 193 us
  blocking collectives  71.6 us (37%)
  waiting for transfers between devices  60.8 us (31%)
  starting transfers between devices  20 us (10%)
  between operations  13.7 us (7%)
  other arithmetic  9.69 us (5%)
  local copies, waits for them, and re-layouts  8.9 us (5%)
  matrix products  8.36 us (4%)
    all_to_all x2, blocking collectives, gather_from_all(): got = lax.all_to_all(copies, axis, 0, 0, tiled=True)  47.3 us
    reduce_scatter x1, waiting for transfers between devices, body(): reduced = lax.psum_scatter(partial, 'col', scatter_dimension=0, tiled=True)  44.6 us
    all_to_all x1, blocking collectives, body(): lax.all_to_all(square_all.reshape(col_count, -1), 'col', split_axis=0, co...  24.3 us
    all_to_all x1, starting transfers between devices, body(): lax.all_to_all(outgoing, 'row', split_axis=0, concat_axis=0, tiled=True)  9.92 us
    all_to_all x1, waiting for transfers between devices, body(): lax.all_to_all(outgoing, 'row', split_axis=0, concat_axis=0, tiled=True)  9.24 us
    all_to_all x1, waiting for transfers between devices, body(): lax.all_to_all(served.reshape((row_count, slot_cap) + served.shape[1:]),...  6.88 us
    dot_general x1, matrix products, body(): jnp.dot(flat_rows, flat_weight, preferred_element_type=jnp.float32)  6.45 us
    ppermute x2, starting transfers between devices, from_partner(): return lax.ppermute(value, axis, pairs)  6.29 us
  transfers between devices with their start and end apart: 5, of which 3 were waited for; matrix products, arithmetic and copies ran while one was open for 3% of the time, Pallas kernels for 0%

profile of v10, /device:TPU:1, one launch (start us, length us, event | category | flops | bytes accessed | tf_op | source)
XLA Modules:
  0.0 193.0 jit_solution(4601060628215382303)
XLA Ops:
  6.5 0.9 copy.54
  7.5 0.7 pad_maximum_fusion.2
  8.2 4.4 %collective-permute-start = (bf16[16,17,64]{2,0,1:T(8,128)(2,1)S(1)}, bf16[16,17,64]{2,0,1:T(8,128)(2,1)S(1)}, u32[]{:S(2)}, u32[]{:S(2)}) collective-permute-start(bf16[16,17,64]{2,0,1:T(8,128)(2,1)S(1)} %pad_maximum_fusion.2), channel_id=1, source_target_pairs={{0,1},{1,0},{2,3},{3,2},{4,5},{5,4},{6,7},{7,6},{8,9},{9,8},{10,11... | collective-permute-start | bytes 104456 | tf_op jit(solution)/shard_map/ppermute | solution.py:13
  12.5 1.9 collective-permute-start.1
  14.5 0.7 fusion.20
  15.1 0.2 convert_reduce_fusion.1
  15.3 0.1 broadcast_in_dim.28
  15.4 0.8 maximum_bitcast_fusion.1
  16.2 0.8 maximum_bitcast_fusion
  16.9 0.1 pad_maximum_fusion.1
  17.1 0.0 copy-start.1
  17.1 0.1 broadcast_in_dim.24
  17.2 1.2 scatter_fusion
  18.4 0.9 copy.56
  19.3 9.9 %all-to-all-start = ((bf16[32,2,18,128]{3,1,2,0:T(2,128)(2,1)}), bf16[32,2,18,128]{3,1,2,0:T(2,128)(2,1)S(1)}, u32[]{:S(2)}, u32[]{:S(2)}) async-start(bf16[32,2,18,128]{3,1,2,0:T(2,128)(2,1)} %copy.56), calls=%async_computation | async-start | bytes 589824 | tf_op jit(solution)/shard_map/all_to_all | solution.py:95
  29.3 9.2 %all-to-all-done = bf16[32,2,18,128]{3,1,2,0:T(2,128)(2,1)S(1)} async-done(((bf16[32,2,18,128]{3,1,2,0:T(2,128)(2,1)}), bf16[32,2,18,128]{3,1,2,0:T(2,128)(2,1)S(1)}, u32[]{:S(2)}, u32[]{:S(2)}) %all-to-all-start) | async-done | bytes 294944 | tf_op jit(solution)/shard_map/all_to_all | solution.py:95
  38.5 0.1 copy.57
  38.6 1.3 fusion.15
  40.0 0.2 fusion.10
  40.2 0.8 gather_fusion
  41.0 1.7 gather_fusion.2
  42.7 0.9 gather_fusion.1
  43.7 0.7 select_reduce_fusion
  44.4 0.4 fusion.4
  44.9 0.0 copy-start.5
  44.9 0.9 fusion.1
  45.9 0.8 reshape.180
  46.7 3.7 %all-to-all-start.1 = ((bf16[32,2,1024]{2,1,0:T(2,128)(2,1)}), bf16[32,2,1024]{2,1,0:T(2,128)(2,1)S(1)}, u32[]{:S(2)}, u32[]{:S(2)}) async-start(bf16[32,2,1024]{2,1,0:T(2,128)(2,1)} %reshape.180), calls=%async_computation.1 | async-start | bytes 262144 | tf_op jit(solution)/shard_map/all_to_all | solution.py:107
  50.5 0.0 reduce-scatter.2.cloned.1.call-start
  50.5 0.7 compare_reduce_fusion
  51.2 6.9 %all-to-all-done.1 = bf16[32,2,1024]{2,1,0:T(2,128)(2,1)S(1)} async-done(((bf16[32,2,1024]{2,1,0:T(2,128)(2,1)}), bf16[32,2,1024]{2,1,0:T(2,128)(2,1)S(1)}, u32[]{:S(2)}, u32[]{:S(2)}) %all-to-all-start.1) | async-done | bytes 131104 | tf_op jit(solution)/shard_map/all_to_all | solution.py:107
  58.1 0.2 reshape.181
  58.3 0.6 gather_fusion.3
  59.0 0.2 multiply_convert_fusion
  59.2 0.1 reshape.135
  59.3 0.7 maximum_select_fusion
  60.0 0.1 copy.67
  60.1 0.1 broadcast_in_dim.32
  60.2 22.5 %all_to_all.29 = bf16[32,16,1152]{2,1,0:T(8,128)(2,1)S(1)} all-to-all(bf16[32,16,1152]{2,1,0:T(8,128)(2,1)S(1)} %broadcast_in_dim.32), channel_id=1, replica_groups=mesh['row'=32,'col'=16] {'row'}, dimensions={0} | all-to-all | bytes 2359296 | tf_op jit(solution)/shard_map/all_to_all | solution.py:19
  82.7 6.4 %fusion.2 = f32[512,2004]{1,0:T(8,128)} fusion(bf16[1024,2004]{1,0:T(8,128)(2,1)} %bitcast.77, bf16[512,1152]{1,0:T(8,128)(2,1)S(1)} %bitcast.64), kind=kOutput, calls=%fused_computation.9 | convolution fusion | flops 2101346304 | bytes 9256960 | tf_op jit(solution)/shard_map/dot_general | solution.py:125
  89.1 0.0 reduce-scatter.2.cloned.1.call-update
  89.2 0.1 copy.66
  89.3 0.1 all_to_all.21
  89.4 24.3 %all_to_all.30 = f32[16,1,32]{2,1,0:T(1,128)S(1)} all-to-all(f32[16,1,32]{2,1,0:T(1,128)S(1)} %all_to_all.21), channel_id=1, replica_groups=mesh['row'=32,'col'=16] {'col'}, dimensions={0} | all-to-all | bytes 4096 | tf_op jit(solution)/shard_map/all_to_all | solution.py:128
  113.8 44.6 %reduce-scatter.2.cloned.1.call-done = f32[32,2004]{1,0:T(8,128)} async-done(((f32[512,2004]{1,0:T(8,128)}), f32[32,2004]{1,0:T(8,128)}) %reduce-scatter.2.cloned.1.call-update) | async-done | bytes 256528 | tf_op jit(solution)/shard_map/reduce_scatter | solution.py:126
  158.4 1.2 exponential_reduce_fusion
  159.6 24.8 %all_to_all.31 = f32[32,1,32]{2,1,0:T(1,128)S(1)} all-to-all(f32[32,1,32]{2,1,0:T(1,128)S(1)} %broadcast_in_dim.33), channel_id=1, replica_groups=mesh['row'=32,'col'=16] {'row'}, dimensions={0} | all-to-all | bytes 8192 | tf_op jit(solution)/shard_map/all_to_all | solution.py:19
  184.4 1.7 multiply_subtract_fusion
  (34 shorter events, 0.3 us)
Async XLA Ops:
  6.5 34.5 %copy-start = (bf16[16,128,64]{1,2,0:T(8,128)(2,1)S(1)}, bf16[16,128,64]{1,2,0:T(8,128)(2,1)}, u32[]{:S(2)}) copy-start(bf16[16,128,64]{1,2,0:T(8,128)(2,1)} %param.16) | copy-start | bytes 786436
  6.5 22.7 %copy-start.3 = (bf16[16,128,64]{1,2,0:T(8,128)(2,1)S(1)}, bf16[16,128,64]{1,2,0:T(8,128)(2,1)}, u32[]{:S(2)}) copy-start(bf16[16,128,64]{1,2,0:T(8,128)(2,1)} %param.15) | copy-start | bytes 786436
  8.2 8.0 %collective-permute-start = (bf16[16,17,64]{2,0,1:T(8,128)(2,1)S(1)}, bf16[16,17,64]{2,0,1:T(8,128)(2,1)S(1)}, u32[]{:S(2)}, u32[]{:S(2)}) collective-permute-start(bf16[16,17,64]{2,0,1:T(8,128)(2,1)S(1)} %pad_maximum_fusion.2), channel_id=1, source_target_pairs={{0,1},{1,0},{2,3},{3,2},{4,5},{5,4},{6,7},{7,6},{8,9},{9,8},{10,11... | collective-permute-start | bytes 104456 | tf_op jit(solution)/shard_map/ppermute | solution.py:13
  12.5 16.7 %collective-permute-start.1 = (bf16[16,128,64]{1,2,0:T(8,128)(2,1)}, bf16[16,128,64]{1,2,0:T(8,128)(2,1)S(1)}, u32[]{:S(2)}, u32[]{:S(2)}) collective-permute-start(bf16[16,128,64]{1,2,0:T(8,128)(2,1)} %param.15), channel_id=1, source_target_pairs={{0,1},{1,0},{2,3},{3,2},{4,5},{5,4},{6,7},{7,6},{8,9},{9,8},{10,11... | collective-permute-start | bytes 786440 | tf_op jit(solution)/shard_map/ppermute | solution.py:13
  17.1 23.1 %copy-start.1 = (s32[16]{0:T(128)S(1)}, s32[16]{0:T(128)}, u32[]{:S(2)}) copy-start(s32[16]{0:T(128)} %param.17) | copy-start | bytes 196
  19.3 19.2 %all-to-all-start = ((bf16[32,2,18,128]{3,1,2,0:T(2,128)(2,1)}), bf16[32,2,18,128]{3,1,2,0:T(2,128)(2,1)S(1)}, u32[]{:S(2)}, u32[]{:S(2)}) async-start(bf16[32,2,18,128]{3,1,2,0:T(2,128)(2,1)} %copy.56), calls=%async_computation | async-start | bytes 589824 | tf_op jit(solution)/shard_map/all_to_all | solution.py:95
  43.6 1.2 copy-start.2
  44.9 5.6 %copy-start.5 = (bf16[16,64]{1,0:T(8,128)(2,1)S(1)}, bf16[16,64]{1,0:T(8,128)(2,1)}, u32[]{:S(2)}) copy-start(bf16[16,64]{1,0:T(8,128)(2,1)} %param.20) | copy-start | bytes 6148
  44.9 14.1 %copy-start.4 = (bf16[16,16,64]{2,1,0:T(8,128)(2,1)S(1)}, bf16[16,16,64]{2,1,0:T(8,128)(2,1)}, u32[]{:S(2)}) copy-start(bf16[16,16,64]{2,1,0:T(8,128)(2,1)} %param.19) | copy-start | bytes 98308
  46.7 11.4 %all-to-all-start.1 = ((bf16[32,2,1024]{2,1,0:T(2,128)(2,1)}), bf16[32,2,1024]{2,1,0:T(2,128)(2,1)S(1)}, u32[]{:S(2)}, u32[]{:S(2)}) async-start(bf16[32,2,1024]{2,1,0:T(2,128)(2,1)} %reshape.180), calls=%async_computation.1 | async-start | bytes 262144 | tf_op jit(solution)/shard_map/all_to_all | solution.py:107
  50.5 107.9 %reduce-scatter.2.cloned.1.call-start = ((), (), s32[]{:S(2)}) async-start(), calls=%async_computation.6 | async-start | bytes 4456448 | tf_op jit(solution)/shard_map/reduce_scatter | solution.py:126
Sparse Core Ops, SparseCore 0:
  89.3 69.0 reduce-scatter.1
